TPU v7x, 32 devices: a whole 2x2x4 slice. The times are simulated.
32 devices in a mesh: energy: 4 (over z), momentum: 4 (over x, core), space: 2 (over y).
Axes of the slice: x: 2, y: 2, z: 4, core: 2. Of those that a mesh axis runs over, the one named last changes fastest.
Arguments:
- blocks: float32 [8, 4, 2, 2, 256, 256], P('energy', 'momentum', 'space'), may hold values from -0.1 to 1.1
- inverse_guess: float32 [8, 4, 2, 2, 256, 256], P('energy', 'momentum', 'space'), may hold values from -1.8 to 2.4, as said below
- coupling: float32 [4, 2, 2, 128, 128], P('momentum', 'space'), may hold values from -0.37625 to 0.37625
- pair_index: int32 [2, 128], P('space'), may hold values from 0 to 255, as said below
- phonon_shift: int32 [8], replicated, may hold values from 1 to 8, as said below
- phonon_strength: float32 [2, 8, 4], replicated, may hold values from 0.05 to 0.5
- momentum_table: int32 [4, 4], replicated, may hold values from 0 to 3, as said below
Outputs:
- green: float32 [8, 4, 2, 2, 256, 256], P('energy', 'momentum', 'space')
- self_energy: float32 [8, 4, 2, 128, 512], P('energy', 'momentum', 'space')
Inputs may be any that keep to these rules, and one draw needn't show every extreme that they name: `inverse_guess`: an approximate inverse of the matching block of blocks. `pair_index`: in each block s, entries 8 a to 8 a + 7 are a 16 + b for 8 distinct atoms b, the first of them b = a. `phonon_shift`: one entry equals 8 and another equals 1. `momentum_table`: each row and each column holds every momentum once.
All inputs are finite; a program needn't handle non-finite values.
Results may differ from a plain program's by a relative error of at most 0.0001.
Values sent between devices are 32-bit elements; how exact they have to be, the bound alone decides.
No kernel may reach another device: no remote copies, remote signals or barrier semaphores. Data moves between devices by JAX's collectives and lax.ppermute only.
A program may use at most 128 MiB of HBM per device.

v0:
```python
import jax
import jax.numpy as jnp
from jax import lax
from jax.sharding import PartitionSpec as P
from jax.experimental import pallas as pl
from jax.experimental.pallas import tpu as pltpu

ORB = 16
ATOMS = 16
NEWTON = 2


HIGHEST = lax.Precision.HIGHEST
NEWTON_PRECISION = lax.Precision.HIGHEST


def from_behind(shard, axis, by):
    count = lax.axis_size(axis)
    pairs = [(i, i + by) for i in range(count) if 0 <= i + by < count]
    return lax.ppermute(shard, axis, pairs)


def complex_product(first_factor, second_factor, precision=HIGHEST):
    first_real, first_imag = first_factor
    second_real, second_imag = second_factor
    real_part = jnp.matmul(first_real, second_real, precision=precision) - jnp.matmul(
        first_imag, second_imag, precision=precision
    )
    imag_part = jnp.matmul(first_real, second_imag, precision=precision) + jnp.matmul(
        first_imag, second_real, precision=precision
    )
    return (real_part, imag_part)


def newton_product(first_factor, second_factor):
    return complex_product(first_factor, second_factor, NEWTON_PRECISION)


def part(pair, rows=slice(None), cols=slice(None)):
    return tuple(value[..., rows, cols] for value in pair)


def combine(first_weight, first, second):
    return tuple(first_weight * a - b for a, b in zip(first, second))


def add(first, second):
    return tuple(a + b for a, b in zip(first, second))


def sweep(blocks, guess, coupling_block):
    space_count = lax.axis_size("space")
    size = blocks[0].shape[-1]
    edge = coupling_block[0].shape[-1]
    lead = slice(0, edge)
    trail = slice(size - edge, size)
    adjoint = (jnp.swapaxes(coupling_block[0], -1, -2), -jnp.swapaxes(coupling_block[1], -1, -2))

    def schur_of(incoming):
        return complex_product(complex_product(adjoint, incoming), coupling_block)

    def lead_rows_minus(values, schur, rows):
        update = newton_product(schur, rows)
        return tuple(v.at[..., lead, :].add(-u) for v, u in zip(values, update))

    first = combine(2.0, guess, newton_product(guess, newton_product(blocks, guess)))
    left = part(guess, cols=lead)
    right = part(guess, rows=lead)

    applied_trail = newton_product(blocks, part(first, cols=trail))
    boundary = combine(
        2.0, part(first, trail, trail), newton_product(part(first, rows=trail), applied_trail)
    )
    applied_left = newton_product(blocks, left)

    for section in range(1, space_count - 1):
        incoming = from_behind(boundary, "space", 1)
        schur = schur_of(incoming)
        mixed = newton_product(schur, right)
        mixed_trail = part(mixed, cols=trail)
        step_trail = add(part(first, cols=trail), newton_product(left, mixed_trail))
        step_rows = add(part(first, rows=trail), newton_product(part(left, rows=trail), mixed))
        system_trail = add(applied_trail, newton_product(applied_left, mixed_trail))
        system_trail = lead_rows_minus(system_trail, schur, part(step_trail, rows=lead))
        boundary = combine(
            2.0, part(step_trail, rows=trail), newton_product(step_rows, system_trail)
        )

    applied = newton_product(blocks, first)
    if space_count > 1:
        incoming = from_behind(boundary, "space", 1)
        schur = schur_of(incoming)
        mixed = newton_product(schur, right)
        step = add(first, newton_product(left, mixed))
        system_step = add(applied, newton_product(applied_left, mixed))
        system_step = lead_rows_minus(system_step, schur, part(step, rows=lead))
    else:
        step = first
        system_step = applied
    return combine(2.0, step, newton_product(step, system_step))


def phonon_matrix(phonon_shift, phonon_strength, momentum_table, energies):
    momenta = momentum_table.shape[0]
    chosen = (
        momentum_table[:, :, None] == jnp.arange(momenta, dtype=jnp.int32)[None, None, :]
    ).astype(jnp.float32)
    momentum_mix = jnp.einsum("kqj,dwq->kjdw", chosen, phonon_strength, precision=HIGHEST)
    energy_rows = jnp.arange(energies, dtype=jnp.int32)
    energy_gap = energy_rows[None, :] - energy_rows[:, None]
    emission = (energy_gap[None, :, :] == -phonon_shift[:, None, None]).astype(jnp.float32)
    absorption = (energy_gap[None, :, :] == phonon_shift[:, None, None]).astype(jnp.float32)
    shift_table = jnp.stack([emission, absorption], axis=0)
    return jnp.einsum("kjdw,dwEF->kjEF", momentum_mix, shift_table, precision=HIGHEST)


def pick_kernel(partner_ref, real_ref, imag_ref, out_ref):
    energy_count, size, _ = real_ref.shape
    atoms = size // ORB
    per_atom = partner_ref.shape[0] // atoms
    width = per_atom * ORB
    groups = 2 * energy_count
    rows = groups * ORB
    flat = ORB * ORB

    spread_rows = lax.broadcasted_iota(jnp.int32, (width, flat), 0)
    spread_cols = lax.broadcasted_iota(jnp.int32, (width, flat), 1)
    spread = (spread_rows % ORB == spread_cols % ORB).astype(jnp.float32)
    keep_rows = lax.broadcasted_iota(jnp.int32, (per_atom * rows, flat), 0)
    keep_cols = lax.broadcasted_iota(jnp.int32, (per_atom * rows, flat), 1)
    keep = keep_rows % ORB == keep_cols // ORB
    total_rows = lax.broadcasted_iota(jnp.int32, (groups * per_atom, per_atom * rows), 0)
    total_cols = lax.broadcasted_iota(jnp.int32, (groups * per_atom, per_atom * rows), 1)
    total = (
        (total_cols // rows == total_rows % per_atom)
        & ((total_cols // ORB) % groups == total_rows // per_atom)
    ).astype(jnp.float32)
    lane_tile = lax.broadcasted_iota(jnp.int32, (rows, width), 1) // ORB
    pick_rows = lax.broadcasted_iota(jnp.int32, (size, width), 0)
    pick_cols = lax.broadcasted_iota(jnp.int32, (size, width), 1)

    def one_atom(atom, carry):
        target = jnp.zeros((size, width), jnp.int32)
        for j in range(per_atom):
            target = jnp.where(pick_cols // ORB == j, partner_ref[atom * per_atom + j], target)
        pick = (
            (pick_rows // ORB == target) & (pick_rows % ORB == pick_cols % ORB)
        ).astype(jnp.float32)
        start = pl.multiple_of(atom * ORB, ORB)
        stripes = []
        for e in range(energy_count):
            stripes.append(real_ref[e, pl.ds(start, ORB), :])
            stripes.append(imag_ref[e, pl.ds(start, ORB), :])
        stripes = jnp.concatenate(stripes, axis=0)
        chosen = jnp.dot(stripes, pick, precision=HIGHEST, preferred_element_type=jnp.float32)
        masked = jnp.concatenate(
            [jnp.where(lane_tile == j, chosen, 0.0) for j in range(per_atom)], axis=0
        )
        spread_out = jnp.dot(masked, spread, precision=HIGHEST, preferred_element_type=jnp.float32)
        spread_out = jnp.where(keep, spread_out, 0.0)
        summed = jnp.dot(total, spread_out, precision=HIGHEST, preferred_element_type=jnp.float32)
        out_start = pl.multiple_of(atom * per_atom, per_atom)
        for e in range(energy_count):
            for component in range(2):
                g = 2 * e + component
                out_ref[e, pl.ds(out_start, per_atom), pl.ds(component * flat, flat)] = summed[
                    g * per_atom : (g + 1) * per_atom, :
                ]
        return carry

    lax.fori_loop(0, atoms, one_atom, 0)


def pick_tiles(green_pair, pair_index):
    energy_count = green_pair[0].shape[0]
    pair_count = pair_index.shape[0]
    partner = pair_index % ATOMS
    return pl.pallas_call(
        pick_kernel,
        out_shape=jax.ShapeDtypeStruct((energy_count, pair_count, 2 * ORB * ORB), jnp.float32),
        in_specs=[
            pl.BlockSpec(memory_space=pltpu.SMEM),
            pl.BlockSpec(memory_space=pltpu.VMEM),
            pl.BlockSpec(memory_space=pltpu.VMEM),
        ],
        out_specs=pl.BlockSpec(memory_space=pltpu.VMEM),
    )(partner, green_pair[0], green_pair[1])


def body(
    blocks, inverse_guess, coupling, pair_index, phonon_shift, phonon_strength, momentum_table
):
    local_blocks = (blocks[:, 0, 0, 0], blocks[:, 0, 0, 1])
    local_guess = (inverse_guess[:, 0, 0, 0], inverse_guess[:, 0, 0, 1])
    coupling_block = (coupling[0, 0, 0], coupling[0, 0, 1])
    energy_count = blocks.shape[0]
    green_pair = sweep(local_blocks, local_guess, coupling_block)
    green_block = jnp.stack(green_pair, axis=1)
    picked = pick_tiles(green_pair, pair_index[0])[:, None, None]
    momenta = momentum_table.shape[0]
    energy_groups = lax.axis_size("energy")
    mixing = phonon_matrix(
        phonon_shift, phonon_strength, momentum_table, energy_count * energy_groups
    )
    by_pairs = lax.all_to_all(
        picked, ("energy", "momentum"), split_axis=3, concat_axis=1, tiled=True
    )
    pair_count = by_pairs.shape[3]
    arranged = by_pairs.reshape(energy_count, energy_groups, momenta, pair_count, by_pairs.shape[4])
    mixing_grid = mixing.reshape(
        momenta, momenta, energy_groups, energy_count, energy_groups, energy_count
    )
    summed = jnp.einsum("kjabcd,dcjpx->bakpx", mixing_grid, arranged, precision=HIGHEST)
    summed = summed.reshape(energy_count, energy_groups * momenta, 1, pair_count, by_pairs.shape[4])
    self_energy = lax.all_to_all(
        summed, ("energy", "momentum"), split_axis=1, concat_axis=3, tiled=True
    )
    return (green_block[:, None, None], self_energy)


def solution(mesh):
    return jax.shard_map(
        body,
        mesh=mesh,
        in_specs=(
            P("energy", "momentum", "space", None, None, None),
            P("energy", "momentum", "space", None, None, None),
            P("momentum", "space", None, None, None),
            P("space", None),
            P(),
            P(),
            P(),
        ),
        out_specs=(
            P("energy", "momentum", "space", None, None, None),
            P("energy", "momentum", "space", None, None),
        ),
        check_vma=False,
    )
```

profile of v0, /device:TPU:0, one launch (start us, length us, event | category | flops | bytes accessed | tf_op | source)
XLA Modules:
  0.0 112.6 jit_solution(14765784402443148257)
XLA Ops:
  0.7 1.9 %fusion.46 = f32[2,256,256]{2,1,0:T(8,128)S(1)} fusion(f32[2,1,1,2,256,256]{5,4,3,2,1,0:T(8,128)} %param.11, f32[2,1,1,2,256,256]{5,4,3,2,1,0:T(8,128)} %param.12), kind=kOutput, calls=%fused_computation.75 | convolution fusion | flops 402653184 | bytes 1572864 | tf_op jit(solution)/shard_map/dot_general | solution.py:26
  2.6 1.8 %fusion.44 = f32[2,256,256]{2,1,0:T(8,128)S(1)} fusion(f32[2,1,1,2,256,256]{5,4,3,2,1,0:T(8,128)S(1)} %copy-done.1, f32[2,1,1,2,256,256]{5,4,3,2,1,0:T(8,128)} %param.12), kind=kOutput, calls=%fused_computation.73 | convolution fusion | flops 402653184 | bytes 1572864 | tf_op jit(solution)/shard_map/dot_general | solution.py:29
  9.2 0.7 fusion.40
  9.9 0.7 convolution_subtract_fusion.9
  11.1 0.7 convolution_add_fusion.9
  12.2 4.9 %collective-permute-start = (f32[2,128,128]{2,1,0:T(8,128)S(1)}, f32[2,128,128]{2,1,0:T(8,128)S(1)}, u32[]{:S(2)}, u32[]{:S(2)}) collective-permute-start(f32[2,128,128]{2,1,0:T(8,128)S(1)} %fusion.21), channel_id=1, source_target_pairs={{0,1},{2,3},{4,5},{6,7},{8,9},{10,11},{12,13},{14,15},{16,17},{18,... | collective-permute-start | bytes 393224 | tf_op jit(solution)/shard_map/ppermute | solution.py:20
  17.9 1.5 %collective-permute-start.1 = (f32[2,128,128]{2,1,0:T(8,128)S(1)}, f32[2,128,128]{2,1,0:T(8,128)S(1)}, u32[]{:S(2)}, u32[]{:S(2)}) collective-permute-start(f32[2,128,128]{2,1,0:T(8,128)S(1)} %fusion.20), channel_id=1, source_target_pairs={{0,1},{2,3},{4,5},{6,7},{8,9},{10,11},{12,13},{14,15},{16,17},{18,... | collective-permute-start | bytes 393224 | tf_op jit(solution)/shard_map/ppermute | solution.py:20
  19.5 1.0 fusion.38
  20.5 1.0 fusion.32
  33.5 0.8 fusion.65
  35.0 1.0 fusion.5
  37.9 1.0 fusion.3
  40.3 1.5 %fusion.1.real_ref = f32[2,256,256]{2,1,0:T(8,128)} fusion(f32[2,256,256]{2,1,0:T(8,128)S(1)} %fusion.131, f32[2,256,256]{2,1,0:T(8,128)S(1)} %fusion.11, f32[2,256,256]{1,2,0:T(8,128)S(1)} %fusion.16, f32[2,256,256]{2,1,0:T(8,128)S(1)} %fusion.13), kind=kOutput, calls=%fused_computation.4 | convolution fusion | flops 403046400 | bytes 2621440 | tf_op jit(solution)/shard_map/dot_general | solution.py:26
  41.8 1.5 %fusion.imag_ref = f32[2,256,256]{2,1,0:T(8,128)} fusion(f32[2,256,256]{2,1,0:T(8,128)S(1)} %fusion.133, f32[2,256,256]{2,1,0:T(8,128)S(1)} %fusion.11, f32[2,256,256]{1,2,0:T(8,128)S(1)} %fusion.19), kind=kOutput, calls=%fused_computation.2 | convolution fusion | flops 403046400 | bytes 2097152 | tf_op jit(solution)/shard_map/dot_general | solution.py:29
  43.3 24.4 %shard_map.86 = f32[2,128,512]{2,1,0:T(8,128)} custom-call(s32[128]{0:T(128)} %and_select_fusion.partner_ref, f32[2,256,256]{2,1,0:T(8,128)} %fusion.1.real_ref, f32[2,256,256]{2,1,0:T(8,128)} %fusion.imag_ref), custom_call_target="tpu_custom_call" | custom-call | tf_op jit(solution)/shard_map/pallas_call | solution.py:178
  67.7 2.2 %copy.216 = f32[2,1,1,128,512]{4,0,2,1,3:T(2,128)} copy(f32[2,1,1,128,512]{4,3,0,2,1:T(8,128)} %bitcast.212) | data formatting | bytes 1048576 | tf_op jit(solution)/shard_map/broadcast_in_dim | solution.py:199
  69.9 6.1 %all-to-all-start = ((f32[2,1,1,128,512]{4,0,2,1,3:T(2,128)}), f32[2,1,1,128,512]{4,0,2,1,3:T(2,128)S(1)}, u32[]{:S(2)}, u32[]{:S(2)}) async-start(f32[2,1,1,128,512]{4,0,2,1,3:T(2,128)} %copy.216), calls=%async_computation | async-start | bytes 1048576 | tf_op jit(solution)/shard_map/all_to_all | solution.py:205
  77.2 13.2 %all-to-all-done = f32[2,1,1,128,512]{4,0,2,1,3:T(2,128)S(1)} async-done(((f32[2,1,1,128,512]{4,0,2,1,3:T(2,128)}), f32[2,1,1,128,512]{4,0,2,1,3:T(2,128)S(1)}, u32[]{:S(2)}, u32[]{:S(2)}) %all-to-all-start) | async-done | bytes 524320 | tf_op jit(solution)/shard_map/all_to_all | solution.py:205
  90.5 1.5 %convolution_bitcast_fusion = f32[2,4,4,8,512]{4,1,0,2,3:T(4,128)S(1)} fusion(f32[2,4,4,8,512,1,1]{4,0,3,2,1,6,5:T(2,128)S(1)} %bitcast.213, f32[4,4,4,2,4,2]{1,5,4,3,2,0:T(2,128)S(1)} %bitcast.215), kind=kOutput, calls=%fused_computation | convolution fusion | flops 50331648 | bytes 1052672 | tf_op jit(solution)/shard_map/kjabcd,dcjpx->bakpx/dot_general | solution.py:213
  91.9 1.1 copy.280
  93.0 4.2 %all-to-all-start.1 = ((f32[2,16,1,8,512]{4,3,0,2,1:T(8,128)}), f32[2,16,1,8,512]{4,3,0,2,1:T(8,128)S(1)}, u32[]{:S(2)}, u32[]{:S(2)}) async-start(f32[2,16,1,8,512]{4,3,0,2,1:T(8,128)} %bitcast.39), calls=%async_computation.1 | async-start | bytes 1048576 | tf_op jit(solution)/shard_map/all_to_all | solution.py:215
  97.4 1.0 copy.224
  98.4 13.3 %all-to-all-done.1 = f32[2,16,1,8,512]{4,3,0,2,1:T(8,128)S(1)} async-done(((f32[2,16,1,8,512]{4,3,0,2,1:T(8,128)}), f32[2,16,1,8,512]{4,3,0,2,1:T(8,128)S(1)}, u32[]{:S(2)}, u32[]{:S(2)}) %all-to-all-start.1) | async-done | bytes 524320 | tf_op jit(solution)/shard_map/all_to_all | solution.py:215
  111.7 0.8 copy.292
  (68 shorter events, 23.2 us)
Async XLA Ops:
  0.6 75.4 %copy-start = (f32[2,8,4]{1,2,0:T(4,128)S(1)}, f32[2,8,4]{1,2,0:T(4,128)}, u32[]{:S(2)}) copy-start(f32[2,8,4]{1,2,0:T(4,128)} %param.16) | copy-start | bytes 772
  0.6 2.0 %copy-start.1 = (f32[2,1,1,2,256,256]{5,4,3,2,1,0:T(8,128)S(1)}, f32[2,1,1,2,256,256]{5,4,3,2,1,0:T(8,128)}, u32[]{:S(2)}) copy-start(f32[2,1,1,2,256,256]{5,4,3,2,1,0:T(8,128)} %param.11) | copy-start | bytes 3145732
  2.6 1.8 %copy-start.2 = (f32[2,1,1,2,256,256]{5,4,3,2,1,0:T(8,128)S(1)}, f32[2,1,1,2,256,256]{5,4,3,2,1,0:T(8,128)}, u32[]{:S(2)}) copy-start(f32[2,1,1,2,256,256]{5,4,3,2,1,0:T(8,128)} %param.12) | copy-start | bytes 3145732
  12.2 12.8 %collective-permute-start = (f32[2,128,128]{2,1,0:T(8,128)S(1)}, f32[2,128,128]{2,1,0:T(8,128)S(1)}, u32[]{:S(2)}, u32[]{:S(2)}) collective-permute-start(f32[2,128,128]{2,1,0:T(8,128)S(1)} %fusion.21), channel_id=1, source_target_pairs={{0,1},{2,3},{4,5},{6,7},{8,9},{10,11},{12,13},{14,15},{16,17},{18,... | collective-permute-start | bytes 393224 | tf_op jit(solution)/shard_map/ppermute | solution.py:20
  17.9 6.7 %collective-permute-start.1 = (f32[2,128,128]{2,1,0:T(8,128)S(1)}, f32[2,128,128]{2,1,0:T(8,128)S(1)}, u32[]{:S(2)}, u32[]{:S(2)}) collective-permute-start(f32[2,128,128]{2,1,0:T(8,128)S(1)} %fusion.20), channel_id=1, source_target_pairs={{0,1},{2,3},{4,5},{6,7},{8,9},{10,11},{12,13},{14,15},{16,17},{18,... | collective-permute-start | bytes 393224 | tf_op jit(solution)/shard_map/ppermute | solution.py:20
  23.4 0.7 copy-start.8
  23.4 1.1 %copy-start.5 = (f32[1,1,2,128,128]{4,3,2,1,0:T(8,128)S(1)}, f32[1,1,2,128,128]{4,3,2,1,0:T(8,128)}, u32[]{:S(2)}) copy-start(f32[1,1,2,128,128]{4,3,2,1,0:T(8,128)} %param.13) | copy-start | bytes 393220
  69.9 6.1 %copy-start.7 = (s32[8]{0:T(128)S(1)}, s32[8]{0:T(128)}, u32[]{:S(2)}) copy-start(s32[8]{0:T(128)} %param.15) | copy-start | bytes 100
  69.9 20.5 %all-to-all-start = ((f32[2,1,1,128,512]{4,0,2,1,3:T(2,128)}), f32[2,1,1,128,512]{4,0,2,1,3:T(2,128)S(1)}, u32[]{:S(2)}, u32[]{:S(2)}) async-start(f32[2,1,1,128,512]{4,0,2,1,3:T(2,128)} %copy.216), calls=%async_computation | async-start | bytes 1048576 | tf_op jit(solution)/shard_map/all_to_all | solution.py:205
  76.0 0.7 copy-start.6
  93.0 4.2 %copy-start.3 = (f32[2,256,256]{2,1,0:T(8,128)S(1)}, f32[2,256,256]{2,1,0:T(8,128)}, u32[]{:S(2)}) copy-start(f32[2,256,256]{2,1,0:T(8,128)} %fusion.1.real_ref) | copy-start | bytes 1572868
  93.0 4.2 %copy-start.4 = (f32[2,256,256]{2,1,0:T(8,128)S(1)}, f32[2,256,256]{2,1,0:T(8,128)}, u32[]{:S(2)}) copy-start(f32[2,256,256]{2,1,0:T(8,128)} %fusion.imag_ref) | copy-start | bytes 1572868
  93.0 18.7 %all-to-all-start.1 = ((f32[2,16,1,8,512]{4,3,0,2,1:T(8,128)}), f32[2,16,1,8,512]{4,3,0,2,1:T(8,128)S(1)}, u32[]{:S(2)}, u32[]{:S(2)}) async-start(f32[2,16,1,8,512]{4,3,0,2,1:T(8,128)} %bitcast.39), calls=%async_computation.1 | async-start | bytes 1048576 | tf_op jit(solution)/shard_map/all_to_all | solution.py:215
where the time goes:
time: 113 us
  matrix products  37.1 us (33%)
  waiting for transfers between devices  26.6 us (24%)
  Pallas kernels  24.4 us (22%)
  starting transfers between devices  16.6 us (15%)
  local copies, waits for them, and re-layouts  6.02 us (5%)
  between operations  1.2 us (1%)
    pallas_call x1, Pallas kernels, pick_tiles(): pl.pallas_call(pick_kernel, out_shape=jax.ShapeDtypeStruct((energy_count,...  24.4 us
    all_to_all x1, waiting for transfers between devices, body(): lax.all_to_all(summed, ('energy', 'momentum'), split_axis=1, concat_axis=...  13.3 us
    all_to_all x1, waiting for transfers between devices, body(): lax.all_to_all(picked, ('energy', 'momentum'), split_axis=3, concat_axis=...  13.2 us
    dot_general x13, matrix products, complex_product(): jnp.matmul(first_real, second_imag, precision=precision)  9.04 us
    dot_general x13, matrix products, complex_product(): jnp.matmul(first_real, second_real, precision=precision)  8.96 us
    dot_general x13, matrix products, complex_product(): jnp.matmul(first_imag, second_imag, precision=precision)  8.59 us
    dot_general x13, matrix products, complex_product(): jnp.matmul(first_imag, second_real, precision=precision)  8.59 us
    ppermute x2, starting transfers between devices, from_behind(): return lax.ppermute(shard, axis, pairs)  6.36 us
  transfers between devices with their start and end apart: 4, of which 2 were waited for; matrix products, arithmetic and copies ran while one was open for 7% of the time, Pallas kernels for 0%

commit v1 on v0

--- a/solution.py
+++ b/solution.py
@@ -11,7 +11,7 @@
 
 
 HIGHEST = lax.Precision.HIGHEST
-NEWTON_PRECISION = lax.Precision.HIGHEST
+NEWTON_PRECISION = lax.Precision.HIGH
 
 
 def from_behind(shard, axis, by):

time: 113 us -> 103 us (0.912)
  matrix products: 37.1 us -> 26.9 us
    dot_general x13, matrix products: 8.59 us -> 6.04 us  [complex_product(): jnp.matmul(first_imag, second_imag, precision=precision)]
    dot_general x13, matrix products: 9.04 us -> 6.49 us  [complex_product(): jnp.matmul(first_real, second_imag, precision=precision)]
    dot_general x13, matrix products: 8.96 us -> 6.42 us  [complex_product(): jnp.matmul(first_real, second_real, precision=precision)]
    dot_general x13, matrix products: 8.59 us -> 6.05 us  [complex_product(): jnp.matmul(first_imag, second_real, precision=precision)]
  transfers between devices with their start and end apart: 4 -> 4, of which waited for: 2 -> 2; matrix products, arithmetic and copies ran while one was open for 7% -> 6% of each run, Pallas kernels for 0% -> 0%
where the time goes in v1:
time: 103 us
  matrix products  26.9 us (26%)
  waiting for transfers between devices  26.6 us (26%)
  Pallas kernels  24.4 us (24%)
  starting transfers between devices  16.6 us (16%)
  local copies, waits for them, and re-layouts  6.24 us (6%)
  between operations  1.2 us (1%)
    pallas_call x1, Pallas kernels, pick_tiles(): pl.pallas_call(pick_kernel, out_shape=jax.ShapeDtypeStruct((energy_count,...  24.4 us
    all_to_all x1, waiting for transfers between devices, body(): lax.all_to_all(summed, ('energy', 'momentum'), split_axis=1, concat_axis=...  13.3 us
    all_to_all x1, waiting for transfers between devices, body(): lax.all_to_all(picked, ('energy', 'momentum'), split_axis=3, concat_axis=...  13.2 us
    dot_general x13, matrix products, complex_product(): jnp.matmul(first_real, second_imag, precision=precision)  6.49 us
    dot_general x13, matrix products, complex_product(): jnp.matmul(first_real, second_real, precision=precision)  6.42 us
    ppermute x2, starting transfers between devices, from_behind(): return lax.ppermute(shard, axis, pairs)  6.36 us
    dot_general x13, matrix products, complex_product(): jnp.matmul(first_imag, second_real, precision=precision)  6.05 us
    all_to_all x1, starting transfers between devices, body(): lax.all_to_all(picked, ('energy', 'momentum'), split_axis=3, concat_axis=...  6.04 us
  transfers between devices with their start and end apart: 4, of which 2 were waited for; matrix products, arithmetic and copies ran while one was open for 6% of the time, Pallas kernels for 0%

profile of v1, /device:TPU:0, one launch (start us, length us, event | category | flops | bytes accessed | tf_op | source)
XLA Modules:
  0.0 102.6 jit_solution(13403854456778008352)
XLA Ops:
  0.7 1.7 %fusion.46 = f32[2,256,256]{2,1,0:T(8,128)S(1)} fusion(f32[2,1,1,2,256,256]{5,4,3,2,1,0:T(8,128)} %param.11, f32[2,1,1,2,256,256]{5,4,3,2,1,0:T(8,128)} %param.12), kind=kOutput, calls=%fused_computation.75 | convolution fusion | flops 201326592 | bytes 1572864 | tf_op jit(solution)/shard_map/dot_general | solution.py:26
  2.4 1.5 %fusion.44 = f32[2,256,256]{2,1,0:T(8,128)S(1)} fusion(f32[2,1,1,2,256,256]{5,4,3,2,1,0:T(8,128)S(1)} %copy-done.1, f32[2,1,1,2,256,256]{5,4,3,2,1,0:T(8,128)} %param.12), kind=kOutput, calls=%fused_computation.73 | convolution fusion | flops 201326592 | bytes 1572864 | tf_op jit(solution)/shard_map/dot_general | solution.py:29
  7.3 0.4 convolution_subtract_fusion.9
  8.7 4.9 %collective-permute-start = (f32[2,128,128]{2,1,0:T(8,128)S(1)}, f32[2,128,128]{2,1,0:T(8,128)S(1)}, u32[]{:S(2)}, u32[]{:S(2)}) collective-permute-start(f32[2,128,128]{2,1,0:T(8,128)S(1)} %fusion.21), channel_id=1, source_target_pairs={{0,1},{2,3},{4,5},{6,7},{8,9},{10,11},{12,13},{14,15},{16,17},{18,... | collective-permute-start | bytes 393224 | tf_op jit(solution)/shard_map/ppermute | solution.py:20
  14.2 1.5 %collective-permute-start.1 = (f32[2,128,128]{2,1,0:T(8,128)S(1)}, f32[2,128,128]{2,1,0:T(8,128)S(1)}, u32[]{:S(2)}, u32[]{:S(2)}) collective-permute-start(f32[2,128,128]{2,1,0:T(8,128)S(1)} %fusion.20), channel_id=1, source_target_pairs={{0,1},{2,3},{4,5},{6,7},{8,9},{10,11},{12,13},{14,15},{16,17},{18,... | collective-permute-start | bytes 393224 | tf_op jit(solution)/shard_map/ppermute | solution.py:20
  15.8 0.6 fusion.38
  16.4 0.6 fusion.32
  18.9 0.5 and_select_fusion.partner_ref
  27.2 0.6 fusion.5
  29.1 0.6 fusion.3
  30.2 0.6 fusion.133
  30.8 1.2 %fusion.1.real_ref = f32[2,256,256]{2,1,0:T(8,128)} fusion(f32[2,256,256]{2,1,0:T(8,128)S(1)} %fusion.131, f32[2,256,256]{2,1,0:T(8,128)S(1)} %fusion.11, f32[2,256,256]{1,2,0:T(8,128)S(1)} %fusion.16, f32[2,256,256]{2,1,0:T(8,128)S(1)} %fusion.13), kind=kOutput, calls=%fused_computation.4 | convolution fusion | flops 201719808 | bytes 2621440 | tf_op jit(solution)/shard_map/dot_general | solution.py:26
  32.1 1.2 %fusion.imag_ref = f32[2,256,256]{2,1,0:T(8,128)} fusion(f32[2,256,256]{2,1,0:T(8,128)S(1)} %fusion.133, f32[2,256,256]{2,1,0:T(8,128)S(1)} %fusion.11, f32[2,256,256]{1,2,0:T(8,128)S(1)} %fusion.19), kind=kOutput, calls=%fused_computation.2 | convolution fusion | flops 201719808 | bytes 2097152 | tf_op jit(solution)/shard_map/dot_general | solution.py:29
  33.3 24.4 %shard_map.86 = f32[2,128,512]{2,1,0:T(8,128)} custom-call(s32[128]{0:T(128)} %and_select_fusion.partner_ref, f32[2,256,256]{2,1,0:T(8,128)} %fusion.1.real_ref, f32[2,256,256]{2,1,0:T(8,128)} %fusion.imag_ref), custom_call_target="tpu_custom_call" | custom-call | tf_op jit(solution)/shard_map/pallas_call | solution.py:178
  57.7 2.2 %copy.216 = f32[2,1,1,128,512]{4,0,2,1,3:T(2,128)} copy(f32[2,1,1,128,512]{4,3,0,2,1:T(8,128)} %bitcast.212) | data formatting | bytes 1048576 | tf_op jit(solution)/shard_map/broadcast_in_dim | solution.py:199
  60.0 6.0 %all-to-all-start = ((f32[2,1,1,128,512]{4,0,2,1,3:T(2,128)}), f32[2,1,1,128,512]{4,0,2,1,3:T(2,128)S(1)}, u32[]{:S(2)}, u32[]{:S(2)}) async-start(f32[2,1,1,128,512]{4,0,2,1,3:T(2,128)} %copy.216), calls=%async_computation | async-start | bytes 1048576 | tf_op jit(solution)/shard_map/all_to_all | solution.py:205
  66.1 0.7 copy-done.6
  67.3 13.2 %all-to-all-done = f32[2,1,1,128,512]{4,0,2,1,3:T(2,128)S(1)} async-done(((f32[2,1,1,128,512]{4,0,2,1,3:T(2,128)}), f32[2,1,1,128,512]{4,0,2,1,3:T(2,128)S(1)}, u32[]{:S(2)}, u32[]{:S(2)}) %all-to-all-start) | async-done | bytes 524320 | tf_op jit(solution)/shard_map/all_to_all | solution.py:205
  80.5 1.5 %convolution_bitcast_fusion = f32[2,4,4,8,512]{4,1,0,2,3:T(4,128)S(1)} fusion(f32[2,4,4,8,512,1,1]{4,0,3,2,1,6,5:T(2,128)S(1)} %bitcast.213, f32[4,4,4,2,4,2]{1,5,4,3,2,0:T(2,128)S(1)} %bitcast.215), kind=kOutput, calls=%fused_computation | convolution fusion | flops 50331648 | bytes 1052672 | tf_op jit(solution)/shard_map/kjabcd,dcjpx->bakpx/dot_general | solution.py:213
  82.0 1.1 %copy.280 = f32[2,4,4,8,512]{4,3,0,2,1:T(8,128)} copy(f32[2,4,4,8,512]{4,1,0,2,3:T(4,128)S(1)} %convolution_bitcast_fusion) | data formatting | bytes 1048576 | tf_op jit(solution)/shard_map/reshape | solution.py:214
  83.1 4.2 %all-to-all-start.1 = ((f32[2,16,1,8,512]{4,3,0,2,1:T(8,128)}), f32[2,16,1,8,512]{4,3,0,2,1:T(8,128)S(1)}, u32[]{:S(2)}, u32[]{:S(2)}) async-start(f32[2,16,1,8,512]{4,3,0,2,1:T(8,128)} %bitcast.39), calls=%async_computation.1 | async-start | bytes 1048576 | tf_op jit(solution)/shard_map/all_to_all | solution.py:215
  87.4 1.0 %copy.224 = f32[2,1,1,2,256,256]{5,4,3,2,1,0:T(8,128)} copy(f32[2,1,1,2,256,256]{5,4,0,3,2,1:T(8,128)S(1)} %maximum_bitcast_fusion) | data formatting | bytes 2097152
  88.4 13.3 %all-to-all-done.1 = f32[2,16,1,8,512]{4,3,0,2,1:T(8,128)S(1)} async-done(((f32[2,16,1,8,512]{4,3,0,2,1:T(8,128)}), f32[2,16,1,8,512]{4,3,0,2,1:T(8,128)S(1)}, u32[]{:S(2)}, u32[]{:S(2)}) %all-to-all-start.1) | async-done | bytes 524320 | tf_op jit(solution)/shard_map/all_to_all | solution.py:215
  101.8 0.8 copy.292
  (68 shorter events, 16.6 us)
Async XLA Ops:
  0.6 65.4 %copy-start = (f32[2,8,4]{1,2,0:T(4,128)S(1)}, f32[2,8,4]{1,2,0:T(4,128)}, u32[]{:S(2)}) copy-start(f32[2,8,4]{1,2,0:T(4,128)} %param.16) | copy-start | bytes 772
  0.6 1.7 %copy-start.1 = (f32[2,1,1,2,256,256]{5,4,3,2,1,0:T(8,128)S(1)}, f32[2,1,1,2,256,256]{5,4,3,2,1,0:T(8,128)}, u32[]{:S(2)}) copy-start(f32[2,1,1,2,256,256]{5,4,3,2,1,0:T(8,128)} %param.11) | copy-start | bytes 3145732
  2.3 1.5 %copy-start.2 = (f32[2,1,1,2,256,256]{5,4,3,2,1,0:T(8,128)S(1)}, f32[2,1,1,2,256,256]{5,4,3,2,1,0:T(8,128)}, u32[]{:S(2)}) copy-start(f32[2,1,1,2,256,256]{5,4,3,2,1,0:T(8,128)} %param.12) | copy-start | bytes 3145732
  8.7 11.1 %collective-permute-start = (f32[2,128,128]{2,1,0:T(8,128)S(1)}, f32[2,128,128]{2,1,0:T(8,128)S(1)}, u32[]{:S(2)}, u32[]{:S(2)}) collective-permute-start(f32[2,128,128]{2,1,0:T(8,128)S(1)} %fusion.21), channel_id=1, source_target_pairs={{0,1},{2,3},{4,5},{6,7},{8,9},{10,11},{12,13},{14,15},{16,17},{18,... | collective-permute-start | bytes 393224 | tf_op jit(solution)/shard_map/ppermute | solution.py:20
  14.2 5.2 %collective-permute-start.1 = (f32[2,128,128]{2,1,0:T(8,128)S(1)}, f32[2,128,128]{2,1,0:T(8,128)S(1)}, u32[]{:S(2)}, u32[]{:S(2)}) collective-permute-start(f32[2,128,128]{2,1,0:T(8,128)S(1)} %fusion.20), channel_id=1, source_target_pairs={{0,1},{2,3},{4,5},{6,7},{8,9},{10,11},{12,13},{14,15},{16,17},{18,... | collective-permute-start | bytes 393224 | tf_op jit(solution)/shard_map/ppermute | solution.py:20
  18.2 0.7 copy-start.8
  18.2 1.1 %copy-start.5 = (f32[1,1,2,128,128]{4,3,2,1,0:T(8,128)S(1)}, f32[1,1,2,128,128]{4,3,2,1,0:T(8,128)}, u32[]{:S(2)}) copy-start(f32[1,1,2,128,128]{4,3,2,1,0:T(8,128)} %param.13) | copy-start | bytes 393220
  60.0 6.1 %copy-start.7 = (s32[8]{0:T(128)S(1)}, s32[8]{0:T(128)}, u32[]{:S(2)}) copy-start(s32[8]{0:T(128)} %param.15) | copy-start | bytes 100
  60.0 20.5 %all-to-all-start = ((f32[2,1,1,128,512]{4,0,2,1,3:T(2,128)}), f32[2,1,1,128,512]{4,0,2,1,3:T(2,128)S(1)}, u32[]{:S(2)}, u32[]{:S(2)}) async-start(f32[2,1,1,128,512]{4,0,2,1,3:T(2,128)} %copy.216), calls=%async_computation | async-start | bytes 1048576 | tf_op jit(solution)/shard_map/all_to_all | solution.py:205
  66.0 0.7 copy-start.6
  83.1 4.2 %copy-start.3 = (f32[2,256,256]{2,1,0:T(8,128)S(1)}, f32[2,256,256]{2,1,0:T(8,128)}, u32[]{:S(2)}) copy-start(f32[2,256,256]{2,1,0:T(8,128)} %fusion.1.real_ref) | copy-start | bytes 1572868
  83.1 4.2 %copy-start.4 = (f32[2,256,256]{2,1,0:T(8,128)S(1)}, f32[2,256,256]{2,1,0:T(8,128)}, u32[]{:S(2)}) copy-start(f32[2,256,256]{2,1,0:T(8,128)} %fusion.imag_ref) | copy-start | bytes 1572868
  83.1 18.7 %all-to-all-start.1 = ((f32[2,16,1,8,512]{4,3,0,2,1:T(8,128)}), f32[2,16,1,8,512]{4,3,0,2,1:T(8,128)S(1)}, u32[]{:S(2)}, u32[]{:S(2)}) async-start(f32[2,16,1,8,512]{4,3,0,2,1:T(8,128)} %bitcast.39), calls=%async_computation.1 | async-start | bytes 1048576 | tf_op jit(solution)/shard_map/all_to_all | solution.py:215

commit v2 on v1

--- a/solution.py
+++ b/solution.py
@@ -11,7 +11,7 @@
 
 
 HIGHEST = lax.Precision.HIGHEST
-NEWTON_PRECISION = lax.Precision.HIGH
+FIRST_STEP_PRECISION = lax.Precision.HIGH
 
 
 def from_behind(shard, axis, by):
@@ -33,7 +33,11 @@
 
 
 def newton_product(first_factor, second_factor):
-    return complex_product(first_factor, second_factor, NEWTON_PRECISION)
+    return complex_product(first_factor, second_factor, HIGHEST)
+
+
+def first_step_product(first_factor, second_factor):
+    return complex_product(first_factor, second_factor, FIRST_STEP_PRECISION)
 
 
 def part(pair, rows=slice(None), cols=slice(None)):
@@ -63,7 +67,7 @@
         update = newton_product(schur, rows)
         return tuple(v.at[..., lead, :].add(-u) for v, u in zip(values, update))
 
-    first = combine(2.0, guess, newton_product(guess, newton_product(blocks, guess)))
+    first = combine(2.0, guess, first_step_product(guess, first_step_product(blocks, guess)))
     left = part(guess, cols=lead)
     right = part(guess, rows=lead)
 
@@ -76,7 +80,7 @@
     for section in range(1, space_count - 1):
         incoming = from_behind(boundary, "space", 1)
         schur = schur_of(incoming)
-        mixed = newton_product(schur, right)
+        mixed = first_step_product(schur, right)
         mixed_trail = part(mixed, cols=trail)
         step_trail = add(part(first, cols=trail), newton_product(left, mixed_trail))
         step_rows = add(part(first, rows=trail), newton_product(part(left, rows=trail), mixed))
@@ -90,7 +94,7 @@
     if space_count > 1:
         incoming = from_behind(boundary, "space", 1)
         schur = schur_of(incoming)
-        mixed = newton_product(schur, right)
+        mixed = first_step_product(schur, right)
         step = add(first, newton_product(left, mixed))
         system_step = add(applied, newton_product(applied_left, mixed))
         system_step = lead_rows_minus(system_step, schur, part(step, rows=lead))

time: 103 us -> 111 us (1.078)
  matrix products: 26.9 us -> 34.5 us
    dot_general x13, matrix products: 6.04 us -> 7.96 us  [complex_product(): jnp.matmul(first_imag, second_imag, precision=precision)]
    dot_general x13, matrix products: 6.42 us -> 8.33 us  [complex_product(): jnp.matmul(first_real, second_real, precision=precision)]
    dot_general x13, matrix products: 6.05 us -> 7.96 us  [complex_product(): jnp.matmul(first_imag, second_real, precision=precision)]
    dot_general x13, matrix products: 6.49 us -> 8.35 us  [complex_product(): jnp.matmul(first_real, second_imag, precision=precision)]
  transfers between devices with their start and end apart: 4 -> 4, of which waited for: 2 -> 2; matrix products, arithmetic and copies ran while one was open for 6% -> 7% of each run, Pallas kernels for 0% -> 0%
where the time goes in v2:
time: 111 us; the launch traced here: 110 us
  matrix products  34.5 us (31%)
  waiting for transfers between devices  26.6 us (24%)
  Pallas kernels  24.4 us (22%)
  starting transfers between devices  16.6 us (15%)
  local copies, waits for them, and re-layouts  6.02 us (5%)
  between operations  1.2 us (1%)
    pallas_call x1, Pallas kernels, pick_tiles(): pl.pallas_call(pick_kernel, out_shape=jax.ShapeDtypeStruct((energy_count,...  24.4 us
    all_to_all x1, waiting for transfers between devices, body(): lax.all_to_all(summed, ('energy', 'momentum'), split_axis=1, concat_axis=...  13.3 us
    all_to_all x1, waiting for transfers between devices, body(): lax.all_to_all(picked, ('energy', 'momentum'), split_axis=3, concat_axis=...  13.2 us
    dot_general x13, matrix products, complex_product(): jnp.matmul(first_real, second_imag, precision=precision)  8.35 us
    dot_general x13, matrix products, complex_product(): jnp.matmul(first_real, second_real, precision=precision)  8.33 us
    dot_general x13, matrix products, complex_product(): jnp.matmul(first_imag, second_real, precision=precision)  7.96 us
    dot_general x13, matrix products, complex_product(): jnp.matmul(first_imag, second_imag, precision=precision)  7.96 us
    ppermute x2, starting transfers between devices, from_behind(): return lax.ppermute(shard, axis, pairs)  6.36 us
  transfers between devices with their start and end apart: 4, of which 2 were waited for; matrix products, arithmetic and copies ran while one was open for 7% of the time, Pallas kernels for 0%

profile of v2, /device:TPU:0, one launch (start us, length us, event | category | flops | bytes accessed | tf_op | source)
XLA Modules:
  0.0 110.0 jit_solution(921296685072645556)
XLA Ops:
  0.7 1.7 %fusion.46 = f32[2,256,256]{2,1,0:T(8,128)S(1)} fusion(f32[2,1,1,2,256,256]{5,4,3,2,1,0:T(8,128)} %param.11, f32[2,1,1,2,256,256]{5,4,3,2,1,0:T(8,128)} %param.12), kind=kOutput, calls=%fused_computation.75 | convolution fusion | flops 201326592 | bytes 1572864 | tf_op jit(solution)/shard_map/dot_general | solution.py:26
  2.4 1.5 %fusion.44 = f32[2,256,256]{2,1,0:T(8,128)S(1)} fusion(f32[2,1,1,2,256,256]{5,4,3,2,1,0:T(8,128)S(1)} %copy-done.1, f32[2,1,1,2,256,256]{5,4,3,2,1,0:T(8,128)} %param.12), kind=kOutput, calls=%fused_computation.73 | convolution fusion | flops 201326592 | bytes 1572864 | tf_op jit(solution)/shard_map/dot_general | solution.py:29
  7.1 0.7 fusion.40
  7.8 0.7 convolution_subtract_fusion.9
  9.0 0.7 convolution_add_fusion.9
  10.1 4.9 %collective-permute-start = (f32[2,128,128]{2,1,0:T(8,128)S(1)}, f32[2,128,128]{2,1,0:T(8,128)S(1)}, u32[]{:S(2)}, u32[]{:S(2)}) collective-permute-start(f32[2,128,128]{2,1,0:T(8,128)S(1)} %fusion.21), channel_id=1, source_target_pairs={{0,1},{2,3},{4,5},{6,7},{8,9},{10,11},{12,13},{14,15},{16,17},{18,... | collective-permute-start | bytes 393224 | tf_op jit(solution)/shard_map/ppermute | solution.py:20
  15.8 1.5 %collective-permute-start.1 = (f32[2,128,128]{2,1,0:T(8,128)S(1)}, f32[2,128,128]{2,1,0:T(8,128)S(1)}, u32[]{:S(2)}, u32[]{:S(2)}) collective-permute-start(f32[2,128,128]{2,1,0:T(8,128)S(1)} %fusion.20), channel_id=1, source_target_pairs={{0,1},{2,3},{4,5},{6,7},{8,9},{10,11},{12,13},{14,15},{16,17},{18,... | collective-permute-start | bytes 393224 | tf_op jit(solution)/shard_map/ppermute | solution.py:20
  17.4 1.0 fusion.38
  18.4 1.0 fusion.32
  31.0 0.8 fusion.65
  32.4 1.0 fusion.5
  35.4 1.0 fusion.3
  37.7 1.5 %fusion.1.real_ref = f32[2,256,256]{2,1,0:T(8,128)} fusion(f32[2,256,256]{2,1,0:T(8,128)S(1)} %fusion.131, f32[2,256,256]{2,1,0:T(8,128)S(1)} %fusion.11, f32[2,256,256]{1,2,0:T(8,128)S(1)} %fusion.16, f32[2,256,256]{2,1,0:T(8,128)S(1)} %fusion.13), kind=kOutput, calls=%fused_computation.4 | convolution fusion | flops 403046400 | bytes 2621440 | tf_op jit(solution)/shard_map/dot_general | solution.py:26
  39.2 1.5 %fusion.imag_ref = f32[2,256,256]{2,1,0:T(8,128)} fusion(f32[2,256,256]{2,1,0:T(8,128)S(1)} %fusion.133, f32[2,256,256]{2,1,0:T(8,128)S(1)} %fusion.11, f32[2,256,256]{1,2,0:T(8,128)S(1)} %fusion.19), kind=kOutput, calls=%fused_computation.2 | convolution fusion | flops 403046400 | bytes 2097152 | tf_op jit(solution)/shard_map/dot_general | solution.py:29
  40.7 24.4 %shard_map.86 = f32[2,128,512]{2,1,0:T(8,128)} custom-call(s32[128]{0:T(128)} %and_select_fusion.partner_ref, f32[2,256,256]{2,1,0:T(8,128)} %fusion.1.real_ref, f32[2,256,256]{2,1,0:T(8,128)} %fusion.imag_ref), custom_call_target="tpu_custom_call" | custom-call | tf_op jit(solution)/shard_map/pallas_call | solution.py:182
  65.1 2.2 %copy.216 = f32[2,1,1,128,512]{4,0,2,1,3:T(2,128)} copy(f32[2,1,1,128,512]{4,3,0,2,1:T(8,128)} %bitcast.212) | data formatting | bytes 1048576 | tf_op jit(solution)/shard_map/broadcast_in_dim | solution.py:203
  67.4 6.0 %all-to-all-start = ((f32[2,1,1,128,512]{4,0,2,1,3:T(2,128)}), f32[2,1,1,128,512]{4,0,2,1,3:T(2,128)S(1)}, u32[]{:S(2)}, u32[]{:S(2)}) async-start(f32[2,1,1,128,512]{4,0,2,1,3:T(2,128)} %copy.216), calls=%async_computation | async-start | bytes 1048576 | tf_op jit(solution)/shard_map/all_to_all | solution.py:209
  74.7 13.2 %all-to-all-done = f32[2,1,1,128,512]{4,0,2,1,3:T(2,128)S(1)} async-done(((f32[2,1,1,128,512]{4,0,2,1,3:T(2,128)}), f32[2,1,1,128,512]{4,0,2,1,3:T(2,128)S(1)}, u32[]{:S(2)}, u32[]{:S(2)}) %all-to-all-start) | async-done | bytes 524320 | tf_op jit(solution)/shard_map/all_to_all | solution.py:209
  87.9 1.5 %convolution_bitcast_fusion = f32[2,4,4,8,512]{4,1,0,2,3:T(4,128)S(1)} fusion(f32[2,4,4,8,512,1,1]{4,0,3,2,1,6,5:T(2,128)S(1)} %bitcast.213, f32[4,4,4,2,4,2]{1,5,4,3,2,0:T(2,128)S(1)} %bitcast.215), kind=kOutput, calls=%fused_computation | convolution fusion | flops 50331648 | bytes 1052672 | tf_op jit(solution)/shard_map/kjabcd,dcjpx->bakpx/dot_general | solution.py:217
  89.4 1.1 %copy.280 = f32[2,4,4,8,512]{4,3,0,2,1:T(8,128)} copy(f32[2,4,4,8,512]{4,1,0,2,3:T(4,128)S(1)} %convolution_bitcast_fusion) | data formatting | bytes 1048576 | tf_op jit(solution)/shard_map/reshape | solution.py:218
  90.5 4.2 %all-to-all-start.1 = ((f32[2,16,1,8,512]{4,3,0,2,1:T(8,128)}), f32[2,16,1,8,512]{4,3,0,2,1:T(8,128)S(1)}, u32[]{:S(2)}, u32[]{:S(2)}) async-start(f32[2,16,1,8,512]{4,3,0,2,1:T(8,128)} %bitcast.39), calls=%async_computation.1 | async-start | bytes 1048576 | tf_op jit(solution)/shard_map/all_to_all | solution.py:219
  94.8 1.0 copy.224
  95.8 13.3 %all-to-all-done.1 = f32[2,16,1,8,512]{4,3,0,2,1:T(8,128)S(1)} async-done(((f32[2,16,1,8,512]{4,3,0,2,1:T(8,128)}), f32[2,16,1,8,512]{4,3,0,2,1:T(8,128)S(1)}, u32[]{:S(2)}, u32[]{:S(2)}) %all-to-all-start.1) | async-done | bytes 524320 | tf_op jit(solution)/shard_map/all_to_all | solution.py:219
  109.2 0.8 copy.292
  (68 shorter events, 21.2 us)
Async XLA Ops:
  0.6 72.8 %copy-start = (f32[2,8,4]{1,2,0:T(4,128)S(1)}, f32[2,8,4]{1,2,0:T(4,128)}, u32[]{:S(2)}) copy-start(f32[2,8,4]{1,2,0:T(4,128)} %param.16) | copy-start | bytes 772
  0.6 1.7 %copy-start.1 = (f32[2,1,1,2,256,256]{5,4,3,2,1,0:T(8,128)S(1)}, f32[2,1,1,2,256,256]{5,4,3,2,1,0:T(8,128)}, u32[]{:S(2)}) copy-start(f32[2,1,1,2,256,256]{5,4,3,2,1,0:T(8,128)} %param.11) | copy-start | bytes 3145732
  2.3 1.5 %copy-start.2 = (f32[2,1,1,2,256,256]{5,4,3,2,1,0:T(8,128)S(1)}, f32[2,1,1,2,256,256]{5,4,3,2,1,0:T(8,128)}, u32[]{:S(2)}) copy-start(f32[2,1,1,2,256,256]{5,4,3,2,1,0:T(8,128)} %param.12) | copy-start | bytes 3145732
  10.1 12.8 %collective-permute-start = (f32[2,128,128]{2,1,0:T(8,128)S(1)}, f32[2,128,128]{2,1,0:T(8,128)S(1)}, u32[]{:S(2)}, u32[]{:S(2)}) collective-permute-start(f32[2,128,128]{2,1,0:T(8,128)S(1)} %fusion.21), channel_id=1, source_target_pairs={{0,1},{2,3},{4,5},{6,7},{8,9},{10,11},{12,13},{14,15},{16,17},{18,... | collective-permute-start | bytes 393224 | tf_op jit(solution)/shard_map/ppermute | solution.py:20
  15.8 6.7 %collective-permute-start.1 = (f32[2,128,128]{2,1,0:T(8,128)S(1)}, f32[2,128,128]{2,1,0:T(8,128)S(1)}, u32[]{:S(2)}, u32[]{:S(2)}) collective-permute-start(f32[2,128,128]{2,1,0:T(8,128)S(1)} %fusion.20), channel_id=1, source_target_pairs={{0,1},{2,3},{4,5},{6,7},{8,9},{10,11},{12,13},{14,15},{16,17},{18,... | collective-permute-start | bytes 393224 | tf_op jit(solution)/shard_map/ppermute | solution.py:20
  21.3 0.7 copy-start.8
  21.3 1.1 %copy-start.5 = (f32[1,1,2,128,128]{4,3,2,1,0:T(8,128)S(1)}, f32[1,1,2,128,128]{4,3,2,1,0:T(8,128)}, u32[]{:S(2)}) copy-start(f32[1,1,2,128,128]{4,3,2,1,0:T(8,128)} %param.13) | copy-start | bytes 393220
  67.4 6.1 %copy-start.7 = (s32[8]{0:T(128)S(1)}, s32[8]{0:T(128)}, u32[]{:S(2)}) copy-start(s32[8]{0:T(128)} %param.15) | copy-start | bytes 100
  67.4 20.5 %all-to-all-start = ((f32[2,1,1,128,512]{4,0,2,1,3:T(2,128)}), f32[2,1,1,128,512]{4,0,2,1,3:T(2,128)S(1)}, u32[]{:S(2)}, u32[]{:S(2)}) async-start(f32[2,1,1,128,512]{4,0,2,1,3:T(2,128)} %copy.216), calls=%async_computation | async-start | bytes 1048576 | tf_op jit(solution)/shard_map/all_to_all | solution.py:209
  73.4 0.7 copy-start.6
  90.5 4.2 %copy-start.3 = (f32[2,256,256]{2,1,0:T(8,128)S(1)}, f32[2,256,256]{2,1,0:T(8,128)}, u32[]{:S(2)}) copy-start(f32[2,256,256]{2,1,0:T(8,128)} %fusion.1.real_ref) | copy-start | bytes 1572868
  90.5 4.2 %copy-start.4 = (f32[2,256,256]{2,1,0:T(8,128)S(1)}, f32[2,256,256]{2,1,0:T(8,128)}, u32[]{:S(2)}) copy-start(f32[2,256,256]{2,1,0:T(8,128)} %fusion.imag_ref) | copy-start | bytes 1572868
  90.5 18.7 %all-to-all-start.1 = ((f32[2,16,1,8,512]{4,3,0,2,1:T(8,128)}), f32[2,16,1,8,512]{4,3,0,2,1:T(8,128)S(1)}, u32[]{:S(2)}, u32[]{:S(2)}) async-start(f32[2,16,1,8,512]{4,3,0,2,1:T(8,128)} %bitcast.39), calls=%async_computation.1 | async-start | bytes 1048576 | tf_op jit(solution)/shard_map/all_to_all | solution.py:219

commit v3 on v2

--- a/solution.py
+++ b/solution.py
@@ -11,7 +11,7 @@
 
 
 HIGHEST = lax.Precision.HIGHEST
-FIRST_STEP_PRECISION = lax.Precision.HIGH
+FIRST_STEP_PRECISION = lax.Precision.HIGHEST
 
 
 def from_behind(shard, axis, by):
@@ -118,38 +118,25 @@
     return jnp.einsum("kjdw,dwEF->kjEF", momentum_mix, shift_table, precision=HIGHEST)
 
 
-def pick_kernel(partner_ref, real_ref, imag_ref, out_ref):
+def pick_kernel(target_ref, real_ref, imag_ref, out_ref):
     energy_count, size, _ = real_ref.shape
-    atoms = size // ORB
-    per_atom = partner_ref.shape[0] // atoms
-    width = per_atom * ORB
-    groups = 2 * energy_count
-    rows = groups * ORB
+    atoms, width = target_ref.shape
+    per_atom = width // ORB
+    sublanes = 8
     flat = ORB * ORB
-
-    spread_rows = lax.broadcasted_iota(jnp.int32, (width, flat), 0)
-    spread_cols = lax.broadcasted_iota(jnp.int32, (width, flat), 1)
-    spread = (spread_rows % ORB == spread_cols % ORB).astype(jnp.float32)
-    keep_rows = lax.broadcasted_iota(jnp.int32, (per_atom * rows, flat), 0)
-    keep_cols = lax.broadcasted_iota(jnp.int32, (per_atom * rows, flat), 1)
-    keep = keep_rows % ORB == keep_cols // ORB
-    total_rows = lax.broadcasted_iota(jnp.int32, (groups * per_atom, per_atom * rows), 0)
-    total_cols = lax.broadcasted_iota(jnp.int32, (groups * per_atom, per_atom * rows), 1)
-    total = (
-        (total_cols // rows == total_rows % per_atom)
-        & ((total_cols // ORB) % groups == total_rows // per_atom)
-    ).astype(jnp.float32)
-    lane_tile = lax.broadcasted_iota(jnp.int32, (rows, width), 1) // ORB
+    halves = ORB // sublanes
+
     pick_rows = lax.broadcasted_iota(jnp.int32, (size, width), 0)
     pick_cols = lax.broadcasted_iota(jnp.int32, (size, width), 1)
+    row_atom = pick_rows // ORB
+    same_orbital = pick_rows % ORB == pick_cols % ORB
+    grid_rows = lax.broadcasted_iota(jnp.int32, (sublanes, width), 0)
+    grid_cols = lax.broadcasted_iota(jnp.int32, (sublanes, width), 1) // ORB
+    diagonal = [(grid_cols - grid_rows) % per_atom == d for d in range(per_atom)]
 
     def one_atom(atom, carry):
-        target = jnp.zeros((size, width), jnp.int32)
-        for j in range(per_atom):
-            target = jnp.where(pick_cols // ORB == j, partner_ref[atom * per_atom + j], target)
-        pick = (
-            (pick_rows // ORB == target) & (pick_rows % ORB == pick_cols % ORB)
-        ).astype(jnp.float32)
+        target = target_ref[pl.ds(atom, 1), :]
+        pick = jnp.where((row_atom == target) & same_orbital, 1.0, 0.0)
         start = pl.multiple_of(atom * ORB, ORB)
         stripes = []
         for e in range(energy_count):
@@ -157,19 +144,18 @@
             stripes.append(imag_ref[e, pl.ds(start, ORB), :])
         stripes = jnp.concatenate(stripes, axis=0)
         chosen = jnp.dot(stripes, pick, precision=HIGHEST, preferred_element_type=jnp.float32)
-        masked = jnp.concatenate(
-            [jnp.where(lane_tile == j, chosen, 0.0) for j in range(per_atom)], axis=0
-        )
-        spread_out = jnp.dot(masked, spread, precision=HIGHEST, preferred_element_type=jnp.float32)
-        spread_out = jnp.where(keep, spread_out, 0.0)
-        summed = jnp.dot(total, spread_out, precision=HIGHEST, preferred_element_type=jnp.float32)
         out_start = pl.multiple_of(atom * per_atom, per_atom)
-        for e in range(energy_count):
-            for component in range(2):
-                g = 2 * e + component
-                out_ref[e, pl.ds(out_start, per_atom), pl.ds(component * flat, flat)] = summed[
-                    g * per_atom : (g + 1) * per_atom, :
-                ]
+        for g in range(2 * energy_count):
+            for half in range(halves):
+                row = g * ORB + half * sublanes
+                grid = chosen[row : row + sublanes, :]
+                flipped = grid
+                for d in range(1, per_atom):
+                    moved = pltpu.roll(grid, (sublanes - d) % sublanes, 0)
+                    moved = pltpu.roll(moved, d * ORB, 1)
+                    flipped = jnp.where(diagonal[d], moved, flipped)
+                lane = (g % 2) * flat + half * width
+                out_ref[g // 2, pl.ds(out_start, per_atom), pl.ds(lane, width)] = flipped
         return carry
 
     lax.fori_loop(0, atoms, one_atom, 0)
@@ -178,17 +164,18 @@
 def pick_tiles(green_pair, pair_index):
     energy_count = green_pair[0].shape[0]
     pair_count = pair_index.shape[0]
-    partner = pair_index % ATOMS
+    partner = (pair_index % ATOMS).reshape(ATOMS, -1)
+    target = jnp.repeat(partner, ORB, axis=1)
     return pl.pallas_call(
         pick_kernel,
         out_shape=jax.ShapeDtypeStruct((energy_count, pair_count, 2 * ORB * ORB), jnp.float32),
         in_specs=[
-            pl.BlockSpec(memory_space=pltpu.SMEM),
+            pl.BlockSpec(memory_space=pltpu.VMEM),
             pl.BlockSpec(memory_space=pltpu.VMEM),
             pl.BlockSpec(memory_space=pltpu.VMEM),
         ],
         out_specs=pl.BlockSpec(memory_space=pltpu.VMEM),
-    )(partner, green_pair[0], green_pair[1])
+    )(target, green_pair[0], green_pair[1])
 
 
 def body(

time: 111 us -> 108 us (0.973)
  Pallas kernels: 24.4 us -> 7.54 us
  matrix products: 34.5 us -> 43.9 us
  local copies, waits for them, and re-layouts: 6.02 us -> 9.75 us
    pallas_call x1, Pallas kernels: 24.4 us -> 7.54 us  [pick_tiles(): pl.pallas_call(pick_kernel, out_shape=jax.ShapeDtypeStruct((energy_count,...]
    dot_general x13, matrix products: 8.35 us -> 11.5 us  [complex_product(): jnp.matmul(first_real, second_imag, precision=precision)]
    dot_general x13, matrix products: 7.96 us -> 10.4 us  [complex_product(): jnp.matmul(first_imag, second_real, precision=precision)]
    dot_general x13, matrix products: 7.96 us -> 10.3 us  [complex_product(): jnp.matmul(first_imag, second_imag, precision=precision)]
    reshape x0 -> x1, local copies, waits for them, and re-layouts: none -> 1.51 us  [pick_tiles(): target = jnp.repeat(partner, ORB, axis=1)]
    dot_general x13, matrix products: 8.33 us -> 9.84 us  [complex_product(): jnp.matmul(first_real, second_real, precision=precision)]
    unnamed x19 -> x24, local copies, waits for them, and re-layouts: 1.76 us -> 3.18 us
  transfers between devices with their start and end apart: 4 -> 4, of which waited for: 2 -> 2; matrix products, arithmetic and copies ran while one was open for 7% -> 15% of each run, Pallas kernels for 0% -> 0%
where the time goes in v3:
time: 108 us; the launch traced here: 107 us
  matrix products  43.9 us (41%)
  waiting for transfers between devices  26.5 us (25%)
  starting transfers between devices  17.1 us (16%)
  local copies, waits for them, and re-layouts  9.75 us (9%)
  Pallas kernels  7.54 us (7%)
  between operations  1.18 us (1%)
    all_to_all x1, waiting for transfers between devices, body(): lax.all_to_all(summed, ('energy', 'momentum'), split_axis=1, concat_axis=...  13.3 us
    all_to_all x1, waiting for transfers between devices, body(): lax.all_to_all(picked, ('energy', 'momentum'), split_axis=3, concat_axis=...  13.2 us
    dot_general x13, matrix products, complex_product(): jnp.matmul(first_real, second_imag, precision=precision)  11.5 us
    dot_general x13, matrix products, complex_product(): jnp.matmul(first_imag, second_real, precision=precision)  10.4 us
    dot_general x13, matrix products, complex_product(): jnp.matmul(first_imag, second_imag, precision=precision)  10.3 us
    dot_general x13, matrix products, complex_product(): jnp.matmul(first_real, second_real, precision=precision)  9.84 us
    pallas_call x1, Pallas kernels, pick_tiles(): pl.pallas_call(pick_kernel, out_shape=jax.ShapeDtypeStruct((energy_count,...  7.54 us
    ppermute x2, starting transfers between devices, from_behind(): return lax.ppermute(shard, axis, pairs)  6.8 us
  transfers between devices with their start and end apart: 4, of which 2 were waited for; matrix products, arithmetic and copies ran while one was open for 15% of the time, Pallas kernels for 0%

profile of v3, /device:TPU:0, one launch (start us, length us, event | category | flops | bytes accessed | tf_op | source)
XLA Modules:
  0.0 106.9 jit_solution(17190174522078310708)
XLA Ops:
  0.7 1.9 %fusion.46 = f32[2,256,256]{2,1,0:T(8,128)S(1)} fusion(f32[2,1,1,2,256,256]{5,4,3,2,1,0:T(8,128)} %param.11, f32[2,1,1,2,256,256]{5,4,3,2,1,0:T(8,128)} %param.12), kind=kOutput, calls=%fused_computation.75 | convolution fusion | flops 402653184 | bytes 1572864 | tf_op jit(solution)/shard_map/dot_general | solution.py:26
  2.6 1.8 %fusion.44 = f32[2,256,256]{2,1,0:T(8,128)S(1)} fusion(f32[2,1,1,2,256,256]{5,4,3,2,1,0:T(8,128)S(1)} %copy-done.1, f32[2,1,1,2,256,256]{5,4,3,2,1,0:T(8,128)} %param.12), kind=kOutput, calls=%fused_computation.73 | convolution fusion | flops 402653184 | bytes 1572864 | tf_op jit(solution)/shard_map/dot_general | solution.py:29
  13.1 4.9 %collective-permute-start = (f32[2,128,128]{2,1,0:T(8,128)}, f32[2,128,128]{2,1,0:T(8,128)S(1)}, u32[]{:S(2)}, u32[]{:S(2)}) collective-permute-start(f32[2,128,128]{2,1,0:T(8,128)} %fusion.21), channel_id=1, source_target_pairs={{0,1},{2,3},{4,5},{6,7},{8,9},{10,11},{12,13},{14,15},{16,17},{18,... | collective-permute-start | bytes 393224 | tf_op jit(solution)/shard_map/ppermute | solution.py:20
  18.4 1.1 fusion.20
  19.4 1.9 %collective-permute-start.1 = (f32[2,128,128]{2,1,0:T(8,128)}, f32[2,128,128]{2,1,0:T(8,128)}, u32[]{:S(2)}, u32[]{:S(2)}) collective-permute-start(f32[2,128,128]{2,1,0:T(8,128)} %fusion.20), channel_id=1, source_target_pairs={{0,1},{2,3},{4,5},{6,7},{8,9},{10,11},{12,13},{14,15},{16,17},{18,... | collective-permute-start | bytes 393224 | tf_op jit(solution)/shard_map/ppermute | solution.py:20
  21.5 1.9 %fusion.38 = f32[2,256,256]{2,1,0:T(8,128)} fusion(f32[2,256,256]{2,1,0:T(8,128)S(1)} %fusion.9, f32[2,1,1,2,256,256]{5,4,3,2,1,0:T(8,128)S(1)} %copy-done.1), kind=kOutput, calls=%fused_computation.67 | convolution fusion | flops 402653184 | bytes 1572864 | tf_op jit(solution)/shard_map/dot_general | solution.py:26
  23.3 1.9 %fusion.32 = f32[2,256,256]{2,1,0:T(8,128)} fusion(f32[2,256,256]{2,1,0:T(8,128)S(1)} %fusion.7, f32[2,1,1,2,256,256]{5,4,3,2,1,0:T(8,128)S(1)} %copy-done.1), kind=kOutput, calls=%fused_computation.61 | convolution fusion | flops 402653184 | bytes 1572864 | tf_op jit(solution)/shard_map/dot_general | solution.py:29
  25.8 1.3 %fusion.34 = f32[2,256,128]{2,1,0:T(8,128)} fusion(f32[2,1,1,2,256,256]{5,4,3,2,1,0:T(8,128)S(1)} %copy-done.1, f32[2,256,256]{2,1,0:T(8,128)S(1)} %get-tuple-element.34), kind=kOutput, calls=%fused_computation.63 | convolution fusion | flops 201326592 | bytes 1048576 | tf_op jit(solution)/shard_map/dot_general | solution.py:29
  29.9 1.5 %reshape.113.target_ref = s32[16,128]{1,0:T(8,128)} reshape(s32[16,8,16]{2,1,0:T(8,128)} %broadcast_in_dim.7) | data formatting | bytes 16384 | tf_op jit(solution)/shard_map/reshape | solution.py:168
  31.4 1.6 %convolution_add_fusion.7 = f32[2,256,128]{2,1,0:T(8,128)S(1)} fusion(f32[2,256,128]{2,1,0:T(8,128)} %fusion.34, f32[2,1,1,2,256,256]{5,4,3,2,1,0:T(8,128)S(1)} %copy-done.1, f32[2,256,256]{2,1,0:T(8,128)S(1)} %get-tuple-element.35), kind=kOutput, calls=%fused_computation.35 | convolution fusion | flops 201392128 | bytes 1310720 | tf_op jit(solution)/shard_map/dot_general | solution.py:29
  33.0 1.3 %fusion.109 = f32[2,128,128]{2,1,0:T(8,128)S(1)} fusion(f32[2,128,128]{2,1,0:T(8,128)} %collective-permute-done.1, f32[1,1,2,128,128]{4,3,2,1,0:T(8,128)S(1)} %copy-done.7), kind=kOutput, calls=%fused_computation.143 | convolution fusion | flops 50348032 | bytes 327680 | tf_op jit(solution)/shard_map/dot_general | solution.py:26
  35.9 1.3 %fusion.22 = f32[2,128,128]{1,2,0:T(8,128)S(1)} fusion(f32[2,128,128]{2,1,0:T(8,128)S(1)} %fusion.107, f32[2,128,128]{2,1,0:T(8,128)} %collective-permute-done.1, f32[1,1,2,128,128]{4,3,2,1,0:T(8,128)S(1)} %copy-done.7), kind=kOutput, calls=%fused_computation.48 | convolution fusion | flops 50364416 | bytes 458752 | tf_op jit(solution)/shard_map/dot_general | solution.py:29
  45.6 1.1 fusion.5
  49.1 1.1 fusion.3
  51.4 1.5 %fusion.1.real_ref = f32[2,256,256]{2,1,0:T(8,128)} fusion(f32[2,256,256]{2,1,0:T(8,128)S(1)} %fusion.131, f32[2,256,256]{2,1,0:T(8,128)S(1)} %fusion.11, f32[2,256,256]{1,2,0:T(8,128)S(1)} %fusion.16, f32[2,256,256]{2,1,0:T(8,128)S(1)} %fusion.13), kind=kOutput, calls=%fused_computation.4 | convolution fusion | flops 403046400 | bytes 2621440 | tf_op jit(solution)/shard_map/dot_general | solution.py:26
  53.0 1.5 %fusion.imag_ref = f32[2,256,256]{2,1,0:T(8,128)} fusion(f32[2,256,256]{2,1,0:T(8,128)S(1)} %fusion.133, f32[2,256,256]{2,1,0:T(8,128)S(1)} %fusion.11, f32[2,256,256]{1,2,0:T(8,128)S(1)} %fusion.19), kind=kOutput, calls=%fused_computation.2 | convolution fusion | flops 403046400 | bytes 2097152 | tf_op jit(solution)/shard_map/dot_general | solution.py:29
  54.5 7.5 %shard_map.86 = f32[2,128,512]{2,1,0:T(8,128)} custom-call(s32[16,128]{1,0:T(8,128)} %reshape.113.target_ref, f32[2,256,256]{2,1,0:T(8,128)} %fusion.1.real_ref, f32[2,256,256]{2,1,0:T(8,128)} %fusion.imag_ref), custom_call_target="tpu_custom_call" | custom-call | tf_op jit(solution)/shard_map/pallas_call | solution.py:169
  62.0 2.2 %copy.216 = f32[2,1,1,128,512]{4,0,2,1,3:T(2,128)} copy(f32[2,1,1,128,512]{4,3,0,2,1:T(8,128)} %bitcast.210) | data formatting | bytes 1048576 | tf_op jit(solution)/shard_map/broadcast_in_dim | solution.py:190
  64.3 6.0 %all-to-all-start = ((f32[2,1,1,128,512]{4,0,2,1,3:T(2,128)}), f32[2,1,1,128,512]{4,0,2,1,3:T(2,128)S(1)}, u32[]{:S(2)}, u32[]{:S(2)}) async-start(f32[2,1,1,128,512]{4,0,2,1,3:T(2,128)} %copy.216), calls=%async_computation | async-start | bytes 1048576 | tf_op jit(solution)/shard_map/all_to_all | solution.py:196
  71.6 13.2 %all-to-all-done = f32[2,1,1,128,512]{4,0,2,1,3:T(2,128)S(1)} async-done(((f32[2,1,1,128,512]{4,0,2,1,3:T(2,128)}), f32[2,1,1,128,512]{4,0,2,1,3:T(2,128)S(1)}, u32[]{:S(2)}, u32[]{:S(2)}) %all-to-all-start) | async-done | bytes 524320 | tf_op jit(solution)/shard_map/all_to_all | solution.py:196
  84.8 1.5 %convolution_bitcast_fusion = f32[2,4,4,8,512]{4,1,0,2,3:T(4,128)S(1)} fusion(f32[2,4,4,8,512,1,1]{4,0,3,2,1,6,5:T(2,128)S(1)} %bitcast.211, f32[4,4,4,2,4,2]{1,5,4,3,2,0:T(2,128)S(1)} %bitcast.213), kind=kOutput, calls=%fused_computation | convolution fusion | flops 50331648 | bytes 1052672 | tf_op jit(solution)/shard_map/kjabcd,dcjpx->bakpx/dot_general | solution.py:204
  86.3 1.1 %copy.280 = f32[2,4,4,8,512]{4,3,0,2,1:T(8,128)} copy(f32[2,4,4,8,512]{4,1,0,2,3:T(4,128)S(1)} %convolution_bitcast_fusion) | data formatting | bytes 1048576 | tf_op jit(solution)/shard_map/reshape | solution.py:205
  87.4 4.2 %all-to-all-start.1 = ((f32[2,16,1,8,512]{4,3,0,2,1:T(8,128)}), f32[2,16,1,8,512]{4,3,0,2,1:T(8,128)S(1)}, u32[]{:S(2)}, u32[]{:S(2)}) async-start(f32[2,16,1,8,512]{4,3,0,2,1:T(8,128)} %bitcast.38), calls=%async_computation.1 | async-start | bytes 1048576 | tf_op jit(solution)/shard_map/all_to_all | solution.py:206
  92.8 13.3 %all-to-all-done.1 = f32[2,16,1,8,512]{4,3,0,2,1:T(8,128)S(1)} async-done(((f32[2,16,1,8,512]{4,3,0,2,1:T(8,128)}), f32[2,16,1,8,512]{4,3,0,2,1:T(8,128)S(1)}, u32[]{:S(2)}, u32[]{:S(2)}) %all-to-all-start.1) | async-done | bytes 524320 | tf_op jit(solution)/shard_map/all_to_all | solution.py:206
  (77 shorter events, 29.0 us)
Async XLA Ops:
  0.6 69.7 %copy-start = (f32[2,8,4]{1,2,0:T(4,128)S(1)}, f32[2,8,4]{1,2,0:T(4,128)}, u32[]{:S(2)}) copy-start(f32[2,8,4]{1,2,0:T(4,128)} %param.16) | copy-start | bytes 772
  0.6 2.0 %copy-start.1 = (f32[2,1,1,2,256,256]{5,4,3,2,1,0:T(8,128)S(1)}, f32[2,1,1,2,256,256]{5,4,3,2,1,0:T(8,128)}, u32[]{:S(2)}) copy-start(f32[2,1,1,2,256,256]{5,4,3,2,1,0:T(8,128)} %param.11) | copy-start | bytes 3145732
  2.6 1.8 %copy-start.2 = (f32[2,1,1,2,256,256]{5,4,3,2,1,0:T(8,128)S(1)}, f32[2,1,1,2,256,256]{5,4,3,2,1,0:T(8,128)}, u32[]{:S(2)}) copy-start(f32[2,1,1,2,256,256]{5,4,3,2,1,0:T(8,128)} %param.12) | copy-start | bytes 3145732
  13.1 21.2 %collective-permute-start = (f32[2,128,128]{2,1,0:T(8,128)}, f32[2,128,128]{2,1,0:T(8,128)S(1)}, u32[]{:S(2)}, u32[]{:S(2)}) collective-permute-start(f32[2,128,128]{2,1,0:T(8,128)} %fusion.21), channel_id=1, source_target_pairs={{0,1},{2,3},{4,5},{6,7},{8,9},{10,11},{12,13},{14,15},{16,17},{18,... | collective-permute-start | bytes 393224 | tf_op jit(solution)/shard_map/ppermute | solution.py:20
  19.4 13.6 %collective-permute-start.1 = (f32[2,128,128]{2,1,0:T(8,128)}, f32[2,128,128]{2,1,0:T(8,128)}, u32[]{:S(2)}, u32[]{:S(2)}) collective-permute-start(f32[2,128,128]{2,1,0:T(8,128)} %fusion.20), channel_id=1, source_target_pairs={{0,1},{2,3},{4,5},{6,7},{8,9},{10,11},{12,13},{14,15},{16,17},{18,... | collective-permute-start | bytes 393224 | tf_op jit(solution)/shard_map/ppermute | solution.py:20
  27.7 0.7 copy-start.10
  31.4 1.6 %copy-start.7 = (f32[1,1,2,128,128]{4,3,2,1,0:T(8,128)S(1)}, f32[1,1,2,128,128]{4,3,2,1,0:T(8,128)}, u32[]{:S(2)}) copy-start(f32[1,1,2,128,128]{4,3,2,1,0:T(8,128)} %param.13) | copy-start | bytes 393220
  44.6 1.0 copy-start.6
  48.0 1.0 copy-start.5
  64.3 6.1 %copy-start.9 = (s32[8]{0:T(128)S(1)}, s32[8]{0:T(128)}, u32[]{:S(2)}) copy-start(s32[8]{0:T(128)} %param.15) | copy-start | bytes 100
  64.3 20.5 %all-to-all-start = ((f32[2,1,1,128,512]{4,0,2,1,3:T(2,128)}), f32[2,1,1,128,512]{4,0,2,1,3:T(2,128)S(1)}, u32[]{:S(2)}, u32[]{:S(2)}) async-start(f32[2,1,1,128,512]{4,0,2,1,3:T(2,128)} %copy.216), calls=%async_computation | async-start | bytes 1048576 | tf_op jit(solution)/shard_map/all_to_all | solution.py:196
  70.4 0.7 copy-start.8
  87.4 4.2 %copy-start.3 = (f32[2,256,256]{2,1,0:T(8,128)S(1)}, f32[2,256,256]{2,1,0:T(8,128)}, u32[]{:S(2)}) copy-start(f32[2,256,256]{2,1,0:T(8,128)} %fusion.1.real_ref) | copy-start | bytes 1572868
  87.4 4.3 %copy-start.4 = (f32[2,256,256]{2,1,0:T(8,128)S(1)}, f32[2,256,256]{2,1,0:T(8,128)}, u32[]{:S(2)}) copy-start(f32[2,256,256]{2,1,0:T(8,128)} %fusion.imag_ref) | copy-start | bytes 1572868
  87.4 18.7 %all-to-all-start.1 = ((f32[2,16,1,8,512]{4,3,0,2,1:T(8,128)}), f32[2,16,1,8,512]{4,3,0,2,1:T(8,128)S(1)}, u32[]{:S(2)}, u32[]{:S(2)}) async-start(f32[2,16,1,8,512]{4,3,0,2,1:T(8,128)} %bitcast.38), calls=%async_computation.1 | async-start | bytes 1048576 | tf_op jit(solution)/shard_map/all_to_all | solution.py:206

commit v4 on v3

--- a/solution.py
+++ b/solution.py
@@ -118,10 +118,11 @@
     return jnp.einsum("kjdw,dwEF->kjEF", momentum_mix, shift_table, precision=HIGHEST)
 
 
-def pick_kernel(target_ref, real_ref, imag_ref, out_ref):
+def pick_kernel(partner_ref, real_ref, imag_ref, out_ref):
     energy_count, size, _ = real_ref.shape
-    atoms, width = target_ref.shape
-    per_atom = width // ORB
+    atoms = size // ORB
+    per_atom = partner_ref.shape[0] // atoms
+    width = per_atom * ORB
     sublanes = 8
     flat = ORB * ORB
     halves = ORB // sublanes
@@ -133,9 +134,12 @@
     grid_rows = lax.broadcasted_iota(jnp.int32, (sublanes, width), 0)
     grid_cols = lax.broadcasted_iota(jnp.int32, (sublanes, width), 1) // ORB
     diagonal = [(grid_cols - grid_rows) % per_atom == d for d in range(per_atom)]
+    lane_tile = lax.broadcasted_iota(jnp.int32, (1, width), 1) // ORB
 
     def one_atom(atom, carry):
-        target = target_ref[pl.ds(atom, 1), :]
+        target = jnp.zeros((1, width), jnp.int32)
+        for j in range(per_atom):
+            target = jnp.where(lane_tile == j, partner_ref[atom * per_atom + j], target)
         pick = jnp.where((row_atom == target) & same_orbital, 1.0, 0.0)
         start = pl.multiple_of(atom * ORB, ORB)
         stripes = []
@@ -164,18 +168,17 @@
 def pick_tiles(green_pair, pair_index):
     energy_count = green_pair[0].shape[0]
     pair_count = pair_index.shape[0]
-    partner = (pair_index % ATOMS).reshape(ATOMS, -1)
-    target = jnp.repeat(partner, ORB, axis=1)
+    partner = pair_index % ATOMS
     return pl.pallas_call(
         pick_kernel,
         out_shape=jax.ShapeDtypeStruct((energy_count, pair_count, 2 * ORB * ORB), jnp.float32),
         in_specs=[
-            pl.BlockSpec(memory_space=pltpu.VMEM),
+            pl.BlockSpec(memory_space=pltpu.SMEM),
             pl.BlockSpec(memory_space=pltpu.VMEM),
             pl.BlockSpec(memory_space=pltpu.VMEM),
         ],
         out_specs=pl.BlockSpec(memory_space=pltpu.VMEM),
-    )(target, green_pair[0], green_pair[1])
+    )(partner, green_pair[0], green_pair[1])
 
 
 def body(

time: 108 us -> 96.3 us (0.89)
  matrix products: 43.9 us -> 37.1 us
  local copies, waits for them, and re-layouts: 9.75 us -> 6.02 us
    dot_general x13, matrix products: 11.5 us -> 9.04 us  [complex_product(): jnp.matmul(first_real, second_imag, precision=precision)]
    dot_general x13, matrix products: 10.4 us -> 8.59 us  [complex_product(): jnp.matmul(first_imag, second_real, precision=precision)]
    dot_general x13, matrix products: 10.3 us -> 8.59 us  [complex_product(): jnp.matmul(first_imag, second_imag, precision=precision)]
    reshape x1 -> x0, local copies, waits for them, and re-layouts: 1.51 us -> none  [pick_tiles(): target = jnp.repeat(partner, ORB, axis=1)]
    unnamed x24 -> x19, local copies, waits for them, and re-layouts: 3.18 us -> 1.76 us
  transfers between devices with their start and end apart: 4 -> 4, of which waited for: 2 -> 2; matrix products, arithmetic and copies ran while one was open for 15% -> 8% of each run, Pallas kernels for 0% -> 0%
where the time goes in v4:
time: 96.3 us; the launch traced here: 95.7 us
  matrix products  37.1 us (39%)
  waiting for transfers between devices  26.6 us (28%)
  starting transfers between devices  16.6 us (17%)
  Pallas kernels  7.57 us (8%)
  local copies, waits for them, and re-layouts  6.02 us (6%)
  between operations  1.2 us (1%)
    all_to_all x1, waiting for transfers between devices, body(): lax.all_to_all(summed, ('energy', 'momentum'), split_axis=1, concat_axis=...  13.3 us
    all_to_all x1, waiting for transfers between devices, body(): lax.all_to_all(picked, ('energy', 'momentum'), split_axis=3, concat_axis=...  13.2 us
    dot_general x13, matrix products, complex_product(): jnp.matmul(first_real, second_imag, precision=precision)  9.04 us
    dot_general x13, matrix products, complex_product(): jnp.matmul(first_real, second_real, precision=precision)  8.96 us
    dot_general x13, matrix products, complex_product(): jnp.matmul(first_imag, second_imag, precision=precision)  8.59 us
    dot_general x13, matrix products, complex_product(): jnp.matmul(first_imag, second_real, precision=precision)  8.59 us
    pallas_call x1, Pallas kernels, pick_tiles(): pl.pallas_call(pick_kernel, out_shape=jax.ShapeDtypeStruct((energy_count,...  7.57 us
    ppermute x2, starting transfers between devices, from_behind(): return lax.ppermute(shard, axis, pairs)  6.36 us
  transfers between devices with their start and end apart: 4, of which 2 were waited for; matrix products, arithmetic and copies ran while one was open for 8% of the time, Pallas kernels for 0%

profile of v4, /device:TPU:0, one launch (start us, length us, event | category | flops | bytes accessed | tf_op | source)
XLA Modules:
  0.0 95.7 jit_solution(11442263387435999131)
XLA Ops:
  0.7 1.9 %fusion.46 = f32[2,256,256]{2,1,0:T(8,128)S(1)} fusion(f32[2,1,1,2,256,256]{5,4,3,2,1,0:T(8,128)} %param.11, f32[2,1,1,2,256,256]{5,4,3,2,1,0:T(8,128)} %param.12), kind=kOutput, calls=%fused_computation.75 | convolution fusion | flops 402653184 | bytes 1572864 | tf_op jit(solution)/shard_map/dot_general | solution.py:26
  2.6 1.8 %fusion.44 = f32[2,256,256]{2,1,0:T(8,128)S(1)} fusion(f32[2,1,1,2,256,256]{5,4,3,2,1,0:T(8,128)S(1)} %copy-done.1, f32[2,1,1,2,256,256]{5,4,3,2,1,0:T(8,128)} %param.12), kind=kOutput, calls=%fused_computation.73 | convolution fusion | flops 402653184 | bytes 1572864 | tf_op jit(solution)/shard_map/dot_general | solution.py:29
  9.2 0.7 fusion.40
  9.9 0.7 convolution_subtract_fusion.9
  11.1 0.7 convolution_add_fusion.9
  12.2 4.9 %collective-permute-start = (f32[2,128,128]{2,1,0:T(8,128)S(1)}, f32[2,128,128]{2,1,0:T(8,128)S(1)}, u32[]{:S(2)}, u32[]{:S(2)}) collective-permute-start(f32[2,128,128]{2,1,0:T(8,128)S(1)} %fusion.21), channel_id=1, source_target_pairs={{0,1},{2,3},{4,5},{6,7},{8,9},{10,11},{12,13},{14,15},{16,17},{18,... | collective-permute-start | bytes 393224 | tf_op jit(solution)/shard_map/ppermute | solution.py:20
  17.9 1.5 %collective-permute-start.1 = (f32[2,128,128]{2,1,0:T(8,128)S(1)}, f32[2,128,128]{2,1,0:T(8,128)S(1)}, u32[]{:S(2)}, u32[]{:S(2)}) collective-permute-start(f32[2,128,128]{2,1,0:T(8,128)S(1)} %fusion.20), channel_id=1, source_target_pairs={{0,1},{2,3},{4,5},{6,7},{8,9},{10,11},{12,13},{14,15},{16,17},{18,... | collective-permute-start | bytes 393224 | tf_op jit(solution)/shard_map/ppermute | solution.py:20
  19.5 1.0 %fusion.38 = f32[2,256,256]{2,1,0:T(8,128)S(1)} fusion(f32[2,256,256]{2,1,0:T(8,128)S(1)} %fusion.9, f32[2,1,1,2,256,256]{5,4,3,2,1,0:T(8,128)S(1)} %copy-done.1), kind=kOutput, calls=%fused_computation.67 | convolution fusion | flops 402653184 | bytes 1572864 | tf_op jit(solution)/shard_map/dot_general | solution.py:26
  20.5 1.0 %fusion.32 = f32[2,256,256]{2,1,0:T(8,128)S(1)} fusion(f32[2,256,256]{2,1,0:T(8,128)S(1)} %fusion.7, f32[2,1,1,2,256,256]{5,4,3,2,1,0:T(8,128)S(1)} %copy-done.1), kind=kOutput, calls=%fused_computation.61 | convolution fusion | flops 402653184 | bytes 1572864 | tf_op jit(solution)/shard_map/dot_general | solution.py:29
  33.5 0.8 fusion.65
  35.0 1.0 %fusion.5 = f32[2,256,256]{1,2,0:T(8,128)S(1)} fusion(f32[2,256,256]{1,2,0:T(8,128)S(1)} %convolution_subtract_fusion.4, f32[2,256,256]{2,1,0:T(8,128)S(1)} %fusion.38, f32[2,256,256]{2,1,0:T(8,128)S(1)} %fusion.7, f32[2,1,1,2,256,256]{5,4,3,2,1,0:T(8,128)S(1)} %copy-done.1), kind=kOutput, calls=%fused_computation.10 | convolution fusion | flops 402915328 | bytes 2621440 | tf_op jit(solution)/shard_map/dot_general | solution.py:26
  37.9 1.0 %fusion.3 = f32[2,256,256]{1,2,0:T(8,128)S(1)} fusion(f32[2,256,256]{1,2,0:T(8,128)S(1)} %convolution_add_fusion.4, f32[2,256,256]{2,1,0:T(8,128)S(1)} %fusion.32, f32[2,256,256]{2,1,0:T(8,128)S(1)} %fusion.9, f32[2,1,1,2,256,256]{5,4,3,2,1,0:T(8,128)S(1)} %copy-done.1), kind=kOutput, calls=%fused_computation.7 | convolution fusion | flops 402915328 | bytes 2621440 | tf_op jit(solution)/shard_map/dot_general | solution.py:29
  40.3 1.5 %fusion.1.real_ref = f32[2,256,256]{2,1,0:T(8,128)} fusion(f32[2,256,256]{2,1,0:T(8,128)S(1)} %fusion.131, f32[2,256,256]{2,1,0:T(8,128)S(1)} %fusion.11, f32[2,256,256]{1,2,0:T(8,128)S(1)} %fusion.16, f32[2,256,256]{2,1,0:T(8,128)S(1)} %fusion.13), kind=kOutput, calls=%fused_computation.4 | convolution fusion | flops 403046400 | bytes 2621440 | tf_op jit(solution)/shard_map/dot_general | solution.py:26
  41.8 1.5 %fusion.imag_ref = f32[2,256,256]{2,1,0:T(8,128)} fusion(f32[2,256,256]{2,1,0:T(8,128)S(1)} %fusion.133, f32[2,256,256]{2,1,0:T(8,128)S(1)} %fusion.11, f32[2,256,256]{1,2,0:T(8,128)S(1)} %fusion.19), kind=kOutput, calls=%fused_computation.2 | convolution fusion | flops 403046400 | bytes 2097152 | tf_op jit(solution)/shard_map/dot_general | solution.py:29
  43.3 7.6 %shard_map.86 = f32[2,128,512]{2,1,0:T(8,128)} custom-call(s32[128]{0:T(128)} %and_select_fusion.partner_ref, f32[2,256,256]{2,1,0:T(8,128)} %fusion.1.real_ref, f32[2,256,256]{2,1,0:T(8,128)} %fusion.imag_ref), custom_call_target="tpu_custom_call" | custom-call | tf_op jit(solution)/shard_map/pallas_call | solution.py:172
  50.8 2.2 %copy.216 = f32[2,1,1,128,512]{4,0,2,1,3:T(2,128)} copy(f32[2,1,1,128,512]{4,3,0,2,1:T(8,128)} %bitcast.212) | data formatting | bytes 1048576 | tf_op jit(solution)/shard_map/broadcast_in_dim | solution.py:193
  53.1 6.0 %all-to-all-start = ((f32[2,1,1,128,512]{4,0,2,1,3:T(2,128)}), f32[2,1,1,128,512]{4,0,2,1,3:T(2,128)S(1)}, u32[]{:S(2)}, u32[]{:S(2)}) async-start(f32[2,1,1,128,512]{4,0,2,1,3:T(2,128)} %copy.216), calls=%async_computation | async-start | bytes 1048576 | tf_op jit(solution)/shard_map/all_to_all | solution.py:199
  60.4 13.2 %all-to-all-done = f32[2,1,1,128,512]{4,0,2,1,3:T(2,128)S(1)} async-done(((f32[2,1,1,128,512]{4,0,2,1,3:T(2,128)}), f32[2,1,1,128,512]{4,0,2,1,3:T(2,128)S(1)}, u32[]{:S(2)}, u32[]{:S(2)}) %all-to-all-start) | async-done | bytes 524320 | tf_op jit(solution)/shard_map/all_to_all | solution.py:199
  73.6 1.5 %convolution_bitcast_fusion = f32[2,4,4,8,512]{4,1,0,2,3:T(4,128)S(1)} fusion(f32[2,4,4,8,512,1,1]{4,0,3,2,1,6,5:T(2,128)S(1)} %bitcast.213, f32[4,4,4,2,4,2]{1,5,4,3,2,0:T(2,128)S(1)} %bitcast.215), kind=kOutput, calls=%fused_computation | convolution fusion | flops 50331648 | bytes 1052672 | tf_op jit(solution)/shard_map/kjabcd,dcjpx->bakpx/dot_general | solution.py:207
  75.1 1.1 %copy.280 = f32[2,4,4,8,512]{4,3,0,2,1:T(8,128)} copy(f32[2,4,4,8,512]{4,1,0,2,3:T(4,128)S(1)} %convolution_bitcast_fusion) | data formatting | bytes 1048576 | tf_op jit(solution)/shard_map/reshape | solution.py:208
  76.2 4.2 %all-to-all-start.1 = ((f32[2,16,1,8,512]{4,3,0,2,1:T(8,128)}), f32[2,16,1,8,512]{4,3,0,2,1:T(8,128)S(1)}, u32[]{:S(2)}, u32[]{:S(2)}) async-start(f32[2,16,1,8,512]{4,3,0,2,1:T(8,128)} %bitcast.39), calls=%async_computation.1 | async-start | bytes 1048576 | tf_op jit(solution)/shard_map/all_to_all | solution.py:209
  80.5 1.0 %copy.224 = f32[2,1,1,2,256,256]{5,4,3,2,1,0:T(8,128)} copy(f32[2,1,1,2,256,256]{5,4,0,3,2,1:T(8,128)S(1)} %maximum_bitcast_fusion) | data formatting | bytes 2097152
  81.6 13.3 %all-to-all-done.1 = f32[2,16,1,8,512]{4,3,0,2,1:T(8,128)S(1)} async-done(((f32[2,16,1,8,512]{4,3,0,2,1:T(8,128)}), f32[2,16,1,8,512]{4,3,0,2,1:T(8,128)S(1)}, u32[]{:S(2)}, u32[]{:S(2)}) %all-to-all-start.1) | async-done | bytes 524320 | tf_op jit(solution)/shard_map/all_to_all | solution.py:209
  94.9 0.8 copy.292
  (68 shorter events, 23.2 us)
Async XLA Ops:
  0.6 58.6 %copy-start = (f32[2,8,4]{1,2,0:T(4,128)S(1)}, f32[2,8,4]{1,2,0:T(4,128)}, u32[]{:S(2)}) copy-start(f32[2,8,4]{1,2,0:T(4,128)} %param.16) | copy-start | bytes 772
  0.6 2.0 %copy-start.1 = (f32[2,1,1,2,256,256]{5,4,3,2,1,0:T(8,128)S(1)}, f32[2,1,1,2,256,256]{5,4,3,2,1,0:T(8,128)}, u32[]{:S(2)}) copy-start(f32[2,1,1,2,256,256]{5,4,3,2,1,0:T(8,128)} %param.11) | copy-start | bytes 3145732
  2.6 1.8 %copy-start.2 = (f32[2,1,1,2,256,256]{5,4,3,2,1,0:T(8,128)S(1)}, f32[2,1,1,2,256,256]{5,4,3,2,1,0:T(8,128)}, u32[]{:S(2)}) copy-start(f32[2,1,1,2,256,256]{5,4,3,2,1,0:T(8,128)} %param.12) | copy-start | bytes 3145732
  12.2 12.8 %collective-permute-start = (f32[2,128,128]{2,1,0:T(8,128)S(1)}, f32[2,128,128]{2,1,0:T(8,128)S(1)}, u32[]{:S(2)}, u32[]{:S(2)}) collective-permute-start(f32[2,128,128]{2,1,0:T(8,128)S(1)} %fusion.21), channel_id=1, source_target_pairs={{0,1},{2,3},{4,5},{6,7},{8,9},{10,11},{12,13},{14,15},{16,17},{18,... | collective-permute-start | bytes 393224 | tf_op jit(solution)/shard_map/ppermute | solution.py:20
  17.9 6.7 %collective-permute-start.1 = (f32[2,128,128]{2,1,0:T(8,128)S(1)}, f32[2,128,128]{2,1,0:T(8,128)S(1)}, u32[]{:S(2)}, u32[]{:S(2)}) collective-permute-start(f32[2,128,128]{2,1,0:T(8,128)S(1)} %fusion.20), channel_id=1, source_target_pairs={{0,1},{2,3},{4,5},{6,7},{8,9},{10,11},{12,13},{14,15},{16,17},{18,... | collective-permute-start | bytes 393224 | tf_op jit(solution)/shard_map/ppermute | solution.py:20
  23.4 0.7 copy-start.8
  23.4 1.1 %copy-start.5 = (f32[1,1,2,128,128]{4,3,2,1,0:T(8,128)S(1)}, f32[1,1,2,128,128]{4,3,2,1,0:T(8,128)}, u32[]{:S(2)}) copy-start(f32[1,1,2,128,128]{4,3,2,1,0:T(8,128)} %param.13) | copy-start | bytes 393220
  53.1 6.1 %copy-start.7 = (s32[8]{0:T(128)S(1)}, s32[8]{0:T(128)}, u32[]{:S(2)}) copy-start(s32[8]{0:T(128)} %param.15) | copy-start | bytes 100
  53.1 20.5 %all-to-all-start = ((f32[2,1,1,128,512]{4,0,2,1,3:T(2,128)}), f32[2,1,1,128,512]{4,0,2,1,3:T(2,128)S(1)}, u32[]{:S(2)}, u32[]{:S(2)}) async-start(f32[2,1,1,128,512]{4,0,2,1,3:T(2,128)} %copy.216), calls=%async_computation | async-start | bytes 1048576 | tf_op jit(solution)/shard_map/all_to_all | solution.py:199
  59.2 0.7 copy-start.6
  76.2 4.2 %copy-start.3 = (f32[2,256,256]{2,1,0:T(8,128)S(1)}, f32[2,256,256]{2,1,0:T(8,128)}, u32[]{:S(2)}) copy-start(f32[2,256,256]{2,1,0:T(8,128)} %fusion.1.real_ref) | copy-start | bytes 1572868
  76.2 4.3 %copy-start.4 = (f32[2,256,256]{2,1,0:T(8,128)S(1)}, f32[2,256,256]{2,1,0:T(8,128)}, u32[]{:S(2)}) copy-start(f32[2,256,256]{2,1,0:T(8,128)} %fusion.imag_ref) | copy-start | bytes 1572868
  76.2 18.7 %all-to-all-start.1 = ((f32[2,16,1,8,512]{4,3,0,2,1:T(8,128)}), f32[2,16,1,8,512]{4,3,0,2,1:T(8,128)S(1)}, u32[]{:S(2)}, u32[]{:S(2)}) async-start(f32[2,16,1,8,512]{4,3,0,2,1:T(8,128)} %bitcast.39), calls=%async_computation.1 | async-start | bytes 1048576 | tf_op jit(solution)/shard_map/all_to_all | solution.py:209

commit v5 on v4

--- a/solution.py
+++ b/solution.py
@@ -190,25 +190,18 @@
     energy_count = blocks.shape[0]
     green_pair = sweep(local_blocks, local_guess, coupling_block)
     green_block = jnp.stack(green_pair, axis=1)
-    picked = pick_tiles(green_pair, pair_index[0])[:, None, None]
-    momenta = momentum_table.shape[0]
+    picked = pick_tiles(green_pair, pair_index[0])
     energy_groups = lax.axis_size("energy")
     mixing = phonon_matrix(
         phonon_shift, phonon_strength, momentum_table, energy_count * energy_groups
     )
-    by_pairs = lax.all_to_all(
-        picked, ("energy", "momentum"), split_axis=3, concat_axis=1, tiled=True
-    )
-    pair_count = by_pairs.shape[3]
-    arranged = by_pairs.reshape(energy_count, energy_groups, momenta, pair_count, by_pairs.shape[4])
-    mixing_grid = mixing.reshape(
-        momenta, momenta, energy_groups, energy_count, energy_groups, energy_count
-    )
-    summed = jnp.einsum("kjabcd,dcjpx->bakpx", mixing_grid, arranged, precision=HIGHEST)
-    summed = summed.reshape(energy_count, energy_groups * momenta, 1, pair_count, by_pairs.shape[4])
-    self_energy = lax.all_to_all(
-        summed, ("energy", "momentum"), split_axis=1, concat_axis=3, tiled=True
-    )
+    gathered = lax.all_gather(picked, "momentum", axis=0)
+    momentum = lax.axis_index("momentum")
+    own_energies = lax.axis_index("energy") * energy_count
+    own_mixing = lax.dynamic_slice_in_dim(mixing[momentum], own_energies, energy_count, axis=2)
+    partial = jnp.einsum("jEd,jdpx->Epx", own_mixing, gathered, precision=HIGHEST)
+    self_energy = lax.psum_scatter(partial, "energy", scatter_dimension=0, tiled=True)
+    self_energy = self_energy[:, None, None]
     return (green_block[:, None, None], self_energy)
 
 

time: 96.3 us -> 140 us (1.45)
  waiting for transfers between devices: 26.6 us -> 63.8 us
  between operations: 1.2 us -> 14.6 us
  starting transfers between devices: 16.6 us -> 6.7 us
  matrix products: 37.1 us -> 41.6 us
    reduce_scatter x0 -> x1, waiting for transfers between devices: none -> 41.7 us  [body(): lax.psum_scatter(partial, 'energy', scatter_dimension=0, tiled=True)]
    all_to_all x2 -> x0, waiting for transfers between devices: 26.6 us -> none  [the longest x1 13.3 us: body(): lax.all_to_all(summed, ('energy', 'momentum'), split_axis=1, concat_axis=...]
    all_gather x0 -> x1, waiting for transfers between devices: none -> 22.1 us  [body(): gathered = lax.all_gather(picked, 'momentum', axis=0)]
    all_to_all x2 -> x0, starting transfers between devices: 10.3 us -> none  [the longest x1 6.05 us: body(): lax.all_to_all(picked, ('energy', 'momentum'), split_axis=3, concat_axis=...]
    dot_general x1, matrix products: 1.47 us -> 5.62 us  [body(): jnp.einsum('jEd,jdpx->Epx', own_mixing, gathered, precision=HIGHEST)]
    dot_general x0 -> x1, local copies, waits for them, and re-layouts: none -> 2.55 us  [body(): jnp.einsum('jEd,jdpx->Epx', own_mixing, gathered, precision=HIGHEST)]
    broadcast_in_dim x1 -> x0, local copies, waits for them, and re-layouts: 2.25 us -> none  [body(): picked = pick_tiles(green_pair, pair_index[0])[:, None, None]]
  transfers between devices with their start and end apart: 4 -> 4, of which waited for: 2 -> 2; matrix products, arithmetic and copies ran while one was open for 8% -> 6% of each run, Pallas kernels for 0% -> 0%
where the time goes in v5:
time: 140 us
  waiting for transfers between devices  63.8 us (46%)
  matrix products  41.6 us (30%)
  between operations  14.6 us (10%)
  Pallas kernels  7.57 us (5%)
  starting transfers between devices  6.7 us (5%)
  local copies, waits for them, and re-layouts  4.98 us (4%)
    reduce_scatter x1, waiting for transfers between devices, body(): lax.psum_scatter(partial, 'energy', scatter_dimension=0, tiled=True)  41.7 us
    all_gather x1, waiting for transfers between devices, body(): gathered = lax.all_gather(picked, 'momentum', axis=0)  22.1 us
    dot_general x13, matrix products, complex_product(): jnp.matmul(first_real, second_imag, precision=precision)  9.15 us
    dot_general x13, matrix products, complex_product(): jnp.matmul(first_real, second_real, precision=precision)  9.05 us
    dot_general x13, matrix products, complex_product(): jnp.matmul(first_imag, second_imag, precision=precision)  8.68 us
    dot_general x13, matrix products, complex_product(): jnp.matmul(first_imag, second_real, precision=precision)  8.64 us
    pallas_call x1, Pallas kernels, pick_tiles(): pl.pallas_call(pick_kernel, out_shape=jax.ShapeDtypeStruct((energy_count,...  7.57 us
    ppermute x2, starting transfers between devices, from_behind(): return lax.ppermute(shard, axis, pairs)  6.36 us
  transfers between devices with their start and end apart: 4, of which 2 were waited for; matrix products, arithmetic and copies ran while one was open for 6% of the time, Pallas kernels for 0%

profile of v5, /device:TPU:0, one launch (start us, length us, event | category | flops | bytes accessed | tf_op | source)
XLA Modules:
  0.0 139.9 jit_solution(5991954084680891255)
XLA Ops:
  7.2 2.0 %fusion.51 = f32[2,256,256]{2,1,0:T(8,128)S(1)} fusion(f32[2,1,1,2,256,256]{5,4,3,2,1,0:T(8,128)} %param.11, f32[2,1,1,2,256,256]{5,4,3,2,1,0:T(8,128)} %param.12), kind=kOutput, calls=%fused_computation.78 | convolution fusion | flops 402653184 | bytes 1572864 | tf_op jit(solution)/shard_map/dot_general | solution.py:26
  9.2 1.9 %fusion.49 = f32[2,256,256]{2,1,0:T(8,128)S(1)} fusion(f32[2,1,1,2,256,256]{5,4,3,2,1,0:T(8,128)} %param.11, f32[2,1,1,2,256,256]{5,4,3,2,1,0:T(8,128)} %param.12), kind=kOutput, calls=%fused_computation.76 | convolution fusion | flops 402653184 | bytes 1572864 | tf_op jit(solution)/shard_map/dot_general | solution.py:29
  13.8 0.7 fusion.14
  14.5 0.7 fusion.47
  15.3 0.7 fusion.12
  16.0 0.7 fusion.45
  16.8 0.7 convolution_subtract_fusion.9
  17.9 0.7 convolution_add_fusion.9
  19.0 4.9 %collective-permute-start = (f32[2,128,128]{2,1,0:T(8,128)S(1)}, f32[2,128,128]{2,1,0:T(8,128)S(1)}, u32[]{:S(2)}, u32[]{:S(2)}) collective-permute-start(f32[2,128,128]{2,1,0:T(8,128)S(1)} %fusion.26), channel_id=1, source_target_pairs={{0,1},{2,3},{4,5},{6,7},{8,9},{10,11},{12,13},{14,15},{16,17},{18,... | collective-permute-start | bytes 393224 | tf_op jit(solution)/shard_map/ppermute | solution.py:20
  24.7 1.5 %collective-permute-start.1 = (f32[2,128,128]{2,1,0:T(8,128)S(1)}, f32[2,128,128]{2,1,0:T(8,128)S(1)}, u32[]{:S(2)}, u32[]{:S(2)}) collective-permute-start(f32[2,128,128]{2,1,0:T(8,128)S(1)} %fusion.25), channel_id=1, source_target_pairs={{0,1},{2,3},{4,5},{6,7},{8,9},{10,11},{12,13},{14,15},{16,17},{18,... | collective-permute-start | bytes 393224 | tf_op jit(solution)/shard_map/ppermute | solution.py:20
  26.3 1.1 fusion.43
  27.4 1.1 fusion.37
  40.4 0.8 fusion.69
  41.9 1.1 fusion.10
  44.8 1.1 fusion.8
  47.2 1.5 %fusion.6.real_ref = f32[2,256,256]{2,1,0:T(8,128)} fusion(f32[2,256,256]{2,1,0:T(8,128)S(1)} %fusion.133, f32[2,256,256]{2,1,0:T(8,128)S(1)} %fusion.16, f32[2,256,256]{1,2,0:T(8,128)S(1)} %fusion.21, f32[2,256,256]{2,1,0:T(8,128)S(1)} %fusion.18), kind=kOutput, calls=%fused_computation.6 | convolution fusion | flops 403046400 | bytes 2621440 | tf_op jit(solution)/shard_map/dot_general | solution.py:26
  48.7 1.5 %fusion.5.imag_ref = f32[2,256,256]{2,1,0:T(8,128)} fusion(f32[2,256,256]{2,1,0:T(8,128)S(1)} %fusion.135, f32[2,256,256]{2,1,0:T(8,128)S(1)} %fusion.16, f32[2,256,256]{1,2,0:T(8,128)S(1)} %fusion.24), kind=kOutput, calls=%fused_computation.4 | convolution fusion | flops 403046400 | bytes 2097152 | tf_op jit(solution)/shard_map/dot_general | solution.py:29
  50.2 7.6 %shard_map.86 = f32[2,128,512]{2,1,0:T(8,128)} custom-call(s32[128]{0:T(128)} %and_select_fusion.partner_ref, f32[2,256,256]{2,1,0:T(8,128)} %fusion.6.real_ref, f32[2,256,256]{2,1,0:T(8,128)} %fusion.5.imag_ref), custom_call_target="tpu_custom_call" | custom-call | tf_op jit(solution)/shard_map/pallas_call | solution.py:172
  58.8 22.1 %all-gather.3.cloned.1.call-done = f32[8,128,512]{2,1,0:T(8,128)} async-done(((f32[2,128,512]{2,1,0:T(8,128)}), f32[8,128,512]{2,1,0:T(8,128)}) %all-gather.3.cloned.1.call-update) | async-done | bytes 2097168 | tf_op jit(solution)/shard_map/all_gather | solution.py:198
  80.9 5.6 %fusion.2 = f32[8,128,512]{2,0,1:T(8,128)S(1)} fusion(f32[4,2,128,512]{3,2,1,0:T(8,128)} %bitcast.203, f32[1,4,8,2]{2,1,3,0:T(4,128)S(1)} %copy.161), kind=kOutput, calls=%fused_computation.2 | convolution fusion | flops 50331648 | bytes 4194560 | tf_op jit(solution)/shard_map/jEd,jdpx->Epx/dot_general | solution.py:202
  86.5 2.5 %copy.163 = f32[8,128,512]{2,1,0:T(8,128)} copy(f32[8,128,512]{2,0,1:T(8,128)S(1)} %fusion.2) | data formatting | bytes 4194304 | tf_op jit(solution)/shard_map/jEd,jdpx->Epx/dot_general | solution.py:202
  89.1 1.0 copy-done.3
  90.3 1.0 copy.164
  91.4 41.7 %reduce-scatter.2.cloned.1.call-done = f32[2,128,512]{2,1,0:T(8,128)} async-done(((f32[8,128,512]{2,1,0:T(8,128)}), f32[2,128,512]{2,1,0:T(8,128)}) %reduce-scatter.2.cloned.1.call-update) | async-done | bytes 524304 | tf_op jit(solution)/shard_map/reduce_scatter | solution.py:203
  (70 shorter events, 21.1 us)
Async XLA Ops:
  7.2 51.0 %copy-start = (f32[2,8,4]{1,2,0:T(4,128)S(1)}, f32[2,8,4]{1,2,0:T(4,128)}, u32[]{:S(2)}) copy-start(f32[2,8,4]{1,2,0:T(4,128)} %param.16) | copy-start | bytes 772
  7.2 3.9 %copy-start.1 = (f32[2,1,1,2,256,256]{5,4,3,2,1,0:T(8,128)S(1)}, f32[2,1,1,2,256,256]{5,4,3,2,1,0:T(8,128)}, u32[]{:S(2)}) copy-start(f32[2,1,1,2,256,256]{5,4,3,2,1,0:T(8,128)} %param.11) | copy-start | bytes 3145732
  7.2 3.9 %copy-start.2 = (f32[2,1,1,2,256,256]{5,4,3,2,1,0:T(8,128)S(1)}, f32[2,1,1,2,256,256]{5,4,3,2,1,0:T(8,128)}, u32[]{:S(2)}) copy-start(f32[2,1,1,2,256,256]{5,4,3,2,1,0:T(8,128)} %param.12) | copy-start | bytes 3145732
  7.2 73.7 %all-gather.3.cloned.1.call-start = ((), (), s32[]{:S(2)}) async-start(), calls=%async_computation.2 | async-start | bytes 2621440 | tf_op jit(solution)/shard_map/all_gather | solution.py:198
  19.0 12.8 %collective-permute-start = (f32[2,128,128]{2,1,0:T(8,128)S(1)}, f32[2,128,128]{2,1,0:T(8,128)S(1)}, u32[]{:S(2)}, u32[]{:S(2)}) collective-permute-start(f32[2,128,128]{2,1,0:T(8,128)S(1)} %fusion.26), channel_id=1, source_target_pairs={{0,1},{2,3},{4,5},{6,7},{8,9},{10,11},{12,13},{14,15},{16,17},{18,... | collective-permute-start | bytes 393224 | tf_op jit(solution)/shard_map/ppermute | solution.py:20
  24.7 6.7 %collective-permute-start.1 = (f32[2,128,128]{2,1,0:T(8,128)S(1)}, f32[2,128,128]{2,1,0:T(8,128)S(1)}, u32[]{:S(2)}, u32[]{:S(2)}) collective-permute-start(f32[2,128,128]{2,1,0:T(8,128)S(1)} %fusion.25), channel_id=1, source_target_pairs={{0,1},{2,3},{4,5},{6,7},{8,9},{10,11},{12,13},{14,15},{16,17},{18,... | collective-permute-start | bytes 393224 | tf_op jit(solution)/shard_map/ppermute | solution.py:20
  29.0 1.9 %copy-start.8 = (s32[1,128]{1,0:T(1,128)S(1)}, s32[1,128]{1,0:T(1,128)}, u32[]{:S(2)}) copy-start(s32[1,128]{1,0:T(1,128)} %param.14) | copy-start | bytes 1540
  29.0 2.4 %copy-start.5 = (f32[1,1,2,128,128]{4,3,2,1,0:T(8,128)S(1)}, f32[1,1,2,128,128]{4,3,2,1,0:T(8,128)}, u32[]{:S(2)}) copy-start(f32[1,1,2,128,128]{4,3,2,1,0:T(8,128)} %param.13) | copy-start | bytes 393220
  48.7 9.4 %copy-start.7 = (s32[8]{0:T(128)S(1)}, s32[8]{0:T(128)}, u32[]{:S(2)}) copy-start(s32[8]{0:T(128)} %param.15) | copy-start | bytes 100
  48.7 9.5 %copy-start.6 = (s32[4,4]{1,0:T(4,128)S(1)}, s32[4,4]{1,0:T(4,128)}, u32[]{:S(2)}) copy-start(s32[4,4]{1,0:T(4,128)} %param.17) | copy-start | bytes 196
  57.8 75.3 %reduce-scatter.2.cloned.1.call-start = ((), (), s32[]{:S(2)}) async-start(), calls=%async_computation.1 | async-start | bytes 2621440 | tf_op jit(solution)/shard_map/reduce_scatter | solution.py:203
  89.0 1.0 copy-start.3
  89.0 1.2 copy-start.4
Sparse Core Ops, SparseCore 0:
  57.9 22.8 all-gather.2
  89.2 43.8 reduce-scatter.1

commit v6 on v4

--- a/solution.py
+++ b/solution.py
@@ -23,13 +23,12 @@
 def complex_product(first_factor, second_factor, precision=HIGHEST):
     first_real, first_imag = first_factor
     second_real, second_imag = second_factor
-    real_part = jnp.matmul(first_real, second_real, precision=precision) - jnp.matmul(
-        first_imag, second_imag, precision=precision
-    )
-    imag_part = jnp.matmul(first_real, second_imag, precision=precision) + jnp.matmul(
-        first_imag, second_real, precision=precision
-    )
-    return (real_part, imag_part)
+    real_real = jnp.matmul(first_real, second_real, precision=precision)
+    imag_imag = jnp.matmul(first_imag, second_imag, precision=precision)
+    summed = jnp.matmul(
+        first_real + first_imag, second_real + second_imag, precision=precision
+    )
+    return (real_real - imag_imag, summed - real_real - imag_imag)
 
 
 def newton_product(first_factor, second_factor):

time: 96.3 us -> 90.5 us (0.940)
  matrix products: 37.1 us -> 30.1 us
  local copies, waits for them, and re-layouts: 6.02 us -> 7.16 us
    dot_general x52 -> x39, matrix products: 35.2 us -> 28.2 us  [the longest x13 10.1 us: complex_product(): real_real = jnp.matmul(first_real, second_real, precision=precision)]
    unnamed x19, local copies, waits for them, and re-layouts: 1.76 us -> 2.89 us
where the time goes in v6:
time: 90.5 us; the launch traced here: 89.9 us
  matrix products  30.1 us (33%)
  waiting for transfers between devices  26.6 us (29%)
  starting transfers between devices  16.6 us (18%)
  Pallas kernels  7.58 us (8%)
  local copies, waits for them, and re-layouts  7.16 us (8%)
  between operations  1.09 us (1%)
    all_to_all x1, waiting for transfers between devices, body(): lax.all_to_all(summed, ('energy', 'momentum'), split_axis=1, concat_axis=...  13.3 us
    all_to_all x1, waiting for transfers between devices, body(): lax.all_to_all(picked, ('energy', 'momentum'), split_axis=3, concat_axis=...  13.2 us
    dot_general x13, matrix products, complex_product(): real_real = jnp.matmul(first_real, second_real, precision=precision)  10.1 us
    dot_general x13, matrix products, complex_product(): imag_imag = jnp.matmul(first_imag, second_imag, precision=precision)  9.03 us
    dot_general x13, matrix products, complex_product(): jnp.matmul(first_real + first_imag, second_real + second_imag, precision=...  9.01 us
    pallas_call x1, Pallas kernels, pick_tiles(): pl.pallas_call(pick_kernel, out_shape=jax.ShapeDtypeStruct((energy_count,...  7.58 us
    ppermute x2, starting transfers between devices, from_behind(): return lax.ppermute(shard, axis, pairs)  6.36 us
    all_to_all x1, starting transfers between devices, body(): lax.all_to_all(picked, ('energy', 'momentum'), split_axis=3, concat_axis=...  6.04 us
  transfers between devices with their start and end apart: 4, of which 2 were waited for; matrix products, arithmetic and copies ran while one was open for 8% of the time, Pallas kernels for 0%

profile of v6, /device:TPU:0, one launch (start us, length us, event | category | flops | bytes accessed | tf_op | source)
XLA Modules:
  0.0 89.9 jit_solution(1460608333728515134)
XLA Ops:
  0.7 1.9 %fusion.26 = f32[2,256,256]{2,1,0:T(8,128)S(1)} fusion(f32[2,1,1,2,256,256]{5,4,3,2,1,0:T(8,128)} %param.11, f32[2,1,1,2,256,256]{5,4,3,2,1,0:T(8,128)} %param.12), kind=kOutput, calls=%fused_computation.53 | convolution fusion | flops 402653184 | bytes 1572864 | tf_op jit(solution)/shard_map/dot_general | solution.py:27
  2.6 1.7 %fusion.32 = f32[2,256,256]{2,1,0:T(8,128)S(1)} fusion(f32[2,1,1,2,256,256]{5,4,3,2,1,0:T(8,128)S(1)} %copy-done.1, f32[2,1,1,2,256,256]{5,4,3,2,1,0:T(8,128)} %param.12), kind=kOutput, calls=%fused_computation.59 | convolution fusion | flops 402653184 | bytes 1572864 | tf_op jit(solution)/shard_map/dot_general | solution.py:26
  4.4 1.1 %copy-done.2 = f32[2,1,1,2,256,256]{5,4,3,2,1,0:T(8,128)S(1)} copy-done((f32[2,1,1,2,256,256]{5,4,3,2,1,0:T(8,128)S(1)}, f32[2,1,1,2,256,256]{5,4,3,2,1,0:T(8,128)}, u32[]{:S(2)}) %copy-start.2) | copy-done | bytes 1048600
  6.9 0.8 subtract_subtract_fusion.1
  7.7 0.8 fusion.5
  8.5 0.7 convolution_bitcast_fusion.7
  11.5 4.9 %collective-permute-start = (f32[2,128,128]{2,1,0:T(8,128)S(1)}, f32[2,128,128]{2,1,0:T(8,128)S(1)}, u32[]{:S(2)}, u32[]{:S(2)}) collective-permute-start(f32[2,128,128]{2,1,0:T(8,128)S(1)} %get-tuple-element.42), channel_id=1, source_target_pairs={{0,1},{2,3},{4,5},{6,7},{8,9},{10,11},{12,13},{14,15},{16,17},{18,... | collective-permute-start | bytes 393224 | tf_op jit(solution)/shard_map/ppermute | solution.py:20
  16.9 1.5 %collective-permute-start.1 = (f32[2,128,128]{2,1,0:T(8,128)S(1)}, f32[2,128,128]{2,1,0:T(8,128)S(1)}, u32[]{:S(2)}, u32[]{:S(2)}) collective-permute-start(f32[2,128,128]{2,1,0:T(8,128)S(1)} %fusion.18), channel_id=1, source_target_pairs={{0,1},{2,3},{4,5},{6,7},{8,9},{10,11},{12,13},{14,15},{16,17},{18,... | collective-permute-start | bytes 393224 | tf_op jit(solution)/shard_map/ppermute | solution.py:20
  18.4 1.1 %convolution_bitcast_fusion.4 = f32[2,256,256]{1,2,0:T(8,128)S(1)} fusion(f32[2,256,256]{2,1,0:T(8,128)S(1)} %get-tuple-element.40, f32[2,1,1,2,256,256]{5,4,3,2,1,0:T(8,128)S(1)} %copy-done.1), kind=kOutput, calls=%fused_computation.20 | convolution fusion | flops 402653184 | bytes 1572864 | tf_op jit(solution)/shard_map/dot_general | solution.py:26
  19.5 1.1 %convolution_bitcast_fusion.3 = f32[2,256,256]{1,2,0:T(8,128)S(1)} fusion(f32[2,256,256]{2,1,0:T(8,128)S(1)} %fusion.5, f32[2,1,1,2,256,256]{5,4,3,2,1,0:T(8,128)S(1)} %copy-done.1), kind=kOutput, calls=%fused_computation.19 | convolution fusion | flops 402653184 | bytes 1572864 | tf_op jit(solution)/shard_map/dot_general | solution.py:27
  30.5 1.1 %fusion.3 = f32[2,256,256]{1,2,0:T(8,128)S(1)} fusion(f32[2,256,256]{1,2,0:T(8,128)S(1)} %fusion.7, f32[2,256,256]{1,2,0:T(8,128)S(1)} %convolution_bitcast_fusion.3, f32[2,256,256]{1,2,0:T(8,128)S(1)} %convolution_bitcast_fusion.4, f32[2,256,256]{2,1,0:T(8,128)S(1)} %bitcast_add_fusion, f32[2,256,256]{2,1,0:T(8,128)S(1)} %get-tuple-element.40, ...), kind=kOutput, calls=%fused_computation.6 | convolution fusion | flops 403177472 | bytes 3670016 | tf_op jit(solution)/shard_map/dot_general | solution.py:28
  32.2 0.8 fusion.47
  34.3 1.5 %subtract_subtract_fusion = (f32[2,256,256]{2,1,0:T(8,128)}, f32[2,256,256]{2,1,0:T(8,128)S(1)}) fusion(f32[2,256,256]{2,1,0:T(8,128)S(1)} %fusion.127, f32[2,256,256]{2,1,0:T(8,128)S(1)} %get-tuple-element.47, f32[2,256,256]{1,2,0:T(8,128)S(1)} %get-tuple-element.51), kind=kOutput, calls=%fused_computation.65 | convolution fusion | flops 403046400 | bytes 2621440 | tf_op jit(solution)/shard_map/dot_general | solution.py:26
  35.8 1.6 %fusion.1.imag_ref = f32[2,256,256]{2,1,0:T(8,128)} fusion(f32[2,256,256]{2,1,0:T(8,128)S(1)} %fusion.127, f32[2,256,256]{2,1,0:T(8,128)S(1)} %get-tuple-element.54, f32[2,256,256]{1,2,0:T(8,128)S(1)} %get-tuple-element.51, f32[2,256,256]{1,2,0:T(8,128)S(1)} %fusion.14, f32[2,256,256]{2,1,0:T(8,128)S(1)} %get-tuple-element.47, f32[2,256,256]{2,1,0:T(8,128)S(1)} %fusion.9), kind=kOutput, calls=%fused_computation.3 | convolution fusion | flops 403439616 | bytes 3670016 | tf_op jit(solution)/shard_map/dot_general | solution.py:28
  37.4 7.6 %shard_map.86 = f32[2,128,512]{2,1,0:T(8,128)} custom-call(s32[128]{0:T(128)} %and_select_fusion.partner_ref, f32[2,256,256]{2,1,0:T(8,128)} %get-tuple-element.53.real_ref, f32[2,256,256]{2,1,0:T(8,128)} %fusion.1.imag_ref), custom_call_target="tpu_custom_call" | custom-call | tf_op jit(solution)/shard_map/pallas_call | solution.py:171
  45.0 2.3 %copy.188 = f32[2,1,1,128,512]{4,0,2,1,3:T(2,128)} copy(f32[2,1,1,128,512]{4,3,0,2,1:T(8,128)} %bitcast.200) | data formatting | bytes 1048576 | tf_op jit(solution)/shard_map/broadcast_in_dim | solution.py:192
  47.3 6.0 %all-to-all-start = ((f32[2,1,1,128,512]{4,0,2,1,3:T(2,128)}), f32[2,1,1,128,512]{4,0,2,1,3:T(2,128)S(1)}, u32[]{:S(2)}, u32[]{:S(2)}) async-start(f32[2,1,1,128,512]{4,0,2,1,3:T(2,128)} %copy.188), calls=%async_computation | async-start | bytes 1048576 | tf_op jit(solution)/shard_map/all_to_all | solution.py:198
  54.6 13.2 %all-to-all-done = f32[2,1,1,128,512]{4,0,2,1,3:T(2,128)S(1)} async-done(((f32[2,1,1,128,512]{4,0,2,1,3:T(2,128)}), f32[2,1,1,128,512]{4,0,2,1,3:T(2,128)S(1)}, u32[]{:S(2)}, u32[]{:S(2)}) %all-to-all-start) | async-done | bytes 524320 | tf_op jit(solution)/shard_map/all_to_all | solution.py:198
  67.8 1.5 %convolution_bitcast_fusion = f32[2,4,4,8,512]{4,1,0,2,3:T(4,128)S(1)} fusion(f32[2,4,4,8,512,1,1]{4,0,3,2,1,6,5:T(2,128)S(1)} %bitcast.201, f32[4,4,4,2,4,2]{1,5,4,3,2,0:T(2,128)S(1)} %bitcast.203), kind=kOutput, calls=%fused_computation | convolution fusion | flops 50331648 | bytes 1052672 | tf_op jit(solution)/shard_map/kjabcd,dcjpx->bakpx/dot_general | solution.py:206
  69.3 1.1 %copy.242 = f32[2,4,4,8,512]{4,3,0,2,1:T(8,128)} copy(f32[2,4,4,8,512]{4,1,0,2,3:T(4,128)S(1)} %convolution_bitcast_fusion) | data formatting | bytes 1048576 | tf_op jit(solution)/shard_map/reshape | solution.py:207
  70.4 4.2 %all-to-all-start.1 = ((f32[2,16,1,8,512]{4,3,0,2,1:T(8,128)}), f32[2,16,1,8,512]{4,3,0,2,1:T(8,128)S(1)}, u32[]{:S(2)}, u32[]{:S(2)}) async-start(f32[2,16,1,8,512]{4,3,0,2,1:T(8,128)} %bitcast.42), calls=%async_computation.1 | async-start | bytes 1048576 | tf_op jit(solution)/shard_map/all_to_all | solution.py:208
  74.7 1.0 %copy.196 = f32[2,1,1,2,256,256]{5,4,3,2,1,0:T(8,128)} copy(f32[2,1,1,2,256,256]{5,4,0,3,2,1:T(8,128)S(1)} %maximum_bitcast_fusion) | data formatting | bytes 2097152
  75.8 13.3 %all-to-all-done.1 = f32[2,16,1,8,512]{4,3,0,2,1:T(8,128)S(1)} async-done(((f32[2,16,1,8,512]{4,3,0,2,1:T(8,128)}), f32[2,16,1,8,512]{4,3,0,2,1:T(8,128)S(1)}, u32[]{:S(2)}, u32[]{:S(2)}) %all-to-all-start.1) | async-done | bytes 524320 | tf_op jit(solution)/shard_map/all_to_all | solution.py:208
  89.1 0.8 copy.254
  (56 shorter events, 17.1 us)
Async XLA Ops:
  0.6 52.7 %copy-start = (f32[2,8,4]{1,2,0:T(4,128)S(1)}, f32[2,8,4]{1,2,0:T(4,128)}, u32[]{:S(2)}) copy-start(f32[2,8,4]{1,2,0:T(4,128)} %param.16) | copy-start | bytes 772
  0.6 2.0 %copy-start.1 = (f32[2,1,1,2,256,256]{5,4,3,2,1,0:T(8,128)S(1)}, f32[2,1,1,2,256,256]{5,4,3,2,1,0:T(8,128)}, u32[]{:S(2)}) copy-start(f32[2,1,1,2,256,256]{5,4,3,2,1,0:T(8,128)} %param.11) | copy-start | bytes 3145732
  4.3 1.2 %copy-start.2 = (f32[2,1,1,2,256,256]{5,4,3,2,1,0:T(8,128)S(1)}, f32[2,1,1,2,256,256]{5,4,3,2,1,0:T(8,128)}, u32[]{:S(2)}) copy-start(f32[2,1,1,2,256,256]{5,4,3,2,1,0:T(8,128)} %param.12) | copy-start | bytes 3145732
  11.5 11.5 %collective-permute-start = (f32[2,128,128]{2,1,0:T(8,128)S(1)}, f32[2,128,128]{2,1,0:T(8,128)S(1)}, u32[]{:S(2)}, u32[]{:S(2)}) collective-permute-start(f32[2,128,128]{2,1,0:T(8,128)S(1)} %get-tuple-element.42), channel_id=1, source_target_pairs={{0,1},{2,3},{4,5},{6,7},{8,9},{10,11},{12,13},{14,15},{16,17},{18,... | collective-permute-start | bytes 393224 | tf_op jit(solution)/shard_map/ppermute | solution.py:20
  16.9 6.6 %collective-permute-start.1 = (f32[2,128,128]{2,1,0:T(8,128)S(1)}, f32[2,128,128]{2,1,0:T(8,128)S(1)}, u32[]{:S(2)}, u32[]{:S(2)}) collective-permute-start(f32[2,128,128]{2,1,0:T(8,128)S(1)} %fusion.18), channel_id=1, source_target_pairs={{0,1},{2,3},{4,5},{6,7},{8,9},{10,11},{12,13},{14,15},{16,17},{18,... | collective-permute-start | bytes 393224 | tf_op jit(solution)/shard_map/ppermute | solution.py:20
  21.8 0.7 copy-start.8
  21.8 1.2 %copy-start.5 = (f32[1,1,2,128,128]{4,3,2,1,0:T(8,128)S(1)}, f32[1,1,2,128,128]{4,3,2,1,0:T(8,128)}, u32[]{:S(2)}) copy-start(f32[1,1,2,128,128]{4,3,2,1,0:T(8,128)} %param.13) | copy-start | bytes 393220
  47.3 6.1 %copy-start.7 = (s32[8]{0:T(128)S(1)}, s32[8]{0:T(128)}, u32[]{:S(2)}) copy-start(s32[8]{0:T(128)} %param.15) | copy-start | bytes 100
  47.3 20.5 %all-to-all-start = ((f32[2,1,1,128,512]{4,0,2,1,3:T(2,128)}), f32[2,1,1,128,512]{4,0,2,1,3:T(2,128)S(1)}, u32[]{:S(2)}, u32[]{:S(2)}) async-start(f32[2,1,1,128,512]{4,0,2,1,3:T(2,128)} %copy.188), calls=%async_computation | async-start | bytes 1048576 | tf_op jit(solution)/shard_map/all_to_all | solution.py:198
  53.3 0.7 copy-start.6
  70.4 4.2 %copy-start.3 = (f32[2,256,256]{2,1,0:T(8,128)S(1)}, f32[2,256,256]{2,1,0:T(8,128)}, u32[]{:S(2)}) copy-start(f32[2,256,256]{2,1,0:T(8,128)} %get-tuple-element.53.real_ref) | copy-start | bytes 1572868
  70.4 4.3 %copy-start.4 = (f32[2,256,256]{2,1,0:T(8,128)S(1)}, f32[2,256,256]{2,1,0:T(8,128)}, u32[]{:S(2)}) copy-start(f32[2,256,256]{2,1,0:T(8,128)} %fusion.1.imag_ref) | copy-start | bytes 1572868
  70.4 18.7 %all-to-all-start.1 = ((f32[2,16,1,8,512]{4,3,0,2,1:T(8,128)}), f32[2,16,1,8,512]{4,3,0,2,1:T(8,128)S(1)}, u32[]{:S(2)}, u32[]{:S(2)}) async-start(f32[2,16,1,8,512]{4,3,0,2,1:T(8,128)} %bitcast.42), calls=%async_computation.1 | async-start | bytes 1048576 | tf_op jit(solution)/shard_map/all_to_all | solution.py:208

commit v7 on v6

--- a/solution.py
+++ b/solution.py
@@ -139,14 +139,21 @@
         target = jnp.zeros((1, width), jnp.int32)
         for j in range(per_atom):
             target = jnp.where(lane_tile == j, partner_ref[atom * per_atom + j], target)
-        pick = jnp.where((row_atom == target) & same_orbital, 1.0, 0.0)
+        pick = jnp.where((row_atom == target) & same_orbital, 1.0, 0.0).astype(jnp.bfloat16)
         start = pl.multiple_of(atom * ORB, ORB)
         stripes = []
         for e in range(energy_count):
             stripes.append(real_ref[e, pl.ds(start, ORB), :])
             stripes.append(imag_ref[e, pl.ds(start, ORB), :])
         stripes = jnp.concatenate(stripes, axis=0)
-        chosen = jnp.dot(stripes, pick, precision=HIGHEST, preferred_element_type=jnp.float32)
+        high = stripes.astype(jnp.bfloat16)
+        rest = stripes - high.astype(jnp.float32)
+        middle = rest.astype(jnp.bfloat16)
+        low = (rest - middle.astype(jnp.float32)).astype(jnp.bfloat16)
+        pieces = jnp.concatenate([high, middle, low], axis=0)
+        selected = jnp.dot(pieces, pick, preferred_element_type=jnp.float32)
+        rows = stripes.shape[0]
+        chosen = (selected[:rows] + selected[rows : 2 * rows]) + selected[2 * rows :]
         out_start = pl.multiple_of(atom * per_atom, per_atom)
         for g in range(2 * energy_count):
             for half in range(halves):

time: 90.5 us -> 89.7 us (level)
  no operation moved by 1% of the time
where the time goes in v7:
time: 89.7 us; the launch traced here: 89.1 us
  matrix products  30.1 us (34%)
  waiting for transfers between devices  26.6 us (30%)
  starting transfers between devices  16.6 us (19%)
  local copies, waits for them, and re-layouts  7.16 us (8%)
  Pallas kernels  6.76 us (8%)
  between operations  1.09 us (1%)
    all_to_all x1, waiting for transfers between devices, body(): lax.all_to_all(summed, ('energy', 'momentum'), split_axis=1, concat_axis=...  13.3 us
    all_to_all x1, waiting for transfers between devices, body(): lax.all_to_all(picked, ('energy', 'momentum'), split_axis=3, concat_axis=...  13.2 us
    dot_general x13, matrix products, complex_product(): real_real = jnp.matmul(first_real, second_real, precision=precision)  10.1 us
    dot_general x13, matrix products, complex_product(): imag_imag = jnp.matmul(first_imag, second_imag, precision=precision)  9.03 us
    dot_general x13, matrix products, complex_product(): jnp.matmul(first_real + first_imag, second_real + second_imag, precision=...  9.01 us
    pallas_call x1, Pallas kernels, pick_tiles(): pl.pallas_call(pick_kernel, out_shape=jax.ShapeDtypeStruct((energy_count,...  6.76 us
    ppermute x2, starting transfers between devices, from_behind(): return lax.ppermute(shard, axis, pairs)  6.36 us
    all_to_all x1, starting transfers between devices, body(): lax.all_to_all(picked, ('energy', 'momentum'), split_axis=3, concat_axis=...  6.04 us
  transfers between devices with their start and end apart: 4, of which 2 were waited for; matrix products, arithmetic and copies ran while one was open for 8% of the time, Pallas kernels for 0%

profile of v7, /device:TPU:0, one launch (start us, length us, event | category | flops | bytes accessed | tf_op | source)
XLA Modules:
  0.0 89.1 jit_solution(3913571571452529879)
XLA Ops:
  0.7 1.9 %fusion.26 = f32[2,256,256]{2,1,0:T(8,128)S(1)} fusion(f32[2,1,1,2,256,256]{5,4,3,2,1,0:T(8,128)} %param.11, f32[2,1,1,2,256,256]{5,4,3,2,1,0:T(8,128)} %param.12), kind=kOutput, calls=%fused_computation.53 | convolution fusion | flops 402653184 | bytes 1572864 | tf_op jit(solution)/shard_map/dot_general | solution.py:27
  2.6 1.7 %fusion.32 = f32[2,256,256]{2,1,0:T(8,128)S(1)} fusion(f32[2,1,1,2,256,256]{5,4,3,2,1,0:T(8,128)S(1)} %copy-done.1, f32[2,1,1,2,256,256]{5,4,3,2,1,0:T(8,128)} %param.12), kind=kOutput, calls=%fused_computation.59 | convolution fusion | flops 402653184 | bytes 1572864 | tf_op jit(solution)/shard_map/dot_general | solution.py:26
  4.4 1.1 %copy-done.2 = f32[2,1,1,2,256,256]{5,4,3,2,1,0:T(8,128)S(1)} copy-done((f32[2,1,1,2,256,256]{5,4,3,2,1,0:T(8,128)S(1)}, f32[2,1,1,2,256,256]{5,4,3,2,1,0:T(8,128)}, u32[]{:S(2)}) %copy-start.2) | copy-done | bytes 1048600
  6.9 0.8 subtract_subtract_fusion.1
  7.7 0.8 fusion.5
  8.5 0.7 convolution_bitcast_fusion.7
  11.5 4.9 %collective-permute-start = (f32[2,128,128]{2,1,0:T(8,128)S(1)}, f32[2,128,128]{2,1,0:T(8,128)S(1)}, u32[]{:S(2)}, u32[]{:S(2)}) collective-permute-start(f32[2,128,128]{2,1,0:T(8,128)S(1)} %get-tuple-element.42), channel_id=1, source_target_pairs={{0,1},{2,3},{4,5},{6,7},{8,9},{10,11},{12,13},{14,15},{16,17},{18,... | collective-permute-start | bytes 393224 | tf_op jit(solution)/shard_map/ppermute | solution.py:20
  16.9 1.5 %collective-permute-start.1 = (f32[2,128,128]{2,1,0:T(8,128)S(1)}, f32[2,128,128]{2,1,0:T(8,128)S(1)}, u32[]{:S(2)}, u32[]{:S(2)}) collective-permute-start(f32[2,128,128]{2,1,0:T(8,128)S(1)} %fusion.18), channel_id=1, source_target_pairs={{0,1},{2,3},{4,5},{6,7},{8,9},{10,11},{12,13},{14,15},{16,17},{18,... | collective-permute-start | bytes 393224 | tf_op jit(solution)/shard_map/ppermute | solution.py:20
  18.4 1.1 %convolution_bitcast_fusion.4 = f32[2,256,256]{1,2,0:T(8,128)S(1)} fusion(f32[2,256,256]{2,1,0:T(8,128)S(1)} %get-tuple-element.40, f32[2,1,1,2,256,256]{5,4,3,2,1,0:T(8,128)S(1)} %copy-done.1), kind=kOutput, calls=%fused_computation.20 | convolution fusion | flops 402653184 | bytes 1572864 | tf_op jit(solution)/shard_map/dot_general | solution.py:26
  19.5 1.1 %convolution_bitcast_fusion.3 = f32[2,256,256]{1,2,0:T(8,128)S(1)} fusion(f32[2,256,256]{2,1,0:T(8,128)S(1)} %fusion.5, f32[2,1,1,2,256,256]{5,4,3,2,1,0:T(8,128)S(1)} %copy-done.1), kind=kOutput, calls=%fused_computation.19 | convolution fusion | flops 402653184 | bytes 1572864 | tf_op jit(solution)/shard_map/dot_general | solution.py:27
  30.5 1.1 %fusion.3 = f32[2,256,256]{1,2,0:T(8,128)S(1)} fusion(f32[2,256,256]{1,2,0:T(8,128)S(1)} %fusion.7, f32[2,256,256]{1,2,0:T(8,128)S(1)} %convolution_bitcast_fusion.3, f32[2,256,256]{1,2,0:T(8,128)S(1)} %convolution_bitcast_fusion.4, f32[2,256,256]{2,1,0:T(8,128)S(1)} %bitcast_add_fusion, f32[2,256,256]{2,1,0:T(8,128)S(1)} %get-tuple-element.40, ...), kind=kOutput, calls=%fused_computation.6 | convolution fusion | flops 403177472 | bytes 3670016 | tf_op jit(solution)/shard_map/dot_general | solution.py:28
  32.2 0.8 fusion.47
  34.3 1.5 %subtract_subtract_fusion = (f32[2,256,256]{2,1,0:T(8,128)}, f32[2,256,256]{2,1,0:T(8,128)S(1)}) fusion(f32[2,256,256]{2,1,0:T(8,128)S(1)} %fusion.127, f32[2,256,256]{2,1,0:T(8,128)S(1)} %get-tuple-element.47, f32[2,256,256]{1,2,0:T(8,128)S(1)} %get-tuple-element.51), kind=kOutput, calls=%fused_computation.65 | convolution fusion | flops 403046400 | bytes 2621440 | tf_op jit(solution)/shard_map/dot_general | solution.py:26
  35.8 1.6 %fusion.1.imag_ref = f32[2,256,256]{2,1,0:T(8,128)} fusion(f32[2,256,256]{2,1,0:T(8,128)S(1)} %fusion.127, f32[2,256,256]{2,1,0:T(8,128)S(1)} %get-tuple-element.54, f32[2,256,256]{1,2,0:T(8,128)S(1)} %get-tuple-element.51, f32[2,256,256]{1,2,0:T(8,128)S(1)} %fusion.14, f32[2,256,256]{2,1,0:T(8,128)S(1)} %get-tuple-element.47, f32[2,256,256]{2,1,0:T(8,128)S(1)} %fusion.9), kind=kOutput, calls=%fused_computation.3 | convolution fusion | flops 403439616 | bytes 3670016 | tf_op jit(solution)/shard_map/dot_general | solution.py:28
  37.4 6.8 %shard_map.86 = f32[2,128,512]{2,1,0:T(8,128)} custom-call(s32[128]{0:T(128)} %and_select_fusion.partner_ref, f32[2,256,256]{2,1,0:T(8,128)} %get-tuple-element.53.real_ref, f32[2,256,256]{2,1,0:T(8,128)} %fusion.1.imag_ref), custom_call_target="tpu_custom_call" | custom-call | tf_op jit(solution)/shard_map/pallas_call | solution.py:178
  44.2 2.3 %copy.188 = f32[2,1,1,128,512]{4,0,2,1,3:T(2,128)} copy(f32[2,1,1,128,512]{4,3,0,2,1:T(8,128)} %bitcast.200) | data formatting | bytes 1048576 | tf_op jit(solution)/shard_map/broadcast_in_dim | solution.py:199
  46.4 6.0 %all-to-all-start = ((f32[2,1,1,128,512]{4,0,2,1,3:T(2,128)}), f32[2,1,1,128,512]{4,0,2,1,3:T(2,128)S(1)}, u32[]{:S(2)}, u32[]{:S(2)}) async-start(f32[2,1,1,128,512]{4,0,2,1,3:T(2,128)} %copy.188), calls=%async_computation | async-start | bytes 1048576 | tf_op jit(solution)/shard_map/all_to_all | solution.py:205
  53.7 13.2 %all-to-all-done = f32[2,1,1,128,512]{4,0,2,1,3:T(2,128)S(1)} async-done(((f32[2,1,1,128,512]{4,0,2,1,3:T(2,128)}), f32[2,1,1,128,512]{4,0,2,1,3:T(2,128)S(1)}, u32[]{:S(2)}, u32[]{:S(2)}) %all-to-all-start) | async-done | bytes 524320 | tf_op jit(solution)/shard_map/all_to_all | solution.py:205
  67.0 1.5 %convolution_bitcast_fusion = f32[2,4,4,8,512]{4,1,0,2,3:T(4,128)S(1)} fusion(f32[2,4,4,8,512,1,1]{4,0,3,2,1,6,5:T(2,128)S(1)} %bitcast.201, f32[4,4,4,2,4,2]{1,5,4,3,2,0:T(2,128)S(1)} %bitcast.203), kind=kOutput, calls=%fused_computation | convolution fusion | flops 50331648 | bytes 1052672 | tf_op jit(solution)/shard_map/kjabcd,dcjpx->bakpx/dot_general | solution.py:213
  68.4 1.1 %copy.242 = f32[2,4,4,8,512]{4,3,0,2,1:T(8,128)} copy(f32[2,4,4,8,512]{4,1,0,2,3:T(4,128)S(1)} %convolution_bitcast_fusion) | data formatting | bytes 1048576 | tf_op jit(solution)/shard_map/reshape | solution.py:214
  69.6 4.2 %all-to-all-start.1 = ((f32[2,16,1,8,512]{4,3,0,2,1:T(8,128)}), f32[2,16,1,8,512]{4,3,0,2,1:T(8,128)S(1)}, u32[]{:S(2)}, u32[]{:S(2)}) async-start(f32[2,16,1,8,512]{4,3,0,2,1:T(8,128)} %bitcast.42), calls=%async_computation.1 | async-start | bytes 1048576 | tf_op jit(solution)/shard_map/all_to_all | solution.py:215
  73.9 1.0 %copy.196 = f32[2,1,1,2,256,256]{5,4,3,2,1,0:T(8,128)} copy(f32[2,1,1,2,256,256]{5,4,0,3,2,1:T(8,128)S(1)} %maximum_bitcast_fusion) | data formatting | bytes 2097152
  74.9 13.3 %all-to-all-done.1 = f32[2,16,1,8,512]{4,3,0,2,1:T(8,128)S(1)} async-done(((f32[2,16,1,8,512]{4,3,0,2,1:T(8,128)}), f32[2,16,1,8,512]{4,3,0,2,1:T(8,128)S(1)}, u32[]{:S(2)}, u32[]{:S(2)}) %all-to-all-start.1) | async-done | bytes 524320 | tf_op jit(solution)/shard_map/all_to_all | solution.py:215
  88.3 0.8 copy.254
  (56 shorter events, 17.1 us)
Async XLA Ops:
  0.6 51.9 %copy-start = (f32[2,8,4]{1,2,0:T(4,128)S(1)}, f32[2,8,4]{1,2,0:T(4,128)}, u32[]{:S(2)}) copy-start(f32[2,8,4]{1,2,0:T(4,128)} %param.16) | copy-start | bytes 772
  0.6 2.0 %copy-start.1 = (f32[2,1,1,2,256,256]{5,4,3,2,1,0:T(8,128)S(1)}, f32[2,1,1,2,256,256]{5,4,3,2,1,0:T(8,128)}, u32[]{:S(2)}) copy-start(f32[2,1,1,2,256,256]{5,4,3,2,1,0:T(8,128)} %param.11) | copy-start | bytes 3145732
  4.3 1.2 %copy-start.2 = (f32[2,1,1,2,256,256]{5,4,3,2,1,0:T(8,128)S(1)}, f32[2,1,1,2,256,256]{5,4,3,2,1,0:T(8,128)}, u32[]{:S(2)}) copy-start(f32[2,1,1,2,256,256]{5,4,3,2,1,0:T(8,128)} %param.12) | copy-start | bytes 3145732
  11.5 11.5 %collective-permute-start = (f32[2,128,128]{2,1,0:T(8,128)S(1)}, f32[2,128,128]{2,1,0:T(8,128)S(1)}, u32[]{:S(2)}, u32[]{:S(2)}) collective-permute-start(f32[2,128,128]{2,1,0:T(8,128)S(1)} %get-tuple-element.42), channel_id=1, source_target_pairs={{0,1},{2,3},{4,5},{6,7},{8,9},{10,11},{12,13},{14,15},{16,17},{18,... | collective-permute-start | bytes 393224 | tf_op jit(solution)/shard_map/ppermute | solution.py:20
  16.9 6.6 %collective-permute-start.1 = (f32[2,128,128]{2,1,0:T(8,128)S(1)}, f32[2,128,128]{2,1,0:T(8,128)S(1)}, u32[]{:S(2)}, u32[]{:S(2)}) collective-permute-start(f32[2,128,128]{2,1,0:T(8,128)S(1)} %fusion.18), channel_id=1, source_target_pairs={{0,1},{2,3},{4,5},{6,7},{8,9},{10,11},{12,13},{14,15},{16,17},{18,... | collective-permute-start | bytes 393224 | tf_op jit(solution)/shard_map/ppermute | solution.py:20
  21.8 0.7 copy-start.8
  21.8 1.2 %copy-start.5 = (f32[1,1,2,128,128]{4,3,2,1,0:T(8,128)S(1)}, f32[1,1,2,128,128]{4,3,2,1,0:T(8,128)}, u32[]{:S(2)}) copy-start(f32[1,1,2,128,128]{4,3,2,1,0:T(8,128)} %param.13) | copy-start | bytes 393220
  46.4 6.1 %copy-start.7 = (s32[8]{0:T(128)S(1)}, s32[8]{0:T(128)}, u32[]{:S(2)}) copy-start(s32[8]{0:T(128)} %param.15) | copy-start | bytes 100
  46.4 20.5 %all-to-all-start = ((f32[2,1,1,128,512]{4,0,2,1,3:T(2,128)}), f32[2,1,1,128,512]{4,0,2,1,3:T(2,128)S(1)}, u32[]{:S(2)}, u32[]{:S(2)}) async-start(f32[2,1,1,128,512]{4,0,2,1,3:T(2,128)} %copy.188), calls=%async_computation | async-start | bytes 1048576 | tf_op jit(solution)/shard_map/all_to_all | solution.py:205
  52.5 0.7 copy-start.6
  69.5 4.2 %copy-start.3 = (f32[2,256,256]{2,1,0:T(8,128)S(1)}, f32[2,256,256]{2,1,0:T(8,128)}, u32[]{:S(2)}) copy-start(f32[2,256,256]{2,1,0:T(8,128)} %get-tuple-element.53.real_ref) | copy-start | bytes 1572868
  69.6 4.3 %copy-start.4 = (f32[2,256,256]{2,1,0:T(8,128)S(1)}, f32[2,256,256]{2,1,0:T(8,128)}, u32[]{:S(2)}) copy-start(f32[2,256,256]{2,1,0:T(8,128)} %fusion.1.imag_ref) | copy-start | bytes 1572868
  69.6 18.7 %all-to-all-start.1 = ((f32[2,16,1,8,512]{4,3,0,2,1:T(8,128)}), f32[2,16,1,8,512]{4,3,0,2,1:T(8,128)S(1)}, u32[]{:S(2)}, u32[]{:S(2)}) async-start(f32[2,16,1,8,512]{4,3,0,2,1:T(8,128)} %bitcast.42), calls=%async_computation.1 | async-start | bytes 1048576 | tf_op jit(solution)/shard_map/all_to_all | solution.py:215

commit v8 on v7

--- a/solution.py
+++ b/solution.py
@@ -119,6 +119,7 @@
 
 def pick_kernel(partner_ref, real_ref, imag_ref, out_ref):
     energy_count, size, _ = real_ref.shape
+    chunk = out_ref.shape[2]
     atoms = size // ORB
     per_atom = partner_ref.shape[0] // atoms
     width = per_atom * ORB
@@ -165,19 +166,28 @@
                     moved = pltpu.roll(moved, d * ORB, 1)
                     flipped = jnp.where(diagonal[d], moved, flipped)
                 lane = (g % 2) * flat + half * width
-                out_ref[g // 2, pl.ds(out_start, per_atom), pl.ds(lane, width)] = flipped
+                if chunk >= per_atom:
+                    out_ref[
+                        out_start // chunk, g // 2, pl.ds(out_start % chunk, per_atom), pl.ds(lane, width)
+                    ] = flipped
+                else:
+                    for q in range(per_atom // chunk):
+                        out_ref[
+                            atom * (per_atom // chunk) + q, g // 2, :, pl.ds(lane, width)
+                        ] = flipped[q * chunk : (q + 1) * chunk]
         return carry
 
     lax.fori_loop(0, atoms, one_atom, 0)
 
 
-def pick_tiles(green_pair, pair_index):
+def pick_tiles(green_pair, pair_index, chunks):
     energy_count = green_pair[0].shape[0]
     pair_count = pair_index.shape[0]
     partner = pair_index % ATOMS
+    shape = (chunks, energy_count, pair_count // chunks, 2 * ORB * ORB)
     return pl.pallas_call(
         pick_kernel,
-        out_shape=jax.ShapeDtypeStruct((energy_count, pair_count, 2 * ORB * ORB), jnp.float32),
+        out_shape=jax.ShapeDtypeStruct(shape, jnp.float32),
         in_specs=[
             pl.BlockSpec(memory_space=pltpu.SMEM),
             pl.BlockSpec(memory_space=pltpu.VMEM),
@@ -196,25 +206,25 @@
     energy_count = blocks.shape[0]
     green_pair = sweep(local_blocks, local_guess, coupling_block)
     green_block = jnp.stack(green_pair, axis=1)
-    picked = pick_tiles(green_pair, pair_index[0])[:, None, None]
     momenta = momentum_table.shape[0]
     energy_groups = lax.axis_size("energy")
+    axes = ("energy", "momentum")
+    group = energy_groups * lax.axis_size("momentum")
+    pair_count = pair_index.shape[1]
+    width = 2 * ORB * ORB
+    picked = pick_tiles(green_pair, pair_index[0], group)
     mixing = phonon_matrix(
         phonon_shift, phonon_strength, momentum_table, energy_count * energy_groups
     )
-    by_pairs = lax.all_to_all(
-        picked, ("energy", "momentum"), split_axis=3, concat_axis=1, tiled=True
-    )
-    pair_count = by_pairs.shape[3]
-    arranged = by_pairs.reshape(energy_count, energy_groups, momenta, pair_count, by_pairs.shape[4])
+    by_pairs = lax.all_to_all(picked, axes, 0, 0, tiled=True)
+    arranged = by_pairs.reshape(energy_groups, momenta, energy_count, pair_count // group, width)
     mixing_grid = mixing.reshape(
         momenta, momenta, energy_groups, energy_count, energy_groups, energy_count
     )
-    summed = jnp.einsum("kjabcd,dcjpx->bakpx", mixing_grid, arranged, precision=HIGHEST)
-    summed = summed.reshape(energy_count, energy_groups * momenta, 1, pair_count, by_pairs.shape[4])
-    self_energy = lax.all_to_all(
-        summed, ("energy", "momentum"), split_axis=1, concat_axis=3, tiled=True
-    )
+    summed = jnp.einsum("kjabcd,cjdpx->akbpx", mixing_grid, arranged, precision=HIGHEST)
+    summed = summed.reshape(group, energy_count, pair_count // group, width)
+    self_energy = lax.all_to_all(summed, axes, 0, 2, tiled=True)
+    self_energy = self_energy.reshape(energy_count, 1, 1, pair_count, width)
     return (green_block[:, None, None], self_energy)
 
 

time: 89.7 us -> 87.2 us (0.972)
  local copies, waits for them, and re-layouts: 7.16 us -> 4.91 us
    broadcast_in_dim x1 -> x0, local copies, waits for them, and re-layouts: 2.26 us -> none  [body(): picked = pick_tiles(green_pair, pair_index[0])[:, None, None]]
    reshape x1 -> x0, local copies, waits for them, and re-layouts: 1.12 us -> none  [body(): summed.reshape(energy_count, energy_groups * momenta, 1, pair_count, by_p...]
    transpose x0 -> x1, local copies, waits for them, and re-layouts: none -> 1.12 us  [body(): jnp.einsum('kjabcd,cjdpx->akbpx', mixing_grid, arranged, precision=HIGHEST)]
    unnamed x19 -> x20, local copies, waits for them, and re-layouts: 2.89 us -> 3.72 us
where the time goes in v8:
time: 87.2 us; the launch traced here: 86.7 us
  matrix products  29.9 us (34%)
  waiting for transfers between devices  26.5 us (30%)
  starting transfers between devices  16.6 us (19%)
  Pallas kernels  6.76 us (8%)
  local copies, waits for them, and re-layouts  4.91 us (6%)
  between operations  1.09 us (1%)
    all_to_all x1, waiting for transfers between devices, body(): self_energy = lax.all_to_all(summed, axes, 0, 2, tiled=True)  13.3 us
    all_to_all x1, waiting for transfers between devices, body(): by_pairs = lax.all_to_all(picked, axes, 0, 0, tiled=True)  13.2 us
    dot_general x13, matrix products, complex_product(): real_real = jnp.matmul(first_real, second_real, precision=precision)  9.81 us
    dot_general x13, matrix products, complex_product(): jnp.matmul(first_real + first_imag, second_real + second_imag, precision=...  9.22 us
    dot_general x13, matrix products, complex_product(): imag_imag = jnp.matmul(first_imag, second_imag, precision=precision)  8.97 us
    pallas_call x1, Pallas kernels, pick_tiles(): pl.pallas_call(pick_kernel, out_shape=jax.ShapeDtypeStruct(shape, jnp.flo...  6.76 us
    ppermute x2, starting transfers between devices, from_behind(): return lax.ppermute(shard, axis, pairs)  6.36 us
    all_to_all x1, starting transfers between devices, body(): by_pairs = lax.all_to_all(picked, axes, 0, 0, tiled=True)  6.03 us
  transfers between devices with their start and end apart: 4, of which 2 were waited for; matrix products, arithmetic and copies ran while one was open for 8% of the time, Pallas kernels for 0%

profile of v8, /device:TPU:0, one launch (start us, length us, event | category | flops | bytes accessed | tf_op | source)
XLA Modules:
  0.0 86.7 jit_solution(13178279546026523616)
XLA Ops:
  0.7 1.9 %fusion.26 = f32[2,256,256]{2,1,0:T(8,128)S(1)} fusion(f32[2,1,1,2,256,256]{5,4,3,2,1,0:T(8,128)} %param.11, f32[2,1,1,2,256,256]{5,4,3,2,1,0:T(8,128)} %param.12), kind=kOutput, calls=%fused_computation.53 | convolution fusion | flops 402653184 | bytes 1572864 | tf_op jit(solution)/shard_map/dot_general | solution.py:27
  2.6 1.7 %fusion.32 = f32[2,256,256]{2,1,0:T(8,128)S(1)} fusion(f32[2,1,1,2,256,256]{5,4,3,2,1,0:T(8,128)S(1)} %copy-done.1, f32[2,1,1,2,256,256]{5,4,3,2,1,0:T(8,128)} %param.12), kind=kOutput, calls=%fused_computation.59 | convolution fusion | flops 402653184 | bytes 1572864 | tf_op jit(solution)/shard_map/dot_general | solution.py:26
  4.4 1.1 %copy-done.2 = f32[2,1,1,2,256,256]{5,4,3,2,1,0:T(8,128)S(1)} copy-done((f32[2,1,1,2,256,256]{5,4,3,2,1,0:T(8,128)S(1)}, f32[2,1,1,2,256,256]{5,4,3,2,1,0:T(8,128)}, u32[]{:S(2)}) %copy-start.2) | copy-done | bytes 1048600
  7.6 0.8 fusion.5
  9.1 0.7 convolution_bitcast_fusion.8
  9.9 0.7 fusion.15
  11.4 4.9 %collective-permute-start = (f32[2,128,128]{2,1,0:T(8,128)S(1)}, f32[2,128,128]{2,1,0:T(8,128)S(1)}, u32[]{:S(2)}, u32[]{:S(2)}) collective-permute-start(f32[2,128,128]{2,1,0:T(8,128)S(1)} %get-tuple-element.40), channel_id=1, source_target_pairs={{0,1},{2,3},{4,5},{6,7},{8,9},{10,11},{12,13},{14,15},{16,17},{18,... | collective-permute-start | bytes 393224 | tf_op jit(solution)/shard_map/ppermute | solution.py:20
  16.7 1.5 %collective-permute-start.1 = (f32[2,128,128]{2,1,0:T(8,128)S(1)}, f32[2,128,128]{2,1,0:T(8,128)S(1)}, u32[]{:S(2)}, u32[]{:S(2)}) collective-permute-start(f32[2,128,128]{2,1,0:T(8,128)S(1)} %fusion.18), channel_id=1, source_target_pairs={{0,1},{2,3},{4,5},{6,7},{8,9},{10,11},{12,13},{14,15},{16,17},{18,... | collective-permute-start | bytes 393224 | tf_op jit(solution)/shard_map/ppermute | solution.py:20
  18.3 1.0 %convolution_bitcast_fusion.4 = f32[2,256,256]{1,2,0:T(8,128)S(1)} fusion(f32[2,256,256]{2,1,0:T(8,128)S(1)} %get-tuple-element.38, f32[2,1,1,2,256,256]{5,4,3,2,1,0:T(8,128)S(1)} %copy-done.1), kind=kOutput, calls=%fused_computation.20 | convolution fusion | flops 402653184 | bytes 1572864 | tf_op jit(solution)/shard_map/dot_general | solution.py:26
  19.4 1.0 %convolution_bitcast_fusion.3 = f32[2,256,256]{1,2,0:T(8,128)S(1)} fusion(f32[2,256,256]{2,1,0:T(8,128)S(1)} %fusion.5, f32[2,1,1,2,256,256]{5,4,3,2,1,0:T(8,128)S(1)} %copy-done.1), kind=kOutput, calls=%fused_computation.19 | convolution fusion | flops 402653184 | bytes 1572864 | tf_op jit(solution)/shard_map/dot_general | solution.py:27
  28.9 0.7 subtract_add_fusion
  30.3 1.1 %fusion.3 = f32[2,256,256]{1,2,0:T(8,128)S(1)} fusion(f32[2,256,256]{1,2,0:T(8,128)S(1)} %fusion.7, f32[2,256,256]{1,2,0:T(8,128)S(1)} %convolution_bitcast_fusion.3, f32[2,256,256]{1,2,0:T(8,128)S(1)} %convolution_bitcast_fusion.4, f32[2,256,256]{2,1,0:T(8,128)S(1)} %bitcast_add_fusion, f32[2,256,256]{2,1,0:T(8,128)S(1)} %get-tuple-element.38, ...), kind=kOutput, calls=%fused_computation.6 | convolution fusion | flops 403177472 | bytes 3670016 | tf_op jit(solution)/shard_map/dot_general | solution.py:28
  32.6 0.8 fusion.14
  34.1 1.5 %subtract_subtract_fusion = (f32[2,256,256]{2,1,0:T(8,128)}, f32[2,256,256]{2,1,0:T(8,128)S(1)}) fusion(f32[2,256,256]{2,1,0:T(8,128)S(1)} %fusion.127, f32[2,256,256]{2,1,0:T(8,128)S(1)} %get-tuple-element.45, f32[2,256,256]{1,2,0:T(8,128)S(1)} %get-tuple-element.49), kind=kOutput, calls=%fused_computation.65 | convolution fusion | flops 403046400 | bytes 2621440 | tf_op jit(solution)/shard_map/dot_general | solution.py:26
  35.7 1.6 %fusion.1.imag_ref = f32[2,256,256]{2,1,0:T(8,128)} fusion(f32[2,256,256]{2,1,0:T(8,128)S(1)} %fusion.127, f32[2,256,256]{2,1,0:T(8,128)S(1)} %get-tuple-element.52, f32[2,256,256]{1,2,0:T(8,128)S(1)} %get-tuple-element.49, f32[2,256,256]{1,2,0:T(8,128)S(1)} %fusion.14, f32[2,256,256]{2,1,0:T(8,128)S(1)} %get-tuple-element.45, f32[2,256,256]{2,1,0:T(8,128)S(1)} %fusion.9), kind=kOutput, calls=%fused_computation.3 | convolution fusion | flops 403439616 | bytes 3670016 | tf_op jit(solution)/shard_map/dot_general | solution.py:28
  37.3 6.8 %shard_map.86 = f32[16,2,8,512]{3,2,1,0:T(8,128)} custom-call(s32[128]{0:T(128)} %and_select_fusion.partner_ref, f32[2,256,256]{2,1,0:T(8,128)} %get-tuple-element.51.real_ref, f32[2,256,256]{2,1,0:T(8,128)} %fusion.1.imag_ref), custom_call_target="tpu_custom_call" | custom-call | tf_op jit(solution)/shard_map/pallas_call | solution.py:188
  44.0 6.0 %all-to-all-start = ((f32[16,2,8,512]{3,2,1,0:T(8,128)}), f32[16,2,8,512]{3,2,1,0:T(8,128)S(1)}, u32[]{:S(2)}, u32[]{:S(2)}) async-start(f32[16,2,8,512]{3,2,1,0:T(8,128)} %shard_map.86), calls=%async_computation | async-start | bytes 1048576 | tf_op jit(solution)/shard_map/all_to_all | solution.py:219
  51.3 13.2 %all-to-all-done = f32[16,2,8,512]{3,2,1,0:T(8,128)S(1)} async-done(((f32[16,2,8,512]{3,2,1,0:T(8,128)}), f32[16,2,8,512]{3,2,1,0:T(8,128)S(1)}, u32[]{:S(2)}, u32[]{:S(2)}) %all-to-all-start) | async-done | bytes 524320 | tf_op jit(solution)/shard_map/all_to_all | solution.py:219
  64.5 1.5 %convolution_bitcast_fusion = f32[4,4,2,8,512]{4,0,2,1,3:T(4,128)S(1)} fusion(f32[4,4,2,8,512,1,1]{4,3,2,1,0,6,5:T(8,128)S(1)} %bitcast.202, f32[4,4,4,2,4,2]{1,5,4,3,2,0:T(2,128)S(1)} %bitcast.203), kind=kOutput, calls=%fused_computation | convolution fusion | flops 50331648 | bytes 1052672 | tf_op jit(solution)/shard_map/kjabcd,cjdpx->akbpx/dot_general | solution.py:224
  66.0 1.1 %copy.143 = f32[4,4,2,8,512]{4,3,2,1,0:T(8,128)} copy(f32[4,4,2,8,512]{4,0,2,1,3:T(4,128)S(1)} %convolution_bitcast_fusion) | data formatting | bytes 1048576 | tf_op jit(solution)/shard_map/kjabcd,cjdpx->akbpx/transpose | solution.py:224
  67.2 4.2 %all-to-all-start.1 = ((f32[16,2,8,512]{3,2,1,0:T(8,128)}), f32[16,2,8,512]{3,2,1,0:T(8,128)S(1)}, u32[]{:S(2)}, u32[]{:S(2)}) async-start(f32[16,2,8,512]{3,2,1,0:T(8,128)} %bitcast.40), calls=%async_computation.1 | async-start | bytes 1048576 | tf_op jit(solution)/shard_map/all_to_all | solution.py:226
  71.5 1.0 %copy.145 = f32[2,1,1,2,256,256]{5,4,3,2,1,0:T(8,128)} copy(f32[2,1,1,2,256,256]{5,4,0,3,2,1:T(8,128)S(1)} %maximum_bitcast_fusion) | data formatting | bytes 2097152
  72.6 13.3 %all-to-all-done.1 = f32[16,2,8,512]{3,2,1,0:T(8,128)S(1)} async-done(((f32[16,2,8,512]{3,2,1,0:T(8,128)}), f32[16,2,8,512]{3,2,1,0:T(8,128)S(1)}, u32[]{:S(2)}, u32[]{:S(2)}) %all-to-all-start.1) | async-done | bytes 524320 | tf_op jit(solution)/shard_map/all_to_all | solution.py:226
  85.9 0.8 copy_bitcast_fusion
  (55 shorter events, 16.3 us)
Async XLA Ops:
  0.6 49.5 %copy-start = (f32[2,8,4]{1,2,0:T(4,128)S(1)}, f32[2,8,4]{1,2,0:T(4,128)}, u32[]{:S(2)}) copy-start(f32[2,8,4]{1,2,0:T(4,128)} %param.16) | copy-start | bytes 772
  0.6 2.0 %copy-start.1 = (f32[2,1,1,2,256,256]{5,4,3,2,1,0:T(8,128)S(1)}, f32[2,1,1,2,256,256]{5,4,3,2,1,0:T(8,128)}, u32[]{:S(2)}) copy-start(f32[2,1,1,2,256,256]{5,4,3,2,1,0:T(8,128)} %param.11) | copy-start | bytes 3145732
  4.3 1.2 %copy-start.2 = (f32[2,1,1,2,256,256]{5,4,3,2,1,0:T(8,128)S(1)}, f32[2,1,1,2,256,256]{5,4,3,2,1,0:T(8,128)}, u32[]{:S(2)}) copy-start(f32[2,1,1,2,256,256]{5,4,3,2,1,0:T(8,128)} %param.12) | copy-start | bytes 3145732
  11.4 11.5 %collective-permute-start = (f32[2,128,128]{2,1,0:T(8,128)S(1)}, f32[2,128,128]{2,1,0:T(8,128)S(1)}, u32[]{:S(2)}, u32[]{:S(2)}) collective-permute-start(f32[2,128,128]{2,1,0:T(8,128)S(1)} %get-tuple-element.40), channel_id=1, source_target_pairs={{0,1},{2,3},{4,5},{6,7},{8,9},{10,11},{12,13},{14,15},{16,17},{18,... | collective-permute-start | bytes 393224 | tf_op jit(solution)/shard_map/ppermute | solution.py:20
  16.7 6.5 %collective-permute-start.1 = (f32[2,128,128]{2,1,0:T(8,128)S(1)}, f32[2,128,128]{2,1,0:T(8,128)S(1)}, u32[]{:S(2)}, u32[]{:S(2)}) collective-permute-start(f32[2,128,128]{2,1,0:T(8,128)S(1)} %fusion.18), channel_id=1, source_target_pairs={{0,1},{2,3},{4,5},{6,7},{8,9},{10,11},{12,13},{14,15},{16,17},{18,... | collective-permute-start | bytes 393224 | tf_op jit(solution)/shard_map/ppermute | solution.py:20
  21.6 0.7 copy-start.8
  21.6 1.2 %copy-start.5 = (f32[1,1,2,128,128]{4,3,2,1,0:T(8,128)S(1)}, f32[1,1,2,128,128]{4,3,2,1,0:T(8,128)}, u32[]{:S(2)}) copy-start(f32[1,1,2,128,128]{4,3,2,1,0:T(8,128)} %param.13) | copy-start | bytes 393220
  44.0 6.0 %copy-start.7 = (s32[8]{0:T(128)S(1)}, s32[8]{0:T(128)}, u32[]{:S(2)}) copy-start(s32[8]{0:T(128)} %param.15) | copy-start | bytes 100
  44.0 20.5 %all-to-all-start = ((f32[16,2,8,512]{3,2,1,0:T(8,128)}), f32[16,2,8,512]{3,2,1,0:T(8,128)S(1)}, u32[]{:S(2)}, u32[]{:S(2)}) async-start(f32[16,2,8,512]{3,2,1,0:T(8,128)} %shard_map.86), calls=%async_computation | async-start | bytes 1048576 | tf_op jit(solution)/shard_map/all_to_all | solution.py:219
  50.1 0.7 copy-start.6
  67.2 4.2 %copy-start.3 = (f32[2,256,256]{2,1,0:T(8,128)S(1)}, f32[2,256,256]{2,1,0:T(8,128)}, u32[]{:S(2)}) copy-start(f32[2,256,256]{2,1,0:T(8,128)} %get-tuple-element.51.real_ref) | copy-start | bytes 1572868
  67.2 4.2 %copy-start.4 = (f32[2,256,256]{2,1,0:T(8,128)S(1)}, f32[2,256,256]{2,1,0:T(8,128)}, u32[]{:S(2)}) copy-start(f32[2,256,256]{2,1,0:T(8,128)} %fusion.1.imag_ref) | copy-start | bytes 1572868
  67.2 18.7 %all-to-all-start.1 = ((f32[16,2,8,512]{3,2,1,0:T(8,128)}), f32[16,2,8,512]{3,2,1,0:T(8,128)S(1)}, u32[]{:S(2)}, u32[]{:S(2)}) async-start(f32[16,2,8,512]{3,2,1,0:T(8,128)} %bitcast.40), calls=%async_computation.1 | async-start | bytes 1048576 | tf_op jit(solution)/shard_map/all_to_all | solution.py:226

commit v9 on v8

--- a/solution.py
+++ b/solution.py
@@ -216,15 +216,20 @@
     mixing = phonon_matrix(
         phonon_shift, phonon_strength, momentum_table, energy_count * energy_groups
     )
-    by_pairs = lax.all_to_all(picked, axes, 0, 0, tiled=True)
-    arranged = by_pairs.reshape(energy_groups, momenta, energy_count, pair_count // group, width)
+    momentum_count = lax.axis_size("momentum")
+    chunk = pair_count // group
+    staged = picked.reshape(energy_groups, momentum_count, energy_count, chunk, width)
+    staged = lax.all_to_all(staged, "momentum", 1, 1, tiled=True)
+    arranged = lax.all_to_all(staged, "energy", 0, 0, tiled=True)
+    arranged = arranged.reshape(energy_groups, momenta, energy_count, chunk, width)
     mixing_grid = mixing.reshape(
         momenta, momenta, energy_groups, energy_count, energy_groups, energy_count
     )
     summed = jnp.einsum("kjabcd,cjdpx->akbpx", mixing_grid, arranged, precision=HIGHEST)
-    summed = summed.reshape(group, energy_count, pair_count // group, width)
-    self_energy = lax.all_to_all(summed, axes, 0, 2, tiled=True)
-    self_energy = self_energy.reshape(energy_count, 1, 1, pair_count, width)
+    summed = summed.reshape(energy_groups, momentum_count, energy_count, chunk, width)
+    summed = lax.all_to_all(summed, "momentum", 1, 1, tiled=True)
+    summed = lax.all_to_all(summed, "energy", 0, 0, tiled=True)
+    self_energy = summed.transpose(2, 0, 1, 3, 4).reshape(energy_count, 1, 1, pair_count, width)
     return (green_block[:, None, None], self_energy)
 
 

time: 87.2 us -> 110 us (1.26)
  blocking collectives: 0 us -> 22.7 us
  local copies, waits for them, and re-layouts: 4.91 us -> 7.77 us
  starting transfers between devices: 16.6 us -> 15 us
    all_to_all x0 -> x2, blocking collectives: none -> 22.7 us  [the longest x1 11.4 us: body(): staged = lax.all_to_all(staged, 'momentum', 1, 1, tiled=True)]
    all_to_all x0 -> x3, local copies, waits for them, and re-layouts: none -> 3.33 us  [the longest x1 1.15 us: body(): staged = lax.all_to_all(staged, 'momentum', 1, 1, tiled=True)]
    all_to_all x2, starting transfers between devices: 10.3 us -> 8.61 us  [the longest x1 5.01 us: body(): arranged = lax.all_to_all(staged, 'energy', 0, 0, tiled=True)]
    reshape x0 -> x1, local copies, waits for them, and re-layouts: none -> 1.45 us  [body(): picked.reshape(energy_groups, momentum_count, energy_count, chunk, width)]
    unnamed x20 -> x19, local copies, waits for them, and re-layouts: 3.72 us -> 2.89 us
  transfers between devices with their start and end apart: 4 -> 4, of which waited for: 2 -> 2; matrix products, arithmetic and copies ran while one was open for 8% -> 6% of each run, Pallas kernels for 0% -> 0%
where the time goes in v9:
time: 110 us
  matrix products  29.7 us (27%)
  waiting for transfers between devices  26.1 us (24%)
  blocking collectives  22.7 us (21%)
  starting transfers between devices  15 us (14%)
  local copies, waits for them, and re-layouts  7.77 us (7%)
  Pallas kernels  6.76 us (6%)
    all_to_all x1, waiting for transfers between devices, body(): summed = lax.all_to_all(summed, 'energy', 0, 0, tiled=True)  13.2 us
    all_to_all x1, waiting for transfers between devices, body(): arranged = lax.all_to_all(staged, 'energy', 0, 0, tiled=True)  12.9 us
    all_to_all x1, blocking collectives, body(): staged = lax.all_to_all(staged, 'momentum', 1, 1, tiled=True)  11.4 us
    all_to_all x1, blocking collectives, body(): summed = lax.all_to_all(summed, 'momentum', 1, 1, tiled=True)  11.2 us
    dot_general x13, matrix products, complex_product(): real_real = jnp.matmul(first_real, second_real, precision=precision)  10.1 us
    dot_general x13, matrix products, complex_product(): imag_imag = jnp.matmul(first_imag, second_imag, precision=precision)  9.03 us
    dot_general x13, matrix products, complex_product(): jnp.matmul(first_real + first_imag, second_real + second_imag, precision=...  9.01 us
    pallas_call x1, Pallas kernels, pick_tiles(): pl.pallas_call(pick_kernel, out_shape=jax.ShapeDtypeStruct(shape, jnp.flo...  6.76 us
  transfers between devices with their start and end apart: 4, of which 2 were waited for; matrix products, arithmetic and copies ran while one was open for 6% of the time, Pallas kernels for 0%

profile of v9, /device:TPU:0, one launch (start us, length us, event | category | flops | bytes accessed | tf_op | source)
XLA Modules:
  0.0 109.9 jit_solution(9153190251109261655)
XLA Ops:
  0.7 1.9 %fusion.26 = f32[2,256,256]{2,1,0:T(8,128)S(1)} fusion(f32[2,1,1,2,256,256]{5,4,3,2,1,0:T(8,128)} %param.11, f32[2,1,1,2,256,256]{5,4,3,2,1,0:T(8,128)} %param.12), kind=kOutput, calls=%fused_computation.53 | convolution fusion | flops 402653184 | bytes 1572864 | tf_op jit(solution)/shard_map/dot_general | solution.py:27
  2.6 1.7 %fusion.32 = f32[2,256,256]{2,1,0:T(8,128)S(1)} fusion(f32[2,1,1,2,256,256]{5,4,3,2,1,0:T(8,128)S(1)} %copy-done.1, f32[2,1,1,2,256,256]{5,4,3,2,1,0:T(8,128)} %param.12), kind=kOutput, calls=%fused_computation.59 | convolution fusion | flops 402653184 | bytes 1572864 | tf_op jit(solution)/shard_map/dot_general | solution.py:26
  4.4 1.1 %copy-done.2 = f32[2,1,1,2,256,256]{5,4,3,2,1,0:T(8,128)S(1)} copy-done((f32[2,1,1,2,256,256]{5,4,3,2,1,0:T(8,128)S(1)}, f32[2,1,1,2,256,256]{5,4,3,2,1,0:T(8,128)}, u32[]{:S(2)}) %copy-start.2) | copy-done | bytes 1048600
  11.5 4.9 %collective-permute-start = (f32[2,128,128]{2,1,0:T(8,128)S(1)}, f32[2,128,128]{2,1,0:T(8,128)S(1)}, u32[]{:S(2)}, u32[]{:S(2)}) collective-permute-start(f32[2,128,128]{2,1,0:T(8,128)S(1)} %get-tuple-element.40), channel_id=1, source_target_pairs={{0,1},{2,3},{4,5},{6,7},{8,9},{10,11},{12,13},{14,15},{16,17},{18,... | collective-permute-start | bytes 393224 | tf_op jit(solution)/shard_map/ppermute | solution.py:20
  16.9 1.5 %collective-permute-start.1 = (f32[2,128,128]{2,1,0:T(8,128)S(1)}, f32[2,128,128]{2,1,0:T(8,128)S(1)}, u32[]{:S(2)}, u32[]{:S(2)}) collective-permute-start(f32[2,128,128]{2,1,0:T(8,128)S(1)} %fusion.18), channel_id=1, source_target_pairs={{0,1},{2,3},{4,5},{6,7},{8,9},{10,11},{12,13},{14,15},{16,17},{18,... | collective-permute-start | bytes 393224 | tf_op jit(solution)/shard_map/ppermute | solution.py:20
  18.4 1.1 convolution_bitcast_fusion.4
  19.5 1.1 convolution_bitcast_fusion.3
  30.5 1.1 %fusion.3 = f32[2,256,256]{1,2,0:T(8,128)S(1)} fusion(f32[2,256,256]{1,2,0:T(8,128)S(1)} %fusion.7, f32[2,256,256]{1,2,0:T(8,128)S(1)} %convolution_bitcast_fusion.3, f32[2,256,256]{1,2,0:T(8,128)S(1)} %convolution_bitcast_fusion.4, f32[2,256,256]{2,1,0:T(8,128)S(1)} %bitcast_add_fusion, f32[2,256,256]{2,1,0:T(8,128)S(1)} %get-tuple-element.38, ...), kind=kOutput, calls=%fused_computation.6 | convolution fusion | flops 403177472 | bytes 3670016 | tf_op jit(solution)/shard_map/dot_general | solution.py:28
  32.2 0.8 fusion.47
  34.3 1.5 %subtract_subtract_fusion = (f32[2,256,256]{2,1,0:T(8,128)}, f32[2,256,256]{2,1,0:T(8,128)S(1)}) fusion(f32[2,256,256]{2,1,0:T(8,128)S(1)} %fusion.127, f32[2,256,256]{2,1,0:T(8,128)S(1)} %get-tuple-element.45, f32[2,256,256]{1,2,0:T(8,128)S(1)} %get-tuple-element.49), kind=kOutput, calls=%fused_computation.64 | convolution fusion | flops 403046400 | bytes 2621440 | tf_op jit(solution)/shard_map/dot_general | solution.py:26
  35.8 1.6 %fusion.1.imag_ref = f32[2,256,256]{2,1,0:T(8,128)} fusion(f32[2,256,256]{2,1,0:T(8,128)S(1)} %fusion.127, f32[2,256,256]{2,1,0:T(8,128)S(1)} %get-tuple-element.52, f32[2,256,256]{1,2,0:T(8,128)S(1)} %get-tuple-element.49, f32[2,256,256]{1,2,0:T(8,128)S(1)} %fusion.14, f32[2,256,256]{2,1,0:T(8,128)S(1)} %get-tuple-element.45, f32[2,256,256]{2,1,0:T(8,128)S(1)} %fusion.9), kind=kOutput, calls=%fused_computation.3 | convolution fusion | flops 403439616 | bytes 3670016 | tf_op jit(solution)/shard_map/dot_general | solution.py:28
  37.4 6.8 %shard_map.86 = f32[16,2,8,512]{3,2,1,0:T(8,128)} custom-call(s32[128]{0:T(128)} %and_select_fusion.partner_ref, f32[2,256,256]{2,1,0:T(8,128)} %get-tuple-element.51.real_ref, f32[2,256,256]{2,1,0:T(8,128)} %fusion.1.imag_ref), custom_call_target="tpu_custom_call" | custom-call | tf_op jit(solution)/shard_map/pallas_call | solution.py:188
  44.2 1.4 %copy.141 = f32[4,4,2,8,512]{4,2,0,3,1:T(2,128)S(1)} copy(f32[4,4,2,8,512]{4,3,2,1,0:T(8,128)} %bitcast.199) | data formatting | bytes 1048576 | tf_op jit(solution)/shard_map/reshape | solution.py:221
  45.6 11.4 %all_to_all.20 = f32[4,4,2,8,512]{4,2,0,3,1:T(2,128)S(1)} all-to-all(f32[4,4,2,8,512]{4,2,0,3,1:T(2,128)S(1)} %copy.141), channel_id=1, replica_groups=mesh['energy'=4,'momentum'=4,'space'=2] {'momentum'}, dimensions={1} | all-to-all | bytes 1048576 | tf_op jit(solution)/shard_map/all_to_all | solution.py:222
  57.0 1.1 %copy.142 = f32[4,4,2,8,512]{4,1,2,3,0:T(4,128)} copy(f32[4,4,2,8,512]{4,2,0,3,1:T(2,128)S(1)} %all_to_all.20) | data formatting | bytes 1048576 | tf_op jit(solution)/shard_map/all_to_all | solution.py:222
  58.2 5.0 %all-to-all-start.1 = ((f32[4,4,2,8,512]{4,1,2,3,0:T(4,128)}), f32[4,4,2,8,512]{4,1,2,3,0:T(4,128)S(1)}, u32[]{:S(2)}, u32[]{:S(2)}) async-start(f32[4,4,2,8,512]{4,1,2,3,0:T(4,128)} %copy.142), calls=%async_computation.1 | async-start | bytes 1048576 | tf_op jit(solution)/shard_map/all_to_all | solution.py:223
  64.4 12.9 %all-to-all-done.1 = f32[4,4,2,8,512]{4,1,2,3,0:T(4,128)S(1)} async-done(((f32[4,4,2,8,512]{4,1,2,3,0:T(4,128)}), f32[4,4,2,8,512]{4,1,2,3,0:T(4,128)S(1)}, u32[]{:S(2)}, u32[]{:S(2)}) %all-to-all-start.1) | async-done | bytes 524320 | tf_op jit(solution)/shard_map/all_to_all | solution.py:223
  77.3 1.1 %convolution_bitcast_fusion = f32[4,4,2,8,512]{4,0,2,1,3:T(4,128)S(1)} fusion(f32[4,4,4,2,4,2]{1,5,4,3,2,0:T(2,128)S(1)} %bitcast.201, f32[4,4,2,8,512]{4,1,2,3,0:T(4,128)S(1)} %all-to-all-done.1), kind=kOutput, calls=%fused_computation | convolution fusion | flops 50331648 | bytes 1052672 | tf_op jit(solution)/shard_map/kjabcd,cjdpx->akbpx/dot_general | solution.py:228
  78.5 11.2 %all_to_all.21 = f32[4,4,2,8,512]{4,0,2,3,1:T(4,128)S(1)} all-to-all(f32[4,4,2,8,512]{4,0,2,3,1:T(4,128)S(1)} %copy.146), channel_id=1, replica_groups=mesh['energy'=4,'momentum'=4,'space'=2] {'momentum'}, dimensions={1} | all-to-all | bytes 1048576 | tf_op jit(solution)/shard_map/all_to_all | solution.py:230
  89.7 1.1 copy.147
  90.8 3.6 %all-to-all-start.3 = ((f32[4,4,2,8,512]{4,2,1,3,0:T(2,128)}), f32[4,4,2,8,512]{4,2,1,3,0:T(2,128)S(1)}, u32[]{:S(2)}, u32[]{:S(2)}) async-start(f32[4,4,2,8,512]{4,2,1,3,0:T(2,128)} %copy.147), calls=%async_computation.3 | async-start | bytes 1048576 | tf_op jit(solution)/shard_map/all_to_all | solution.py:231
  94.5 1.0 copy.149
  95.6 13.2 %all-to-all-done.3 = f32[4,4,2,8,512]{4,2,1,3,0:T(2,128)S(1)} async-done(((f32[4,4,2,8,512]{4,2,1,3,0:T(2,128)}), f32[4,4,2,8,512]{4,2,1,3,0:T(2,128)S(1)}, u32[]{:S(2)}, u32[]{:S(2)}) %all-to-all-start.3) | async-done | bytes 524320 | tf_op jit(solution)/shard_map/all_to_all | solution.py:231
  108.8 1.1 %copy.148 = f32[4,4,2,8,512]{4,3,1,0,2:T(8,128)} copy(f32[4,4,2,8,512]{4,2,1,3,0:T(2,128)S(1)} %all-to-all-done.3) | data formatting | bytes 1048576 | tf_op jit(solution)/shard_map/all_to_all | solution.py:231
  (60 shorter events, 19.4 us)
Async XLA Ops:
  0.6 62.6 %copy-start = (f32[2,8,4]{1,2,0:T(4,128)S(1)}, f32[2,8,4]{1,2,0:T(4,128)}, u32[]{:S(2)}) copy-start(f32[2,8,4]{1,2,0:T(4,128)} %param.16) | copy-start | bytes 772
  0.6 2.0 %copy-start.1 = (f32[2,1,1,2,256,256]{5,4,3,2,1,0:T(8,128)S(1)}, f32[2,1,1,2,256,256]{5,4,3,2,1,0:T(8,128)}, u32[]{:S(2)}) copy-start(f32[2,1,1,2,256,256]{5,4,3,2,1,0:T(8,128)} %param.11) | copy-start | bytes 3145732
  4.3 1.2 %copy-start.2 = (f32[2,1,1,2,256,256]{5,4,3,2,1,0:T(8,128)S(1)}, f32[2,1,1,2,256,256]{5,4,3,2,1,0:T(8,128)}, u32[]{:S(2)}) copy-start(f32[2,1,1,2,256,256]{5,4,3,2,1,0:T(8,128)} %param.12) | copy-start | bytes 3145732
  11.5 11.5 %collective-permute-start = (f32[2,128,128]{2,1,0:T(8,128)S(1)}, f32[2,128,128]{2,1,0:T(8,128)S(1)}, u32[]{:S(2)}, u32[]{:S(2)}) collective-permute-start(f32[2,128,128]{2,1,0:T(8,128)S(1)} %get-tuple-element.40), channel_id=1, source_target_pairs={{0,1},{2,3},{4,5},{6,7},{8,9},{10,11},{12,13},{14,15},{16,17},{18,... | collective-permute-start | bytes 393224 | tf_op jit(solution)/shard_map/ppermute | solution.py:20
  16.9 6.6 %collective-permute-start.1 = (f32[2,128,128]{2,1,0:T(8,128)S(1)}, f32[2,128,128]{2,1,0:T(8,128)S(1)}, u32[]{:S(2)}, u32[]{:S(2)}) collective-permute-start(f32[2,128,128]{2,1,0:T(8,128)S(1)} %fusion.18), channel_id=1, source_target_pairs={{0,1},{2,3},{4,5},{6,7},{8,9},{10,11},{12,13},{14,15},{16,17},{18,... | collective-permute-start | bytes 393224 | tf_op jit(solution)/shard_map/ppermute | solution.py:20
  21.8 0.7 copy-start.8
  21.8 1.2 %copy-start.5 = (f32[1,1,2,128,128]{4,3,2,1,0:T(8,128)S(1)}, f32[1,1,2,128,128]{4,3,2,1,0:T(8,128)}, u32[]{:S(2)}) copy-start(f32[1,1,2,128,128]{4,3,2,1,0:T(8,128)} %param.13) | copy-start | bytes 393220
  58.2 5.0 %copy-start.7 = (s32[8]{0:T(128)S(1)}, s32[8]{0:T(128)}, u32[]{:S(2)}) copy-start(s32[8]{0:T(128)} %param.15) | copy-start | bytes 100
  58.2 19.1 %all-to-all-start.1 = ((f32[4,4,2,8,512]{4,1,2,3,0:T(4,128)}), f32[4,4,2,8,512]{4,1,2,3,0:T(4,128)S(1)}, u32[]{:S(2)}, u32[]{:S(2)}) async-start(f32[4,4,2,8,512]{4,1,2,3,0:T(4,128)} %copy.142), calls=%async_computation.1 | async-start | bytes 1048576 | tf_op jit(solution)/shard_map/all_to_all | solution.py:223
  63.2 0.7 copy-start.6
  90.8 3.6 %copy-start.3 = (f32[2,256,256]{2,1,0:T(8,128)S(1)}, f32[2,256,256]{2,1,0:T(8,128)}, u32[]{:S(2)}) copy-start(f32[2,256,256]{2,1,0:T(8,128)} %get-tuple-element.51.real_ref) | copy-start | bytes 1572868
  90.8 3.6 %copy-start.4 = (f32[2,256,256]{2,1,0:T(8,128)S(1)}, f32[2,256,256]{2,1,0:T(8,128)}, u32[]{:S(2)}) copy-start(f32[2,256,256]{2,1,0:T(8,128)} %fusion.1.imag_ref) | copy-start | bytes 1572868
  90.8 18.0 %all-to-all-start.3 = ((f32[4,4,2,8,512]{4,2,1,3,0:T(2,128)}), f32[4,4,2,8,512]{4,2,1,3,0:T(2,128)S(1)}, u32[]{:S(2)}, u32[]{:S(2)}) async-start(f32[4,4,2,8,512]{4,2,1,3,0:T(2,128)} %copy.147), calls=%async_computation.3 | async-start | bytes 1048576 | tf_op jit(solution)/shard_map/all_to_all | solution.py:231

commit v10 on v8

--- a/solution.py
+++ b/solution.py
@@ -18,6 +18,11 @@
     count = lax.axis_size(axis)
     pairs = [(i, i + by) for i in range(count) if 0 <= i + by < count]
     return lax.ppermute(shard, axis, pairs)
+
+
+def pass_boundary(boundary):
+    moved = from_behind(jnp.stack(boundary, axis=0), "space", 1)
+    return (moved[0], moved[1])
 
 
 def complex_product(first_factor, second_factor, precision=HIGHEST):
@@ -77,7 +82,7 @@
     applied_left = newton_product(blocks, left)
 
     for section in range(1, space_count - 1):
-        incoming = from_behind(boundary, "space", 1)
+        incoming = pass_boundary(boundary)
         schur = schur_of(incoming)
         mixed = first_step_product(schur, right)
         mixed_trail = part(mixed, cols=trail)
@@ -91,7 +96,7 @@
 
     applied = newton_product(blocks, first)
     if space_count > 1:
-        incoming = from_behind(boundary, "space", 1)
+        incoming = pass_boundary(boundary)
         schur = schur_of(incoming)
         mixed = first_step_product(schur, right)
         step = add(first, newton_product(left, mixed))

time: 87.2 us -> 86.6 us (level)
  starting transfers between devices: 16.6 us -> 15.3 us
    ppermute x2 -> x1, starting transfers between devices: 6.36 us -> 5.07 us  [from_behind(): return lax.ppermute(shard, axis, pairs)]
  transfers between devices with their start and end apart: 4 -> 3, of which waited for: 2 -> 3; matrix products, arithmetic and copies ran while one was open for 8% -> 7% of each run, Pallas kernels for 0% -> 0%
where the time goes in v10:
time: 86.6 us; the launch traced here: 86.1 us
  matrix products  29.9 us (35%)
  waiting for transfers between devices  27.2 us (31%)
  starting transfers between devices  15.3 us (18%)
  Pallas kernels  6.76 us (8%)
  local copies, waits for them, and re-layouts  4.93 us (6%)
  between operations  1.08 us (1%)
  other arithmetic  0.88 us (1%)
    all_to_all x1, waiting for transfers between devices, body(): self_energy = lax.all_to_all(summed, axes, 0, 2, tiled=True)  13.3 us
    all_to_all x1, waiting for transfers between devices, body(): by_pairs = lax.all_to_all(picked, axes, 0, 0, tiled=True)  13.2 us
    dot_general x13, matrix products, complex_product(): real_real = jnp.matmul(first_real, second_real, precision=precision)  9.8 us
    dot_general x13, matrix products, complex_product(): jnp.matmul(first_real + first_imag, second_real + second_imag, precision=...  9.2 us
    dot_general x13, matrix products, complex_product(): imag_imag = jnp.matmul(first_imag, second_imag, precision=precision)  8.96 us
    pallas_call x1, Pallas kernels, pick_tiles(): pl.pallas_call(pick_kernel, out_shape=jax.ShapeDtypeStruct(shape, jnp.flo...  6.76 us
    all_to_all x1, starting transfers between devices, body(): by_pairs = lax.all_to_all(picked, axes, 0, 0, tiled=True)  6.04 us
    ppermute x1, starting transfers between devices, from_behind(): return lax.ppermute(shard, axis, pairs)  5.07 us
  transfers between devices with their start and end apart: 3, of which 3 were waited for; matrix products, arithmetic and copies ran while one was open for 7% of the time, Pallas kernels for 0%

profile of v10, /device:TPU:0, one launch (start us, length us, event | category | flops | bytes accessed | tf_op | source)
XLA Modules:
  0.0 86.1 jit_solution(7827609206674498557)
XLA Ops:
  0.7 1.9 %fusion.27 = f32[2,256,256]{2,1,0:T(8,128)S(1)} fusion(f32[2,1,1,2,256,256]{5,4,3,2,1,0:T(8,128)} %param.11, f32[2,1,1,2,256,256]{5,4,3,2,1,0:T(8,128)} %param.12), kind=kOutput, calls=%fused_computation.54 | convolution fusion | flops 402653184 | bytes 1572864 | tf_op jit(solution)/shard_map/dot_general | solution.py:32
  2.6 1.7 %fusion.33 = f32[2,256,256]{2,1,0:T(8,128)S(1)} fusion(f32[2,1,1,2,256,256]{5,4,3,2,1,0:T(8,128)S(1)} %copy-done.1, f32[2,1,1,2,256,256]{5,4,3,2,1,0:T(8,128)} %param.12), kind=kOutput, calls=%fused_computation.60 | convolution fusion | flops 402653184 | bytes 1572864 | tf_op jit(solution)/shard_map/dot_general | solution.py:31
  4.4 1.1 %copy-done.2 = f32[2,1,1,2,256,256]{5,4,3,2,1,0:T(8,128)S(1)} copy-done((f32[2,1,1,2,256,256]{5,4,3,2,1,0:T(8,128)S(1)}, f32[2,1,1,2,256,256]{5,4,3,2,1,0:T(8,128)}, u32[]{:S(2)}) %copy-start.2) | copy-done | bytes 1048600
  7.6 0.8 fusion.5
  8.4 0.7 convolution_bitcast_fusion.7
  9.1 0.7 convolution_bitcast_fusion.8
  9.9 0.7 fusion.15
  11.9 5.1 %collective-permute-start = (f32[2,2,128,128]{3,2,1,0:T(8,128)S(1)}, f32[2,2,128,128]{3,2,1,0:T(8,128)S(1)}, u32[]{:S(2)}, u32[]{:S(2)}) collective-permute-start(f32[2,2,128,128]{3,2,1,0:T(8,128)S(1)} %pad_maximum_fusion), channel_id=1, source_target_pairs={{0,1},{2,3},{4,5},{6,7},{8,9},{10,11},{12,13},{14,15},{16,17},{18,... | collective-permute-start | bytes 786440 | tf_op jit(solution)/shard_map/ppermute | solution.py:20
  17.1 1.0 %convolution_bitcast_fusion.4 = f32[2,256,256]{1,2,0:T(8,128)S(1)} fusion(f32[2,256,256]{2,1,0:T(8,128)S(1)} %get-tuple-element.38, f32[2,1,1,2,256,256]{5,4,3,2,1,0:T(8,128)S(1)} %copy-done.1), kind=kOutput, calls=%fused_computation.20 | convolution fusion | flops 402653184 | bytes 1572864 | tf_op jit(solution)/shard_map/dot_general | solution.py:31
  20.6 1.0 %convolution_bitcast_fusion.3 = f32[2,256,256]{1,2,0:T(8,128)S(1)} fusion(f32[2,256,256]{2,1,0:T(8,128)S(1)} %fusion.5, f32[2,1,1,2,256,256]{5,4,3,2,1,0:T(8,128)S(1)} %copy-done.1), kind=kOutput, calls=%fused_computation.19 | convolution fusion | flops 402653184 | bytes 1572864 | tf_op jit(solution)/shard_map/dot_general | solution.py:32
  28.3 0.7 subtract_add_fusion
  29.7 1.1 %fusion.3 = f32[2,256,256]{1,2,0:T(8,128)S(1)} fusion(f32[2,256,256]{1,2,0:T(8,128)S(1)} %fusion.7, f32[2,256,256]{1,2,0:T(8,128)S(1)} %convolution_bitcast_fusion.3, f32[2,256,256]{1,2,0:T(8,128)S(1)} %convolution_bitcast_fusion.4, f32[2,256,256]{2,1,0:T(8,128)S(1)} %bitcast_add_fusion, f32[2,256,256]{2,1,0:T(8,128)S(1)} %get-tuple-element.38, ...), kind=kOutput, calls=%fused_computation.6 | convolution fusion | flops 403177472 | bytes 3670016 | tf_op jit(solution)/shard_map/dot_general | solution.py:33
  32.0 0.8 fusion.14
  33.6 1.5 %subtract_subtract_fusion = (f32[2,256,256]{2,1,0:T(8,128)}, f32[2,256,256]{2,1,0:T(8,128)S(1)}) fusion(f32[2,256,256]{2,1,0:T(8,128)S(1)} %fusion.129, f32[2,256,256]{2,1,0:T(8,128)S(1)} %get-tuple-element.43, f32[2,256,256]{1,2,0:T(8,128)S(1)} %get-tuple-element.47), kind=kOutput, calls=%fused_computation.66 | convolution fusion | flops 403046400 | bytes 2621440 | tf_op jit(solution)/shard_map/dot_general | solution.py:31
  35.1 1.6 %fusion.1.imag_ref = f32[2,256,256]{2,1,0:T(8,128)} fusion(f32[2,256,256]{2,1,0:T(8,128)S(1)} %fusion.129, f32[2,256,256]{2,1,0:T(8,128)S(1)} %get-tuple-element.50, f32[2,256,256]{1,2,0:T(8,128)S(1)} %get-tuple-element.47, f32[2,256,256]{1,2,0:T(8,128)S(1)} %fusion.14, f32[2,256,256]{2,1,0:T(8,128)S(1)} %get-tuple-element.43, f32[2,256,256]{2,1,0:T(8,128)S(1)} %fusion.9), kind=kOutput, calls=%fused_computation.3 | convolution fusion | flops 403439616 | bytes 3670016 | tf_op jit(solution)/shard_map/dot_general | solution.py:33
  36.7 6.8 %shard_map.86 = f32[16,2,8,512]{3,2,1,0:T(8,128)} custom-call(s32[128]{0:T(128)} %and_select_fusion.partner_ref, f32[2,256,256]{2,1,0:T(8,128)} %get-tuple-element.49.real_ref, f32[2,256,256]{2,1,0:T(8,128)} %fusion.1.imag_ref), custom_call_target="tpu_custom_call" | custom-call | tf_op jit(solution)/shard_map/pallas_call | solution.py:193
  43.4 6.0 %all-to-all-start = ((f32[16,2,8,512]{3,2,1,0:T(8,128)}), f32[16,2,8,512]{3,2,1,0:T(8,128)S(1)}, u32[]{:S(2)}, u32[]{:S(2)}) async-start(f32[16,2,8,512]{3,2,1,0:T(8,128)} %shard_map.86), calls=%async_computation | async-start | bytes 1048576 | tf_op jit(solution)/shard_map/all_to_all | solution.py:224
  50.7 13.2 %all-to-all-done = f32[16,2,8,512]{3,2,1,0:T(8,128)S(1)} async-done(((f32[16,2,8,512]{3,2,1,0:T(8,128)}), f32[16,2,8,512]{3,2,1,0:T(8,128)S(1)}, u32[]{:S(2)}, u32[]{:S(2)}) %all-to-all-start) | async-done | bytes 524320 | tf_op jit(solution)/shard_map/all_to_all | solution.py:224
  63.9 1.5 %convolution_bitcast_fusion = f32[4,4,2,8,512]{4,0,2,1,3:T(4,128)S(1)} fusion(f32[4,4,2,8,512,1,1]{4,3,2,1,0,6,5:T(8,128)S(1)} %bitcast.216, f32[4,4,4,2,4,2]{1,5,4,3,2,0:T(2,128)S(1)} %bitcast.217), kind=kOutput, calls=%fused_computation | convolution fusion | flops 50331648 | bytes 1052672 | tf_op jit(solution)/shard_map/kjabcd,cjdpx->akbpx/dot_general | solution.py:229
  65.5 1.1 %copy.143 = f32[4,4,2,8,512]{4,3,2,1,0:T(8,128)} copy(f32[4,4,2,8,512]{4,0,2,1,3:T(4,128)S(1)} %convolution_bitcast_fusion) | data formatting | bytes 1048576 | tf_op jit(solution)/shard_map/kjabcd,cjdpx->akbpx/transpose | solution.py:229
  66.6 4.2 %all-to-all-start.1 = ((f32[16,2,8,512]{3,2,1,0:T(8,128)}), f32[16,2,8,512]{3,2,1,0:T(8,128)S(1)}, u32[]{:S(2)}, u32[]{:S(2)}) async-start(f32[16,2,8,512]{3,2,1,0:T(8,128)} %bitcast.44), calls=%async_computation.1 | async-start | bytes 1048576 | tf_op jit(solution)/shard_map/all_to_all | solution.py:231
  70.9 1.0 %copy.145 = f32[2,1,1,2,256,256]{5,4,3,2,1,0:T(8,128)} copy(f32[2,1,1,2,256,256]{5,4,0,3,2,1:T(8,128)S(1)} %maximum_bitcast_fusion) | data formatting | bytes 2097152
  72.0 13.3 %all-to-all-done.1 = f32[16,2,8,512]{3,2,1,0:T(8,128)S(1)} async-done(((f32[16,2,8,512]{3,2,1,0:T(8,128)}), f32[16,2,8,512]{3,2,1,0:T(8,128)S(1)}, u32[]{:S(2)}, u32[]{:S(2)}) %all-to-all-start.1) | async-done | bytes 524320 | tf_op jit(solution)/shard_map/all_to_all | solution.py:231
  85.3 0.8 copy_bitcast_fusion
  (55 shorter events, 16.3 us)
Async XLA Ops:
  0.6 48.9 %copy-start = (f32[2,8,4]{1,2,0:T(4,128)S(1)}, f32[2,8,4]{1,2,0:T(4,128)}, u32[]{:S(2)}) copy-start(f32[2,8,4]{1,2,0:T(4,128)} %param.16) | copy-start | bytes 772
  0.6 2.0 %copy-start.1 = (f32[2,1,1,2,256,256]{5,4,3,2,1,0:T(8,128)S(1)}, f32[2,1,1,2,256,256]{5,4,3,2,1,0:T(8,128)}, u32[]{:S(2)}) copy-start(f32[2,1,1,2,256,256]{5,4,3,2,1,0:T(8,128)} %param.11) | copy-start | bytes 3145732
  4.3 1.2 %copy-start.2 = (f32[2,1,1,2,256,256]{5,4,3,2,1,0:T(8,128)S(1)}, f32[2,1,1,2,256,256]{5,4,3,2,1,0:T(8,128)}, u32[]{:S(2)}) copy-start(f32[2,1,1,2,256,256]{5,4,3,2,1,0:T(8,128)} %param.12) | copy-start | bytes 3145732
  11.9 10.4 %collective-permute-start = (f32[2,2,128,128]{3,2,1,0:T(8,128)S(1)}, f32[2,2,128,128]{3,2,1,0:T(8,128)S(1)}, u32[]{:S(2)}, u32[]{:S(2)}) collective-permute-start(f32[2,2,128,128]{3,2,1,0:T(8,128)S(1)} %pad_maximum_fusion), channel_id=1, source_target_pairs={{0,1},{2,3},{4,5},{6,7},{8,9},{10,11},{12,13},{14,15},{16,17},{18,... | collective-permute-start | bytes 786440 | tf_op jit(solution)/shard_map/ppermute | solution.py:20
  18.7 0.7 copy-start.8
  20.6 1.7 %copy-start.5 = (f32[1,1,2,128,128]{4,3,2,1,0:T(8,128)S(1)}, f32[1,1,2,128,128]{4,3,2,1,0:T(8,128)}, u32[]{:S(2)}) copy-start(f32[1,1,2,128,128]{4,3,2,1,0:T(8,128)} %param.13) | copy-start | bytes 393220
  43.4 6.1 %copy-start.7 = (s32[8]{0:T(128)S(1)}, s32[8]{0:T(128)}, u32[]{:S(2)}) copy-start(s32[8]{0:T(128)} %param.15) | copy-start | bytes 100
  43.4 20.5 %all-to-all-start = ((f32[16,2,8,512]{3,2,1,0:T(8,128)}), f32[16,2,8,512]{3,2,1,0:T(8,128)S(1)}, u32[]{:S(2)}, u32[]{:S(2)}) async-start(f32[16,2,8,512]{3,2,1,0:T(8,128)} %shard_map.86), calls=%async_computation | async-start | bytes 1048576 | tf_op jit(solution)/shard_map/all_to_all | solution.py:224
  49.5 0.7 copy-start.6
  66.6 4.2 %copy-start.3 = (f32[2,256,256]{2,1,0:T(8,128)S(1)}, f32[2,256,256]{2,1,0:T(8,128)}, u32[]{:S(2)}) copy-start(f32[2,256,256]{2,1,0:T(8,128)} %get-tuple-element.49.real_ref) | copy-start | bytes 1572868
  66.6 4.3 %copy-start.4 = (f32[2,256,256]{2,1,0:T(8,128)S(1)}, f32[2,256,256]{2,1,0:T(8,128)}, u32[]{:S(2)}) copy-start(f32[2,256,256]{2,1,0:T(8,128)} %fusion.1.imag_ref) | copy-start | bytes 1572868
  66.6 18.7 %all-to-all-start.1 = ((f32[16,2,8,512]{3,2,1,0:T(8,128)}), f32[16,2,8,512]{3,2,1,0:T(8,128)S(1)}, u32[]{:S(2)}, u32[]{:S(2)}) async-start(f32[16,2,8,512]{3,2,1,0:T(8,128)} %bitcast.44), calls=%async_computation.1 | async-start | bytes 1048576 | tf_op jit(solution)/shard_map/all_to_all | solution.py:231

commit v11 on v10

--- a/solution.py
+++ b/solution.py
@@ -95,12 +95,14 @@
         )
 
     applied = newton_product(blocks, first)
+    stacked_left = tuple(jnp.concatenate(pair, axis=-2) for pair in zip(left, applied_left))
     if space_count > 1:
         incoming = pass_boundary(boundary)
         schur = schur_of(incoming)
         mixed = first_step_product(schur, right)
-        step = add(first, newton_product(left, mixed))
-        system_step = add(applied, newton_product(applied_left, mixed))
+        both = newton_product(stacked_left, mixed)
+        step = add(first, part(both, rows=slice(0, size)))
+        system_step = add(applied, part(both, rows=slice(size, 2 * size)))
         system_step = lead_rows_minus(system_step, schur, part(step, rows=lead))
     else:
         step = first

time: 86.6 us -> 84.7 us (0.978)
  matrix products: 29.9 us -> 26.3 us
  waiting for transfers between devices: 27.2 us -> 28.6 us
  other arithmetic: 0.88 us -> 2.24 us
  local copies, waits for them, and re-layouts: 4.93 us -> 3.99 us
    dot_general x13 -> x12, matrix products: 9.8 us -> 7.91 us  [complex_product(): real_real = jnp.matmul(first_real, second_real, precision=precision)]
    ppermute x1, waiting for transfers between devices: 0.68 us -> 2.07 us  [from_behind(): return lax.ppermute(shard, axis, pairs)]
    add x1, other arithmetic: 0.07 us -> 1.36 us  [complex_product(): first_real + first_imag]
    unnamed x20, local copies, waits for them, and re-layouts: 3.74 us -> 2.76 us
    dot_general x13 -> x12, matrix products: 8.96 us -> 7.99 us  [complex_product(): imag_imag = jnp.matmul(first_imag, second_imag, precision=precision)]
    dot_general x13 -> x12, matrix products: 9.2 us -> 8.41 us  [complex_product(): jnp.matmul(first_real + first_imag, second_real + second_imag, precision=...]
  transfers between devices with their start and end apart: 3 -> 3, of which waited for: 3 -> 3; matrix products, arithmetic and copies ran while one was open for 7% -> 6% of each run, Pallas kernels for 0% -> 0%
where the time goes in v11:
time: 84.7 us; the launch traced here: 84.3 us
  waiting for transfers between devices  28.6 us (34%)
  matrix products  26.3 us (31%)
  starting transfers between devices  15.3 us (18%)
  Pallas kernels  6.76 us (8%)
  local copies, waits for them, and re-layouts  3.99 us (5%)
  other arithmetic  2.24 us (3%)
  between operations  1.06 us (1%)
    all_to_all x1, waiting for transfers between devices, body(): self_energy = lax.all_to_all(summed, axes, 0, 2, tiled=True)  13.3 us
    all_to_all x1, waiting for transfers between devices, body(): by_pairs = lax.all_to_all(picked, axes, 0, 0, tiled=True)  13.2 us
    dot_general x12, matrix products, complex_product(): jnp.matmul(first_real + first_imag, second_real + second_imag, precision=...  8.41 us
    dot_general x12, matrix products, complex_product(): imag_imag = jnp.matmul(first_imag, second_imag, precision=precision)  7.99 us
    dot_general x12, matrix products, complex_product(): real_real = jnp.matmul(first_real, second_real, precision=precision)  7.91 us
    pallas_call x1, Pallas kernels, pick_tiles(): pl.pallas_call(pick_kernel, out_shape=jax.ShapeDtypeStruct(shape, jnp.flo...  6.76 us
    all_to_all x1, starting transfers between devices, body(): by_pairs = lax.all_to_all(picked, axes, 0, 0, tiled=True)  6.04 us
    ppermute x1, starting transfers between devices, from_behind(): return lax.ppermute(shard, axis, pairs)  5.07 us
  transfers between devices with their start and end apart: 3, of which 3 were waited for; matrix products, arithmetic and copies ran while one was open for 6% of the time, Pallas kernels for 0%

profile of v11, /device:TPU:0, one launch (start us, length us, event | category | flops | bytes accessed | tf_op | source)
XLA Modules:
  0.0 84.3 jit_solution(13667613670313801685)
XLA Ops:
  0.7 1.4 %bitcast_add_fusion = f32[2,256,256]{2,1,0:T(8,128)S(1)} fusion(f32[2,1,1,2,256,256]{5,4,3,2,1,0:T(8,128)} %param.11), kind=kLoop, calls=%fused_computation.53 | loop fusion | flops 131072 | bytes 1572864 | tf_op jit(solution)/shard_map/add | solution.py:34
  2.2 1.8 %fusion.25 = f32[2,256,256]{2,1,0:T(8,128)S(1)} fusion(f32[2,1,1,2,256,256]{5,4,3,2,1,0:T(8,128)S(1)} %copy-done.1, f32[2,1,1,2,256,256]{5,4,3,2,1,0:T(8,128)} %param.12), kind=kOutput, calls=%fused_computation.54 | convolution fusion | flops 402653184 | bytes 1572864 | tf_op jit(solution)/shard_map/dot_general | solution.py:32
  6.0 0.7 subtract_subtract_fusion.1
  6.8 0.8 fusion.6
  7.5 0.7 convolution_bitcast_fusion.5
  8.3 0.7 convolution_bitcast_fusion.6
  9.0 0.7 fusion.13
  11.0 5.1 %collective-permute-start = (f32[2,2,128,128]{3,2,1,0:T(8,128)S(1)}, f32[2,2,128,128]{3,2,1,0:T(8,128)S(1)}, u32[]{:S(2)}, u32[]{:S(2)}) collective-permute-start(f32[2,2,128,128]{3,2,1,0:T(8,128)S(1)} %pad_maximum_fusion.6), channel_id=1, source_target_pairs={{0,1},{2,3},{4,5},{6,7},{8,9},{10,11},{12,13},{14,15},{16,17},{18,... | collective-permute-start | bytes 786440 | tf_op jit(solution)/shard_map/ppermute | solution.py:20
  19.4 2.1 %collective-permute-done = f32[2,2,128,128]{3,2,1,0:T(8,128)S(1)} collective-permute-done((f32[2,2,128,128]{3,2,1,0:T(8,128)S(1)}, f32[2,2,128,128]{3,2,1,0:T(8,128)S(1)}, u32[]{:S(2)}, u32[]{:S(2)}) %collective-permute-start) | collective-permute-done | bytes 262176 | tf_op jit(solution)/shard_map/ppermute | solution.py:20
  25.0 1.0 %fusion.39 = f32[2,512,256]{2,1,0:T(8,128)S(1)} fusion(f32[2,128,256]{2,1,0:T(8,128)S(1)} %fusion.10, f32[2,256,128]{2,1,0:T(8,128)S(1)} %fusion.14, f32[2,256,128]{2,1,0:T(8,128)S(1)} %slice.147), kind=kOutput, calls=%fused_computation.73 | convolution fusion | flops 402784256 | bytes 1835008 | tf_op jit(solution)/shard_map/dot_general | solution.py:32
  26.0 1.0 %fusion.130 = (f32[2,512,256]{2,1,0:T(8,128)S(1)}, f32[2,512,256]{2,1,0:T(8,128)S(1)}) fusion(f32[2,512,256]{2,1,0:T(8,128)S(1)} %fusion.39, f32[2,128,256]{2,1,0:T(8,128)S(1)} %fusion.67, f32[2,128,256]{2,1,0:T(8,128)S(1)} %fusion.64, f32[2,256,128]{2,1,0:T(8,128)S(1)} %get-tuple-element.43, f32[2,256,128]{2,1,0:T(8,128)S(1)} %slice.146), kind=kOutput, calls=%fused_computation.180 | convolution fusion | flops 403111936 | bytes 4194304 | tf_op jit(solution)/shard_map/dot_general | solution.py:31
  27.0 1.0 %fusion = f32[2,512,256]{2,1,0:T(8,128)S(1)} fusion(f32[2,512,256]{2,1,0:T(8,128)S(1)} %fusion.39, f32[2,512,256]{2,1,0:T(8,128)S(1)} %get-tuple-element.46, f32[2,256,128]{2,1,0:T(8,128)S(1)} %fusion.14, f32[2,256,128]{2,1,0:T(8,128)S(1)} %slice.147, f32[2,256,128]{2,1,0:T(8,128)S(1)} %get-tuple-element.43, f32[2,256,128]{2,1,0:T(8,128)S(1)} %slice.146, ...), kind=kOutput, calls=%fused_computation.1 | convolution fusion | flops 403701760 | bytes 4980736 | tf_op jit(solution)/shard_map/dot_general | solution.py:33
  28.5 0.7 slice_add_fusion.1
  31.5 1.5 %subtract_subtract_fusion = (f32[2,256,256]{2,1,0:T(8,128)}, f32[2,256,256]{2,1,0:T(8,128)S(1)}) fusion(f32[2,256,256]{2,1,0:T(8,128)S(1)} %fusion.131, f32[2,256,256]{2,1,0:T(8,128)S(1)} %get-tuple-element.35, f32[2,256,256]{2,1,0:T(8,128)S(1)} %get-tuple-element.48), kind=kOutput, calls=%fused_computation.66 | convolution fusion | flops 403046400 | bytes 2621440 | tf_op jit(solution)/shard_map/dot_general | solution.py:31
  33.0 1.8 %fusion.2.imag_ref = f32[2,256,256]{2,1,0:T(8,128)} fusion(f32[2,256,256]{2,1,0:T(8,128)S(1)} %fusion.131, f32[2,256,256]{2,1,0:T(8,128)S(1)} %get-tuple-element.51, f32[2,256,256]{2,1,0:T(8,128)S(1)} %get-tuple-element.48, f32[2,256,256]{2,1,0:T(8,128)S(1)} %fusion.12, f32[2,256,256]{2,1,0:T(8,128)S(1)} %get-tuple-element.35, ...), kind=kOutput, calls=%fused_computation.5 | convolution fusion | flops 403439616 | bytes 3670016 | tf_op jit(solution)/shard_map/dot_general | solution.py:33
  34.8 6.8 %shard_map.86 = f32[16,2,8,512]{3,2,1,0:T(8,128)} custom-call(s32[128]{0:T(128)} %and_select_fusion.partner_ref, f32[2,256,256]{2,1,0:T(8,128)} %get-tuple-element.50.real_ref, f32[2,256,256]{2,1,0:T(8,128)} %fusion.2.imag_ref), custom_call_target="tpu_custom_call" | custom-call | tf_op jit(solution)/shard_map/pallas_call | solution.py:195
  41.6 6.0 %all-to-all-start = ((f32[16,2,8,512]{3,2,1,0:T(8,128)}), f32[16,2,8,512]{3,2,1,0:T(8,128)S(1)}, u32[]{:S(2)}, u32[]{:S(2)}) async-start(f32[16,2,8,512]{3,2,1,0:T(8,128)} %shard_map.86), calls=%async_computation | async-start | bytes 1048576 | tf_op jit(solution)/shard_map/all_to_all | solution.py:226
  48.9 13.2 %all-to-all-done = f32[16,2,8,512]{3,2,1,0:T(8,128)S(1)} async-done(((f32[16,2,8,512]{3,2,1,0:T(8,128)}), f32[16,2,8,512]{3,2,1,0:T(8,128)S(1)}, u32[]{:S(2)}, u32[]{:S(2)}) %all-to-all-start) | async-done | bytes 524320 | tf_op jit(solution)/shard_map/all_to_all | solution.py:226
  62.1 1.5 %convolution_bitcast_fusion = f32[4,4,2,8,512]{4,0,2,1,3:T(4,128)S(1)} fusion(f32[4,4,2,8,512,1,1]{4,3,2,1,0,6,5:T(8,128)S(1)} %bitcast.212, f32[4,4,4,2,4,2]{1,5,4,3,2,0:T(2,128)S(1)} %bitcast.213), kind=kOutput, calls=%fused_computation.2 | convolution fusion | flops 50331648 | bytes 1052672 | tf_op jit(solution)/shard_map/kjabcd,cjdpx->akbpx/dot_general | solution.py:231
  63.6 1.1 %copy.95 = f32[4,4,2,8,512]{4,3,2,1,0:T(8,128)} copy(f32[4,4,2,8,512]{4,0,2,1,3:T(4,128)S(1)} %convolution_bitcast_fusion) | data formatting | bytes 1048576 | tf_op jit(solution)/shard_map/kjabcd,cjdpx->akbpx/transpose | solution.py:231
  64.7 4.2 %all-to-all-start.1 = ((f32[16,2,8,512]{3,2,1,0:T(8,128)}), f32[16,2,8,512]{3,2,1,0:T(8,128)S(1)}, u32[]{:S(2)}, u32[]{:S(2)}) async-start(f32[16,2,8,512]{3,2,1,0:T(8,128)} %bitcast.42), calls=%async_computation.1 | async-start | bytes 1048576 | tf_op jit(solution)/shard_map/all_to_all | solution.py:233
  69.1 1.0 %copy.97 = f32[2,1,1,2,256,256]{5,4,3,2,1,0:T(8,128)} copy(f32[2,1,1,2,256,256]{5,4,0,3,2,1:T(8,128)S(1)} %maximum_bitcast_fusion) | data formatting | bytes 2097152
  70.1 13.3 %all-to-all-done.1 = f32[16,2,8,512]{3,2,1,0:T(8,128)S(1)} async-done(((f32[16,2,8,512]{3,2,1,0:T(8,128)}), f32[16,2,8,512]{3,2,1,0:T(8,128)S(1)}, u32[]{:S(2)}, u32[]{:S(2)}) %all-to-all-start.1) | async-done | bytes 524320 | tf_op jit(solution)/shard_map/all_to_all | solution.py:233
  83.4 0.8 copy_bitcast_fusion
  (55 shorter events, 14.1 us)
Async XLA Ops:
  0.6 47.0 %copy-start = (f32[2,8,4]{1,2,0:T(4,128)S(1)}, f32[2,8,4]{1,2,0:T(4,128)}, u32[]{:S(2)}) copy-start(f32[2,8,4]{1,2,0:T(4,128)} %param.16) | copy-start | bytes 772
  0.6 1.5 %copy-start.1 = (f32[2,1,1,2,256,256]{5,4,3,2,1,0:T(8,128)S(1)}, f32[2,1,1,2,256,256]{5,4,3,2,1,0:T(8,128)}, u32[]{:S(2)}) copy-start(f32[2,1,1,2,256,256]{5,4,3,2,1,0:T(8,128)} %param.11) | copy-start | bytes 3145732
  2.2 1.8 %copy-start.2 = (f32[2,1,1,2,256,256]{5,4,3,2,1,0:T(8,128)S(1)}, f32[2,1,1,2,256,256]{5,4,3,2,1,0:T(8,128)}, u32[]{:S(2)}) copy-start(f32[2,1,1,2,256,256]{5,4,3,2,1,0:T(8,128)} %param.12) | copy-start | bytes 3145732
  11.0 10.4 %collective-permute-start = (f32[2,2,128,128]{3,2,1,0:T(8,128)S(1)}, f32[2,2,128,128]{3,2,1,0:T(8,128)S(1)}, u32[]{:S(2)}, u32[]{:S(2)}) collective-permute-start(f32[2,2,128,128]{3,2,1,0:T(8,128)S(1)} %pad_maximum_fusion.6), channel_id=1, source_target_pairs={{0,1},{2,3},{4,5},{6,7},{8,9},{10,11},{12,13},{14,15},{16,17},{18,... | collective-permute-start | bytes 786440 | tf_op jit(solution)/shard_map/ppermute | solution.py:20
  17.5 0.7 copy-start.8
  18.7 2.8 %copy-start.5 = (f32[1,1,2,128,128]{4,3,2,1,0:T(8,128)S(1)}, f32[1,1,2,128,128]{4,3,2,1,0:T(8,128)}, u32[]{:S(2)}) copy-start(f32[1,1,2,128,128]{4,3,2,1,0:T(8,128)} %param.13) | copy-start | bytes 393220
  41.6 6.1 %copy-start.7 = (s32[8]{0:T(128)S(1)}, s32[8]{0:T(128)}, u32[]{:S(2)}) copy-start(s32[8]{0:T(128)} %param.15) | copy-start | bytes 100
  41.6 20.5 %all-to-all-start = ((f32[16,2,8,512]{3,2,1,0:T(8,128)}), f32[16,2,8,512]{3,2,1,0:T(8,128)S(1)}, u32[]{:S(2)}, u32[]{:S(2)}) async-start(f32[16,2,8,512]{3,2,1,0:T(8,128)} %shard_map.86), calls=%async_computation | async-start | bytes 1048576 | tf_op jit(solution)/shard_map/all_to_all | solution.py:226
  47.6 0.7 copy-start.6
  64.7 4.2 %copy-start.3 = (f32[2,256,256]{2,1,0:T(8,128)S(1)}, f32[2,256,256]{2,1,0:T(8,128)}, u32[]{:S(2)}) copy-start(f32[2,256,256]{2,1,0:T(8,128)} %get-tuple-element.50.real_ref) | copy-start | bytes 1572868
  64.7 4.3 %copy-start.4 = (f32[2,256,256]{2,1,0:T(8,128)S(1)}, f32[2,256,256]{2,1,0:T(8,128)}, u32[]{:S(2)}) copy-start(f32[2,256,256]{2,1,0:T(8,128)} %fusion.2.imag_ref) | copy-start | bytes 1572868
  64.7 18.7 %all-to-all-start.1 = ((f32[16,2,8,512]{3,2,1,0:T(8,128)}), f32[16,2,8,512]{3,2,1,0:T(8,128)S(1)}, u32[]{:S(2)}, u32[]{:S(2)}) async-start(f32[16,2,8,512]{3,2,1,0:T(8,128)} %bitcast.42), calls=%async_computation.1 | async-start | bytes 1048576 | tf_op jit(solution)/shard_map/all_to_all | solution.py:233

commit v12 on v11

--- a/solution.py
+++ b/solution.py
@@ -71,7 +71,8 @@
         update = newton_product(schur, rows)
         return tuple(v.at[..., lead, :].add(-u) for v, u in zip(values, update))
 
-    first = combine(2.0, guess, first_step_product(guess, first_step_product(blocks, guess)))
+    applied_guess = first_step_product(blocks, guess)
+    first = combine(2.0, guess, first_step_product(guess, applied_guess))
     left = part(guess, cols=lead)
     right = part(guess, rows=lead)
 
@@ -79,7 +80,7 @@
     boundary = combine(
         2.0, part(first, trail, trail), newton_product(part(first, rows=trail), applied_trail)
     )
-    applied_left = newton_product(blocks, left)
+    applied_left = part(applied_guess, cols=lead)
 
     for section in range(1, space_count - 1):
         incoming = pass_boundary(boundary)

time: 84.7 us -> 84.3 us (level)
  other arithmetic: 2.24 us -> 0.87 us
  waiting for transfers between devices: 28.6 us -> 29.8 us
    add x1 -> x0, other arithmetic: 1.36 us -> none  [complex_product(): first_real + first_imag]
    ppermute x1, waiting for transfers between devices: 2.07 us -> 3.26 us  [from_behind(): return lax.ppermute(shard, axis, pairs)]
    dot_general x12 -> x11, matrix products: 8.41 us -> 7.6 us  [complex_product(): jnp.matmul(first_real + first_imag, second_real + second_imag, precision=...]
    dot_general x12 -> x11, matrix products: 7.91 us -> 8.45 us  [complex_product(): real_real = jnp.matmul(first_real, second_real, precision=precision)]
    dot_general x12 -> x11, matrix products: 7.99 us -> 7.56 us  [complex_product(): imag_imag = jnp.matmul(first_imag, second_imag, precision=precision)]
  transfers between devices with their start and end apart: 3 -> 3, of which waited for: 3 -> 3; matrix products, arithmetic and copies ran while one was open for 6% -> 4% of each run, Pallas kernels for 0% -> 0%
where the time goes in v12:
time: 84.3 us; the launch traced here: 83.9 us
  waiting for transfers between devices  29.8 us (35%)
  matrix products  25.6 us (30%)
  starting transfers between devices  15.3 us (18%)
  Pallas kernels  6.76 us (8%)
  local copies, waits for them, and re-layouts  4.45 us (5%)
  between operations  1.08 us (1%)
  other arithmetic  0.87 us (1%)
    all_to_all x1, waiting for transfers between devices, body(): self_energy = lax.all_to_all(summed, axes, 0, 2, tiled=True)  13.3 us
    all_to_all x1, waiting for transfers between devices, body(): by_pairs = lax.all_to_all(picked, axes, 0, 0, tiled=True)  13.2 us
    dot_general x11, matrix products, complex_product(): real_real = jnp.matmul(first_real, second_real, precision=precision)  8.45 us
    dot_general x11, matrix products, complex_product(): jnp.matmul(first_real + first_imag, second_real + second_imag, precision=...  7.6 us
    dot_general x11, matrix products, complex_product(): imag_imag = jnp.matmul(first_imag, second_imag, precision=precision)  7.56 us
    pallas_call x1, Pallas kernels, pick_tiles(): pl.pallas_call(pick_kernel, out_shape=jax.ShapeDtypeStruct(shape, jnp.flo...  6.76 us
    all_to_all x1, starting transfers between devices, body(): by_pairs = lax.all_to_all(picked, axes, 0, 0, tiled=True)  6.05 us
    ppermute x1, starting transfers between devices, from_behind(): return lax.ppermute(shard, axis, pairs)  5.07 us
  transfers between devices with their start and end apart: 3, of which 3 were waited for; matrix products, arithmetic and copies ran while one was open for 4% of the time, Pallas kernels for 0%

profile of v12, /device:TPU:0, one launch (start us, length us, event | category | flops | bytes accessed | tf_op | source)
XLA Modules:
  0.0 83.9 jit_solution(5033626441811851117)
XLA Ops:
  0.7 1.9 %fusion.22 = f32[2,256,256]{2,1,0:T(8,128)S(1)} fusion(f32[2,1,1,2,256,256]{5,4,3,2,1,0:T(8,128)} %param.11, f32[2,1,1,2,256,256]{5,4,3,2,1,0:T(8,128)} %param.12), kind=kOutput, calls=%fused_computation.50 | convolution fusion | flops 402653184 | bytes 1572864 | tf_op jit(solution)/shard_map/dot_general | solution.py:32
  2.6 1.8 %fusion.116 = (f32[2,256,256]{2,1,0:T(8,128)S(1)}, f32[2,256,256]{2,1,0:T(8,128)S(1)}) fusion(f32[2,256,256]{2,1,0:T(8,128)S(1)} %fusion.22, f32[2,1,1,2,256,256]{5,4,3,2,1,0:T(8,128)} %param.12, f32[2,1,1,2,256,256]{5,4,3,2,1,0:T(8,128)S(1)} %copy-done.1), kind=kOutput, calls=%fused_computation.163 | convolution fusion | flops 402784256 | bytes 2621440 | tf_op jit(solution)/shard_map/dot_general | solution.py:31
  5.8 0.7 subtract_subtract_fusion.1
  6.6 0.8 fusion.6
  7.3 0.7 convolution_bitcast_fusion.5
  8.1 0.7 convolution_bitcast_fusion.6
  8.8 0.8 fusion.13
  10.9 5.1 %collective-permute-start = (f32[2,2,128,128]{3,2,1,0:T(8,128)S(1)}, f32[2,2,128,128]{3,2,1,0:T(8,128)S(1)}, u32[]{:S(2)}, u32[]{:S(2)}) collective-permute-start(f32[2,2,128,128]{3,2,1,0:T(8,128)S(1)} %pad_maximum_fusion.6), channel_id=1, source_target_pairs={{0,1},{2,3},{4,5},{6,7},{8,9},{10,11},{12,13},{14,15},{16,17},{18,... | collective-permute-start | bytes 786440 | tf_op jit(solution)/shard_map/ppermute | solution.py:20
  18.0 3.3 %collective-permute-done = f32[2,2,128,128]{3,2,1,0:T(8,128)S(1)} collective-permute-done((f32[2,2,128,128]{3,2,1,0:T(8,128)S(1)}, f32[2,2,128,128]{3,2,1,0:T(8,128)S(1)}, u32[]{:S(2)}, u32[]{:S(2)}) %collective-permute-start) | collective-permute-done | bytes 262176 | tf_op jit(solution)/shard_map/ppermute | solution.py:20
  24.8 1.0 %fusion.34 = f32[2,512,256]{2,1,0:T(8,128)S(1)} fusion(f32[2,128,256]{2,1,0:T(8,128)S(1)} %fusion.10, f32[2,256,128]{2,1,0:T(8,128)S(1)} %slice.167, f32[2,256,128]{2,1,0:T(8,128)S(1)} %slice.166), kind=kOutput, calls=%fused_computation.67 | convolution fusion | flops 402784256 | bytes 1835008 | tf_op jit(solution)/shard_map/dot_general | solution.py:32
  25.8 1.0 %fusion.117 = (f32[2,512,256]{2,1,0:T(8,128)S(1)}, f32[2,512,256]{2,1,0:T(8,128)S(1)}) fusion(f32[2,512,256]{2,1,0:T(8,128)S(1)} %fusion.34, f32[2,128,256]{2,1,0:T(8,128)S(1)} %fusion.59, f32[2,128,256]{2,1,0:T(8,128)S(1)} %fusion.56, f32[2,256,128]{2,1,0:T(8,128)S(1)} %slice.155, f32[2,256,128]{2,1,0:T(8,128)S(1)} %slice.154), kind=kOutput, calls=%fused_computation.164 | convolution fusion | flops 403111936 | bytes 4194304 | tf_op jit(solution)/shard_map/dot_general | solution.py:31
  26.8 1.0 %fusion = f32[2,512,256]{2,1,0:T(8,128)S(1)} fusion(f32[2,512,256]{2,1,0:T(8,128)S(1)} %fusion.34, f32[2,512,256]{2,1,0:T(8,128)S(1)} %get-tuple-element.46, f32[2,256,128]{2,1,0:T(8,128)S(1)} %slice.167, f32[2,256,128]{2,1,0:T(8,128)S(1)} %slice.166, f32[2,256,128]{2,1,0:T(8,128)S(1)} %slice.155, f32[2,256,128]{2,1,0:T(8,128)S(1)} %slice.154, ...), kind=kOutput, calls=%fused_computation.1 | convolution fusion | flops 403701760 | bytes 4980736 | tf_op jit(solution)/shard_map/dot_general | solution.py:33
  29.0 0.7 fusion.4
  31.3 1.5 %subtract_subtract_fusion = (f32[2,256,256]{2,1,0:T(8,128)}, f32[2,256,256]{2,1,0:T(8,128)S(1)}) fusion(f32[2,256,256]{2,1,0:T(8,128)S(1)} %fusion.118, f32[2,256,256]{2,1,0:T(8,128)S(1)} %get-tuple-element.35, f32[2,256,256]{2,1,0:T(8,128)S(1)} %get-tuple-element.48), kind=kOutput, calls=%fused_computation.60 | convolution fusion | flops 403046400 | bytes 2621440 | tf_op jit(solution)/shard_map/dot_general | solution.py:31
  32.8 1.6 %fusion.2.imag_ref = f32[2,256,256]{2,1,0:T(8,128)} fusion(f32[2,256,256]{2,1,0:T(8,128)S(1)} %fusion.118, f32[2,256,256]{2,1,0:T(8,128)S(1)} %get-tuple-element.51, f32[2,256,256]{2,1,0:T(8,128)S(1)} %get-tuple-element.48, f32[2,256,256]{2,1,0:T(8,128)S(1)} %fusion.12, f32[2,256,256]{2,1,0:T(8,128)S(1)} %get-tuple-element.35, ...), kind=kOutput, calls=%fused_computation.5 | convolution fusion | flops 403439616 | bytes 3670016 | tf_op jit(solution)/shard_map/dot_general | solution.py:33
  34.4 6.8 %shard_map.86 = f32[16,2,8,512]{3,2,1,0:T(8,128)} custom-call(s32[128]{0:T(128)} %and_select_fusion.partner_ref, f32[2,256,256]{2,1,0:T(8,128)} %get-tuple-element.50.real_ref, f32[2,256,256]{2,1,0:T(8,128)} %fusion.2.imag_ref), custom_call_target="tpu_custom_call" | custom-call | tf_op jit(solution)/shard_map/pallas_call | solution.py:196
  41.2 6.0 %all-to-all-start = ((f32[16,2,8,512]{3,2,1,0:T(8,128)}), f32[16,2,8,512]{3,2,1,0:T(8,128)S(1)}, u32[]{:S(2)}, u32[]{:S(2)}) async-start(f32[16,2,8,512]{3,2,1,0:T(8,128)} %shard_map.86), calls=%async_computation | async-start | bytes 1048576 | tf_op jit(solution)/shard_map/all_to_all | solution.py:227
  48.5 13.2 %all-to-all-done = f32[16,2,8,512]{3,2,1,0:T(8,128)S(1)} async-done(((f32[16,2,8,512]{3,2,1,0:T(8,128)}), f32[16,2,8,512]{3,2,1,0:T(8,128)S(1)}, u32[]{:S(2)}, u32[]{:S(2)}) %all-to-all-start) | async-done | bytes 524320 | tf_op jit(solution)/shard_map/all_to_all | solution.py:227
  61.7 1.5 %convolution_bitcast_fusion = f32[4,4,2,8,512]{4,0,2,1,3:T(4,128)S(1)} fusion(f32[4,4,2,8,512,1,1]{4,3,2,1,0,6,5:T(8,128)S(1)} %bitcast.211, f32[4,4,4,2,4,2]{1,5,4,3,2,0:T(2,128)S(1)} %bitcast.212), kind=kOutput, calls=%fused_computation.2 | convolution fusion | flops 50331648 | bytes 1052672 | tf_op jit(solution)/shard_map/kjabcd,cjdpx->akbpx/dot_general | solution.py:232
  63.2 1.1 %copy.95 = f32[4,4,2,8,512]{4,3,2,1,0:T(8,128)} copy(f32[4,4,2,8,512]{4,0,2,1,3:T(4,128)S(1)} %convolution_bitcast_fusion) | data formatting | bytes 1048576 | tf_op jit(solution)/shard_map/kjabcd,cjdpx->akbpx/transpose | solution.py:232
  64.3 4.2 %all-to-all-start.1 = ((f32[16,2,8,512]{3,2,1,0:T(8,128)}), f32[16,2,8,512]{3,2,1,0:T(8,128)S(1)}, u32[]{:S(2)}, u32[]{:S(2)}) async-start(f32[16,2,8,512]{3,2,1,0:T(8,128)} %bitcast.42), calls=%async_computation.1 | async-start | bytes 1048576 | tf_op jit(solution)/shard_map/all_to_all | solution.py:234
  68.7 1.0 %copy.97 = f32[2,1,1,2,256,256]{5,4,3,2,1,0:T(8,128)} copy(f32[2,1,1,2,256,256]{5,4,0,3,2,1:T(8,128)S(1)} %maximum_bitcast_fusion) | data formatting | bytes 2097152
  69.7 13.3 %all-to-all-done.1 = f32[16,2,8,512]{3,2,1,0:T(8,128)S(1)} async-done(((f32[16,2,8,512]{3,2,1,0:T(8,128)}), f32[16,2,8,512]{3,2,1,0:T(8,128)S(1)}, u32[]{:S(2)}, u32[]{:S(2)}) %all-to-all-start.1) | async-done | bytes 524320 | tf_op jit(solution)/shard_map/all_to_all | solution.py:234
  83.0 0.8 copy_bitcast_fusion
  (53 shorter events, 12.1 us)
Async XLA Ops:
  0.6 46.7 %copy-start = (f32[2,8,4]{1,2,0:T(4,128)S(1)}, f32[2,8,4]{1,2,0:T(4,128)}, u32[]{:S(2)}) copy-start(f32[2,8,4]{1,2,0:T(4,128)} %param.16) | copy-start | bytes 772
  0.6 2.0 %copy-start.1 = (f32[2,1,1,2,256,256]{5,4,3,2,1,0:T(8,128)S(1)}, f32[2,1,1,2,256,256]{5,4,3,2,1,0:T(8,128)}, u32[]{:S(2)}) copy-start(f32[2,1,1,2,256,256]{5,4,3,2,1,0:T(8,128)} %param.11) | copy-start | bytes 3145732
  2.6 1.8 %copy-start.2 = (f32[2,1,1,2,256,256]{5,4,3,2,1,0:T(8,128)S(1)}, f32[2,1,1,2,256,256]{5,4,3,2,1,0:T(8,128)}, u32[]{:S(2)}) copy-start(f32[2,1,1,2,256,256]{5,4,3,2,1,0:T(8,128)} %param.12) | copy-start | bytes 3145732
  10.9 10.4 %collective-permute-start = (f32[2,2,128,128]{3,2,1,0:T(8,128)S(1)}, f32[2,2,128,128]{3,2,1,0:T(8,128)S(1)}, u32[]{:S(2)}, u32[]{:S(2)}) collective-permute-start(f32[2,2,128,128]{3,2,1,0:T(8,128)S(1)} %pad_maximum_fusion.6), channel_id=1, source_target_pairs={{0,1},{2,3},{4,5},{6,7},{8,9},{10,11},{12,13},{14,15},{16,17},{18,... | collective-permute-start | bytes 786440 | tf_op jit(solution)/shard_map/ppermute | solution.py:20
  16.1 0.7 copy-start.8
  17.4 3.9 %copy-start.5 = (f32[1,1,2,128,128]{4,3,2,1,0:T(8,128)S(1)}, f32[1,1,2,128,128]{4,3,2,1,0:T(8,128)}, u32[]{:S(2)}) copy-start(f32[1,1,2,128,128]{4,3,2,1,0:T(8,128)} %param.13) | copy-start | bytes 393220
  41.2 6.1 %copy-start.7 = (s32[8]{0:T(128)S(1)}, s32[8]{0:T(128)}, u32[]{:S(2)}) copy-start(s32[8]{0:T(128)} %param.15) | copy-start | bytes 100
  41.2 20.5 %all-to-all-start = ((f32[16,2,8,512]{3,2,1,0:T(8,128)}), f32[16,2,8,512]{3,2,1,0:T(8,128)S(1)}, u32[]{:S(2)}, u32[]{:S(2)}) async-start(f32[16,2,8,512]{3,2,1,0:T(8,128)} %shard_map.86), calls=%async_computation | async-start | bytes 1048576 | tf_op jit(solution)/shard_map/all_to_all | solution.py:227
  47.3 0.7 copy-start.6
  64.3 4.2 %copy-start.3 = (f32[2,256,256]{2,1,0:T(8,128)S(1)}, f32[2,256,256]{2,1,0:T(8,128)}, u32[]{:S(2)}) copy-start(f32[2,256,256]{2,1,0:T(8,128)} %get-tuple-element.50.real_ref) | copy-start | bytes 1572868
  64.3 4.2 %copy-start.4 = (f32[2,256,256]{2,1,0:T(8,128)S(1)}, f32[2,256,256]{2,1,0:T(8,128)}, u32[]{:S(2)}) copy-start(f32[2,256,256]{2,1,0:T(8,128)} %fusion.2.imag_ref) | copy-start | bytes 1572868
  64.3 18.7 %all-to-all-start.1 = ((f32[16,2,8,512]{3,2,1,0:T(8,128)}), f32[16,2,8,512]{3,2,1,0:T(8,128)S(1)}, u32[]{:S(2)}, u32[]{:S(2)}) async-start(f32[16,2,8,512]{3,2,1,0:T(8,128)} %bitcast.42), calls=%async_computation.1 | async-start | bytes 1048576 | tf_op jit(solution)/shard_map/all_to_all | solution.py:234

commit v13 on v12

--- a/solution.py
+++ b/solution.py
@@ -95,7 +95,8 @@
             2.0, part(step_trail, rows=trail), newton_product(step_rows, system_trail)
         )
 
-    applied = newton_product(blocks, first)
+    applied_lead = newton_product(blocks, part(first, cols=slice(0, size - edge)))
+    applied = tuple(jnp.concatenate(pair, axis=-1) for pair in zip(applied_lead, applied_trail))
     stacked_left = tuple(jnp.concatenate(pair, axis=-2) for pair in zip(left, applied_left))
     if space_count > 1:
         incoming = pass_boundary(boundary)

time: 84.3 us -> 82.8 us (0.982)
  transfers between devices with their start and end apart: 3 -> 3, of which waited for: 3 -> 3; matrix products, arithmetic and copies ran while one was open for 4% -> 5% of each run, Pallas kernels for 0% -> 0%
where the time goes in v13:
time: 82.8 us; the launch traced here: 82.3 us
  waiting for transfers between devices  29.2 us (35%)
  matrix products  25.1 us (30%)
  starting transfers between devices  15.4 us (19%)
  Pallas kernels  6.76 us (8%)
  local copies, waits for them, and re-layouts  3.85 us (5%)
  between operations  1.07 us (1%)
  other arithmetic  1.04 us (1%)
    all_to_all x1, waiting for transfers between devices, body(): self_energy = lax.all_to_all(summed, axes, 0, 2, tiled=True)  13.3 us
    all_to_all x1, waiting for transfers between devices, body(): by_pairs = lax.all_to_all(picked, axes, 0, 0, tiled=True)  13.2 us
    dot_general x11, matrix products, complex_product(): real_real = jnp.matmul(first_real, second_real, precision=precision)  8.23 us
    dot_general x11, matrix products, complex_product(): jnp.matmul(first_real + first_imag, second_real + second_imag, precision=...  7.51 us
    dot_general x11, matrix products, complex_product(): imag_imag = jnp.matmul(first_imag, second_imag, precision=precision)  7.37 us
    pallas_call x1, Pallas kernels, pick_tiles(): pl.pallas_call(pick_kernel, out_shape=jax.ShapeDtypeStruct(shape, jnp.flo...  6.76 us
    all_to_all x1, starting transfers between devices, body(): by_pairs = lax.all_to_all(picked, axes, 0, 0, tiled=True)  6.06 us
    ppermute x1, starting transfers between devices, from_behind(): return lax.ppermute(shard, axis, pairs)  5.07 us
  transfers between devices with their start and end apart: 3, of which 3 were waited for; matrix products, arithmetic and copies ran while one was open for 5% of the time, Pallas kernels for 0%

profile of v13, /device:TPU:0, one launch (start us, length us, event | category | flops | bytes accessed | tf_op | source)
XLA Modules:
  0.0 82.3 jit_solution(12675861678609851919)
XLA Ops:
  0.7 1.9 %fusion.21 = f32[2,256,256]{2,1,0:T(8,128)S(1)} fusion(f32[2,1,1,2,256,256]{5,4,3,2,1,0:T(8,128)} %param.11, f32[2,1,1,2,256,256]{5,4,3,2,1,0:T(8,128)} %param.12), kind=kOutput, calls=%fused_computation.50 | convolution fusion | flops 402653184 | bytes 1572864 | tf_op jit(solution)/shard_map/dot_general | solution.py:32
  2.6 1.8 %fusion.117 = (f32[2,256,256]{2,1,0:T(8,128)S(1)}, f32[2,256,256]{2,1,0:T(8,128)S(1)}) fusion(f32[2,256,256]{2,1,0:T(8,128)S(1)} %fusion.21, f32[2,1,1,2,256,256]{5,4,3,2,1,0:T(8,128)} %param.12, f32[2,1,1,2,256,256]{5,4,3,2,1,0:T(8,128)S(1)} %copy-done.1), kind=kOutput, calls=%fused_computation.165 | convolution fusion | flops 402784256 | bytes 2621440 | tf_op jit(solution)/shard_map/dot_general | solution.py:31
  4.4 0.7 fusion.5
  5.2 0.7 convolution_bitcast_fusion.1
  5.8 0.7 subtract_subtract_fusion.1
  6.6 0.8 fusion.4
  10.5 5.1 %collective-permute-start = (f32[2,2,128,128]{3,2,1,0:T(8,128)S(1)}, f32[2,2,128,128]{3,2,1,0:T(8,128)S(1)}, u32[]{:S(2)}, u32[]{:S(2)}) collective-permute-start(f32[2,2,128,128]{3,2,1,0:T(8,128)S(1)} %pad_maximum_fusion.6), channel_id=1, source_target_pairs={{0,1},{2,3},{4,5},{6,7},{8,9},{10,11},{12,13},{14,15},{16,17},{18,... | collective-permute-start | bytes 786440 | tf_op jit(solution)/shard_map/ppermute | solution.py:20
  18.3 2.6 %collective-permute-done = f32[2,2,128,128]{3,2,1,0:T(8,128)S(1)} collective-permute-done((f32[2,2,128,128]{3,2,1,0:T(8,128)S(1)}, f32[2,2,128,128]{3,2,1,0:T(8,128)S(1)}, u32[]{:S(2)}, u32[]{:S(2)}) %collective-permute-start) | collective-permute-done | bytes 262176 | tf_op jit(solution)/shard_map/ppermute | solution.py:20
  24.5 1.0 %fusion.32 = f32[2,512,256]{2,1,0:T(8,128)S(1)} fusion(f32[2,128,256]{2,1,0:T(8,128)S(1)} %fusion.8, f32[2,256,128]{2,1,0:T(8,128)S(1)} %slice.175, f32[2,256,128]{2,1,0:T(8,128)S(1)} %slice.174), kind=kOutput, calls=%fused_computation.66 | convolution fusion | flops 402784256 | bytes 1835008 | tf_op jit(solution)/shard_map/dot_general | solution.py:32
  25.5 1.0 %fusion.119 = (f32[2,512,256]{2,1,0:T(8,128)S(1)}, f32[2,512,256]{2,1,0:T(8,128)S(1)}) fusion(f32[2,512,256]{2,1,0:T(8,128)S(1)} %fusion.32, f32[2,128,256]{2,1,0:T(8,128)S(1)} %fusion.62, f32[2,128,256]{2,1,0:T(8,128)S(1)} %fusion.59, f32[2,256,128]{2,1,0:T(8,128)S(1)} %slice.163, f32[2,256,128]{2,1,0:T(8,128)S(1)} %slice.162), kind=kOutput, calls=%fused_computation.167 | convolution fusion | flops 403111936 | bytes 4194304 | tf_op jit(solution)/shard_map/dot_general | solution.py:31
  26.5 1.1 %fusion = f32[2,512,256]{2,1,0:T(8,128)S(1)} fusion(f32[2,512,256]{2,1,0:T(8,128)S(1)} %fusion.32, f32[2,512,256]{2,1,0:T(8,128)S(1)} %get-tuple-element.50, f32[2,256,128]{2,1,0:T(8,128)S(1)} %slice.175, f32[2,256,128]{2,1,0:T(8,128)S(1)} %slice.174, f32[2,256,128]{2,1,0:T(8,128)S(1)} %slice.163, f32[2,256,128]{2,1,0:T(8,128)S(1)} %slice.162, ...), kind=kOutput, calls=%fused_computation.1 | convolution fusion | flops 403701760 | bytes 4980736 | tf_op jit(solution)/shard_map/dot_general | solution.py:33
  29.1 0.7 fusion.121
  29.7 1.5 %subtract_subtract_fusion = (f32[2,256,256]{2,1,0:T(8,128)}, f32[2,256,256]{2,1,0:T(8,128)S(1)}) fusion(f32[2,256,256]{2,1,0:T(8,128)S(1)} %fusion.121, f32[2,256,256]{2,1,0:T(8,128)S(1)} %get-tuple-element.57, f32[2,256,256]{2,1,0:T(8,128)S(1)} %get-tuple-element.53), kind=kOutput, calls=%fused_computation.60 | convolution fusion | flops 403046400 | bytes 2621440 | tf_op jit(solution)/shard_map/dot_general | solution.py:31
  31.3 1.6 %fusion.2.imag_ref = f32[2,256,256]{2,1,0:T(8,128)} fusion(f32[2,256,256]{2,1,0:T(8,128)S(1)} %fusion.121, f32[2,256,256]{2,1,0:T(8,128)S(1)} %get-tuple-element.56, f32[2,256,256]{2,1,0:T(8,128)S(1)} %get-tuple-element.53, f32[2,256,256]{2,1,0:T(8,128)S(1)} %fusion.10, f32[2,256,256]{2,1,0:T(8,128)S(1)} %get-tuple-element.57, ...), kind=kOutput, calls=%fused_computation.5 | convolution fusion | flops 403439616 | bytes 3670016 | tf_op jit(solution)/shard_map/dot_general | solution.py:33
  32.8 6.8 %shard_map.86 = f32[16,2,8,512]{3,2,1,0:T(8,128)} custom-call(s32[128]{0:T(128)} %and_select_fusion.partner_ref, f32[2,256,256]{2,1,0:T(8,128)} %get-tuple-element.55.real_ref, f32[2,256,256]{2,1,0:T(8,128)} %fusion.2.imag_ref), custom_call_target="tpu_custom_call" | custom-call | tf_op jit(solution)/shard_map/pallas_call | solution.py:197
  39.6 6.1 %all-to-all-start = ((f32[16,2,8,512]{3,2,1,0:T(8,128)}), f32[16,2,8,512]{3,2,1,0:T(8,128)S(1)}, u32[]{:S(2)}, u32[]{:S(2)}) async-start(f32[16,2,8,512]{3,2,1,0:T(8,128)} %shard_map.86), calls=%async_computation | async-start | bytes 1048576 | tf_op jit(solution)/shard_map/all_to_all | solution.py:228
  45.7 0.7 copy-done.6
  46.9 13.2 %all-to-all-done = f32[16,2,8,512]{3,2,1,0:T(8,128)S(1)} async-done(((f32[16,2,8,512]{3,2,1,0:T(8,128)}), f32[16,2,8,512]{3,2,1,0:T(8,128)S(1)}, u32[]{:S(2)}, u32[]{:S(2)}) %all-to-all-start) | async-done | bytes 524320 | tf_op jit(solution)/shard_map/all_to_all | solution.py:228
  60.1 1.5 %convolution_bitcast_fusion = f32[4,4,2,8,512]{4,0,2,1,3:T(4,128)S(1)} fusion(f32[4,4,2,8,512,1,1]{4,3,2,1,0,6,5:T(8,128)S(1)} %bitcast.212, f32[4,4,4,2,4,2]{1,5,4,3,2,0:T(2,128)S(1)} %bitcast.213), kind=kOutput, calls=%fused_computation.2 | convolution fusion | flops 50331648 | bytes 1052672 | tf_op jit(solution)/shard_map/kjabcd,cjdpx->akbpx/dot_general | solution.py:233
  61.6 1.1 %copy.101 = f32[4,4,2,8,512]{4,3,2,1,0:T(8,128)} copy(f32[4,4,2,8,512]{4,0,2,1,3:T(4,128)S(1)} %convolution_bitcast_fusion) | data formatting | bytes 1048576 | tf_op jit(solution)/shard_map/kjabcd,cjdpx->akbpx/transpose | solution.py:233
  62.8 4.2 %all-to-all-start.1 = ((f32[16,2,8,512]{3,2,1,0:T(8,128)}), f32[16,2,8,512]{3,2,1,0:T(8,128)S(1)}, u32[]{:S(2)}, u32[]{:S(2)}) async-start(f32[16,2,8,512]{3,2,1,0:T(8,128)} %bitcast.42), calls=%async_computation.1 | async-start | bytes 1048576 | tf_op jit(solution)/shard_map/all_to_all | solution.py:235
  67.1 1.0 %copy.103 = f32[2,1,1,2,256,256]{5,4,3,2,1,0:T(8,128)} copy(f32[2,1,1,2,256,256]{5,4,0,3,2,1:T(8,128)S(1)} %maximum_bitcast_fusion) | data formatting | bytes 2097152
  68.1 13.3 %all-to-all-done.1 = f32[16,2,8,512]{3,2,1,0:T(8,128)S(1)} async-done(((f32[16,2,8,512]{3,2,1,0:T(8,128)}), f32[16,2,8,512]{3,2,1,0:T(8,128)S(1)}, u32[]{:S(2)}, u32[]{:S(2)}) %all-to-all-start.1) | async-done | bytes 524320 | tf_op jit(solution)/shard_map/all_to_all | solution.py:235
  81.5 0.8 %copy_bitcast_fusion = f32[2,1,1,128,512]{4,3,2,1,0:T(8,128)} fusion(f32[16,2,8,512]{3,2,1,0:T(8,128)S(1)} %all-to-all-done.1), kind=kLoop, calls=%fused_computation.57 | loop fusion | bytes 1048576
  (53 shorter events, 11.3 us)
Async XLA Ops:
  0.6 45.1 %copy-start = (f32[2,8,4]{1,2,0:T(4,128)S(1)}, f32[2,8,4]{1,2,0:T(4,128)}, u32[]{:S(2)}) copy-start(f32[2,8,4]{1,2,0:T(4,128)} %param.16) | copy-start | bytes 772
  0.6 2.0 %copy-start.1 = (f32[2,1,1,2,256,256]{5,4,3,2,1,0:T(8,128)S(1)}, f32[2,1,1,2,256,256]{5,4,3,2,1,0:T(8,128)}, u32[]{:S(2)}) copy-start(f32[2,1,1,2,256,256]{5,4,3,2,1,0:T(8,128)} %param.11) | copy-start | bytes 3145732
  2.6 1.8 %copy-start.2 = (f32[2,1,1,2,256,256]{5,4,3,2,1,0:T(8,128)S(1)}, f32[2,1,1,2,256,256]{5,4,3,2,1,0:T(8,128)}, u32[]{:S(2)}) copy-start(f32[2,1,1,2,256,256]{5,4,3,2,1,0:T(8,128)} %param.12) | copy-start | bytes 3145732
  10.5 10.4 %collective-permute-start = (f32[2,2,128,128]{3,2,1,0:T(8,128)S(1)}, f32[2,2,128,128]{3,2,1,0:T(8,128)S(1)}, u32[]{:S(2)}, u32[]{:S(2)}) collective-permute-start(f32[2,2,128,128]{3,2,1,0:T(8,128)S(1)} %pad_maximum_fusion.6), channel_id=1, source_target_pairs={{0,1},{2,3},{4,5},{6,7},{8,9},{10,11},{12,13},{14,15},{16,17},{18,... | collective-permute-start | bytes 786440 | tf_op jit(solution)/shard_map/ppermute | solution.py:20
  16.4 0.7 copy-start.8
  17.7 3.3 %copy-start.5 = (f32[1,1,2,128,128]{4,3,2,1,0:T(8,128)S(1)}, f32[1,1,2,128,128]{4,3,2,1,0:T(8,128)}, u32[]{:S(2)}) copy-start(f32[1,1,2,128,128]{4,3,2,1,0:T(8,128)} %param.13) | copy-start | bytes 393220
  39.6 6.1 %copy-start.7 = (s32[8]{0:T(128)S(1)}, s32[8]{0:T(128)}, u32[]{:S(2)}) copy-start(s32[8]{0:T(128)} %param.15) | copy-start | bytes 100
  39.6 20.5 %all-to-all-start = ((f32[16,2,8,512]{3,2,1,0:T(8,128)}), f32[16,2,8,512]{3,2,1,0:T(8,128)S(1)}, u32[]{:S(2)}, u32[]{:S(2)}) async-start(f32[16,2,8,512]{3,2,1,0:T(8,128)} %shard_map.86), calls=%async_computation | async-start | bytes 1048576 | tf_op jit(solution)/shard_map/all_to_all | solution.py:228
  45.7 0.7 copy-start.6
  62.8 4.2 %copy-start.3 = (f32[2,256,256]{2,1,0:T(8,128)S(1)}, f32[2,256,256]{2,1,0:T(8,128)}, u32[]{:S(2)}) copy-start(f32[2,256,256]{2,1,0:T(8,128)} %get-tuple-element.55.real_ref) | copy-start | bytes 1572868
  62.8 4.3 %copy-start.4 = (f32[2,256,256]{2,1,0:T(8,128)S(1)}, f32[2,256,256]{2,1,0:T(8,128)}, u32[]{:S(2)}) copy-start(f32[2,256,256]{2,1,0:T(8,128)} %fusion.2.imag_ref) | copy-start | bytes 1572868
  62.8 18.7 %all-to-all-start.1 = ((f32[16,2,8,512]{3,2,1,0:T(8,128)}), f32[16,2,8,512]{3,2,1,0:T(8,128)S(1)}, u32[]{:S(2)}, u32[]{:S(2)}) async-start(f32[16,2,8,512]{3,2,1,0:T(8,128)} %bitcast.42), calls=%async_computation.1 | async-start | bytes 1048576 | tf_op jit(solution)/shard_map/all_to_all | solution.py:235

commit v14 on v13

--- a/solution.py
+++ b/solution.py
@@ -124,6 +124,10 @@
     absorption = (energy_gap[None, :, :] == phonon_shift[:, None, None]).astype(jnp.float32)
     shift_table = jnp.stack([emission, absorption], axis=0)
     return jnp.einsum("kjdw,dwEF->kjEF", momentum_mix, shift_table, precision=HIGHEST)
+
+
+def part_of(pair, index):
+    return tuple(value[index : index + 1] for value in pair)
 
 
 def pick_kernel(partner_ref, real_ref, imag_ref, out_ref):
@@ -213,7 +217,11 @@
     local_guess = (inverse_guess[:, 0, 0, 0], inverse_guess[:, 0, 0, 1])
     coupling_block = (coupling[0, 0, 0], coupling[0, 0, 1])
     energy_count = blocks.shape[0]
-    green_pair = sweep(local_blocks, local_guess, coupling_block)
+    swept = [
+        sweep(part_of(local_blocks, e), part_of(local_guess, e), coupling_block)
+        for e in range(energy_count)
+    ]
+    green_pair = tuple(jnp.concatenate(values, axis=0) for values in zip(*swept))
     green_block = jnp.stack(green_pair, axis=1)
     momenta = momentum_table.shape[0]
     energy_groups = lax.axis_size("energy")

time: 82.8 us -> 88.4 us (1.068)
  matrix products: 25.1 us -> 28.9 us
  waiting for transfers between devices: 29.2 us -> 26.6 us
  other arithmetic: 1.04 us -> 3.2 us
  starting transfers between devices: 15.4 us -> 16.5 us
    ppermute x1 -> x2, waiting for transfers between devices: 2.63 us -> 0.01 us  [from_behind(): return lax.ppermute(shard, axis, pairs)]
    concatenate x0 -> x2, other arithmetic: none -> 1.76 us  [body(): jnp.concatenate(values, axis=0)]
    dot_general x11 -> x22, matrix products: 7.37 us -> 9.02 us  [complex_product(): imag_imag = jnp.matmul(first_imag, second_imag, precision=precision)]
    dot_general x11 -> x22, matrix products: 7.51 us -> 9.02 us  [complex_product(): jnp.matmul(first_real + first_imag, second_real + second_imag, precision=...]
    ppermute x1 -> x2, starting transfers between devices: 5.07 us -> 6.36 us  [from_behind(): return lax.ppermute(shard, axis, pairs)]
    unnamed x20 -> x16, local copies, waits for them, and re-layouts: 2.58 us -> 3.33 us
    dot_general x11 -> x22, matrix products: 8.23 us -> 8.91 us  [complex_product(): real_real = jnp.matmul(first_real, second_real, precision=precision)]
  transfers between devices with their start and end apart: 3 -> 4, of which waited for: 3 -> 2; matrix products, arithmetic and copies ran while one was open for 5% -> 16% of each run, Pallas kernels for 0% -> 0%
where the time goes in v14:
time: 88.4 us; the launch traced here: 87.9 us
  matrix products  28.9 us (33%)
  waiting for transfers between devices  26.6 us (30%)
  starting transfers between devices  16.5 us (19%)
  Pallas kernels  6.75 us (8%)
  local copies, waits for them, and re-layouts  4.65 us (5%)
  other arithmetic  3.2 us (4%)
  between operations  1.42 us (2%)
    all_to_all x1, waiting for transfers between devices, body(): self_energy = lax.all_to_all(summed, axes, 0, 2, tiled=True)  13.3 us
    all_to_all x1, waiting for transfers between devices, body(): by_pairs = lax.all_to_all(picked, axes, 0, 0, tiled=True)  13.2 us
    dot_general x22, matrix products, complex_product(): imag_imag = jnp.matmul(first_imag, second_imag, precision=precision)  9.02 us
    dot_general x22, matrix products, complex_product(): jnp.matmul(first_real + first_imag, second_real + second_imag, precision=...  9.02 us
    dot_general x22, matrix products, complex_product(): real_real = jnp.matmul(first_real, second_real, precision=precision)  8.91 us
    pallas_call x1, Pallas kernels, pick_tiles(): pl.pallas_call(pick_kernel, out_shape=jax.ShapeDtypeStruct(shape, jnp.flo...  6.75 us
    ppermute x2, starting transfers between devices, from_behind(): return lax.ppermute(shard, axis, pairs)  6.36 us
    all_to_all x1, starting transfers between devices, body(): by_pairs = lax.all_to_all(picked, axes, 0, 0, tiled=True)  6.02 us
  transfers between devices with their start and end apart: 4, of which 2 were waited for; matrix products, arithmetic and copies ran while one was open for 16% of the time, Pallas kernels for 0%

profile of v14, /device:TPU:0, one launch (start us, length us, event | category | flops | bytes accessed | tf_op | source)
XLA Modules:
  0.0 87.9 jit_solution(9403109165961634482)
XLA Ops:
  0.7 1.5 %fusion.87 = f32[256,256]{1,0:T(8,128)S(1)} fusion(f32[2,1,1,2,256,256]{5,4,3,2,1,0:T(8,128)} %param.15, f32[2,1,1,2,256,256]{5,4,3,2,1,0:T(8,128)} %param.16), kind=kOutput, calls=%fused_computation.149 | convolution fusion | flops 201326592 | bytes 786432 | tf_op jit(solution)/shard_map/dot_general | solution.py:32
  2.2 1.5 %fusion.94 = f32[256,256]{1,0:T(8,128)S(1)} fusion(f32[2,1,1,2,256,256]{5,4,3,2,1,0:T(8,128)} %param.15, f32[2,1,1,2,256,256]{5,4,3,2,1,0:T(8,128)} %param.16), kind=kOutput, calls=%fused_computation.156 | convolution fusion | flops 201326592 | bytes 786432 | tf_op jit(solution)/shard_map/dot_general | solution.py:31
  3.7 1.4 %fusion.9 = f32[256,256]{1,0:T(8,128)S(1)} fusion(f32[256,256]{1,0:T(8,128)S(1)} %fusion.87, f32[256,256]{1,0:T(8,128)S(1)} %fusion.94, f32[2,1,1,2,256,256]{5,4,3,2,1,0:T(8,128)} %param.16, f32[2,1,1,2,256,256]{5,4,3,2,1,0:T(8,128)S(1)} %copy-done.1), kind=kOutput, calls=%fused_computation.17 | convolution fusion | flops 201588736 | bytes 1835008 | tf_op jit(solution)/shard_map/dot_general | solution.py:33
  10.5 4.9 %collective-permute-start.1 = (f32[2,1,128,128]{3,2,1,0:T(8,128)S(1)}, f32[2,1,128,128]{3,2,1,0:T(8,128)S(1)}, u32[]{:S(2)}, u32[]{:S(2)}) collective-permute-start(f32[2,1,128,128]{3,2,1,0:T(8,128)S(1)} %pad_maximum_fusion.3), channel_id=1, source_target_pairs={{0,1},{2,3},{4,5},{6,7},{8,9},{10,11},{12,13},{14,15},{16,17},{18,... | collective-permute-start | bytes 393224 | tf_op jit(solution)/shard_map/ppermute | solution.py:20
  17.9 1.5 %collective-permute-start = (f32[2,1,128,128]{3,2,1,0:T(8,128)S(1)}, f32[2,1,128,128]{3,2,1,0:T(8,128)S(1)}, u32[]{:S(2)}, u32[]{:S(2)}) collective-permute-start(f32[2,1,128,128]{3,2,1,0:T(8,128)S(1)} %pad_maximum_fusion.2), channel_id=1, source_target_pairs={{0,1},{2,3},{4,5},{6,7},{8,9},{10,11},{12,13},{14,15},{16,17},{18,... | collective-permute-start | bytes 393224 | tf_op jit(solution)/shard_map/ppermute | solution.py:20
  26.0 0.6 fusion.60
  26.6 0.6 fusion.63
  27.2 0.6 fusion.1
  32.6 0.6 fusion.49
  33.2 0.6 fusion.52
  33.9 0.6 fusion.3
  35.5 0.6 fusion.100
  36.9 0.9 %pad_maximum_fusion.1 = (f32[2,256,256]{2,1,0:T(8,128)}, f32[2,1,256,256]{3,2,0,1:T(8,128)S(1)}) fusion(f32[1,256,256]{2,1,0:T(8,128)S(1)} %fusion.17, f32[1,256,256]{2,1,0:T(8,128)S(1)} %fusion.16), kind=kLoop, calls=%fused_computation.90 | loop fusion | flops 131072 | bytes 1572864 | tf_op jit(solution)/shard_map/concatenate | solution.py:224
  37.8 0.9 %pad_maximum_fusion = (f32[2,256,256]{2,1,0:T(8,128)}, f32[2,1,256,256]{3,2,0,1:T(8,128)S(1)}) fusion(f32[1,256,256]{2,1,0:T(8,128)S(1)} %get-tuple-element.102, f32[1,256,256]{2,1,0:T(8,128)S(1)} %get-tuple-element.104), kind=kLoop, calls=%fused_computation.89 | loop fusion | flops 131072 | bytes 1572864 | tf_op jit(solution)/shard_map/concatenate | solution.py:224
  38.7 6.7 %shard_map.86 = f32[16,2,8,512]{3,2,1,0:T(8,128)} custom-call(s32[128]{0:T(128)} %and_select_fusion.partner_ref, f32[2,256,256]{2,1,0:T(8,128)} %get-tuple-element.68.real_ref, f32[2,256,256]{2,1,0:T(8,128)} %get-tuple-element.66.imag_ref), custom_call_target="tpu_custom_call" | custom-call | tf_op jit(solution)/shard_map/pallas_call | solution.py:201
  45.4 6.0 %all-to-all-start = ((f32[16,2,8,512]{3,2,1,0:T(8,128)}), f32[16,2,8,512]{3,2,1,0:T(8,128)S(1)}, u32[]{:S(2)}, u32[]{:S(2)}) async-start(f32[16,2,8,512]{3,2,1,0:T(8,128)} %shard_map.86), calls=%async_computation | async-start | bytes 1048576 | tf_op jit(solution)/shard_map/all_to_all | solution.py:236
  51.5 0.7 copy-done.4
  52.7 13.2 %all-to-all-done = f32[16,2,8,512]{3,2,1,0:T(8,128)S(1)} async-done(((f32[16,2,8,512]{3,2,1,0:T(8,128)}), f32[16,2,8,512]{3,2,1,0:T(8,128)S(1)}, u32[]{:S(2)}, u32[]{:S(2)}) %all-to-all-start) | async-done | bytes 524320 | tf_op jit(solution)/shard_map/all_to_all | solution.py:236
  65.9 1.5 %convolution_bitcast_fusion = f32[4,4,2,8,512]{4,0,2,1,3:T(4,128)S(1)} fusion(f32[4,4,2,8,512,1,1]{4,3,2,1,0,6,5:T(8,128)S(1)} %bitcast.512, f32[4,4,4,2,4,2]{1,5,4,3,2,0:T(2,128)S(1)} %bitcast.513), kind=kOutput, calls=%fused_computation | convolution fusion | flops 50331648 | bytes 1052672 | tf_op jit(solution)/shard_map/kjabcd,cjdpx->akbpx/dot_general | solution.py:241
  67.4 1.1 %copy.74 = f32[4,4,2,8,512]{4,3,2,1,0:T(8,128)} copy(f32[4,4,2,8,512]{4,0,2,1,3:T(4,128)S(1)} %convolution_bitcast_fusion) | data formatting | bytes 1048576 | tf_op jit(solution)/shard_map/kjabcd,cjdpx->akbpx/transpose | solution.py:241
  68.5 4.1 %all-to-all-start.1 = ((f32[16,2,8,512]{3,2,1,0:T(8,128)}), f32[16,2,8,512]{3,2,1,0:T(8,128)S(1)}, u32[]{:S(2)}, u32[]{:S(2)}) async-start(f32[16,2,8,512]{3,2,1,0:T(8,128)} %bitcast.147), calls=%async_computation.1 | async-start | bytes 1048576 | tf_op jit(solution)/shard_map/all_to_all | solution.py:243
  72.7 1.0 %copy.76 = f32[2,1,1,2,256,256]{5,4,3,2,1,0:T(8,128)} copy(f32[2,1,1,2,256,256]{5,4,0,3,2,1:T(8,128)S(1)} %maximum_bitcast_fusion) | data formatting | bytes 2097152
  73.8 13.3 %all-to-all-done.1 = f32[16,2,8,512]{3,2,1,0:T(8,128)S(1)} async-done(((f32[16,2,8,512]{3,2,1,0:T(8,128)}), f32[16,2,8,512]{3,2,1,0:T(8,128)S(1)}, u32[]{:S(2)}, u32[]{:S(2)}) %all-to-all-start.1) | async-done | bytes 524320 | tf_op jit(solution)/shard_map/all_to_all | solution.py:243
  87.1 0.8 copy_bitcast_fusion
  (98 shorter events, 21.4 us)
Async XLA Ops:
  0.6 50.9 %copy-start = (f32[2,8,4]{1,2,0:T(4,128)S(1)}, f32[2,8,4]{1,2,0:T(4,128)}, u32[]{:S(2)}) copy-start(f32[2,8,4]{1,2,0:T(4,128)} %param.20) | copy-start | bytes 772
  0.6 3.0 %copy-start.1 = (f32[2,1,1,2,256,256]{5,4,3,2,1,0:T(8,128)S(1)}, f32[2,1,1,2,256,256]{5,4,3,2,1,0:T(8,128)}, u32[]{:S(2)}) copy-start(f32[2,1,1,2,256,256]{5,4,3,2,1,0:T(8,128)} %param.15) | copy-start | bytes 3145732
  2.2 3.0 %copy-start.2 = (f32[2,1,1,2,256,256]{5,4,3,2,1,0:T(8,128)S(1)}, f32[2,1,1,2,256,256]{5,4,3,2,1,0:T(8,128)}, u32[]{:S(2)}) copy-start(f32[2,1,1,2,256,256]{5,4,3,2,1,0:T(8,128)} %param.16) | copy-start | bytes 3145732
  10.5 12.4 %collective-permute-start.1 = (f32[2,1,128,128]{3,2,1,0:T(8,128)S(1)}, f32[2,1,128,128]{3,2,1,0:T(8,128)S(1)}, u32[]{:S(2)}, u32[]{:S(2)}) collective-permute-start(f32[2,1,128,128]{3,2,1,0:T(8,128)S(1)} %pad_maximum_fusion.3), channel_id=1, source_target_pairs={{0,1},{2,3},{4,5},{6,7},{8,9},{10,11},{12,13},{14,15},{16,17},{18,... | collective-permute-start | bytes 393224 | tf_op jit(solution)/shard_map/ppermute | solution.py:20
  17.9 12.2 %collective-permute-start = (f32[2,1,128,128]{3,2,1,0:T(8,128)S(1)}, f32[2,1,128,128]{3,2,1,0:T(8,128)S(1)}, u32[]{:S(2)}, u32[]{:S(2)}) collective-permute-start(f32[2,1,128,128]{3,2,1,0:T(8,128)S(1)} %pad_maximum_fusion.2), channel_id=1, source_target_pairs={{0,1},{2,3},{4,5},{6,7},{8,9},{10,11},{12,13},{14,15},{16,17},{18,... | collective-permute-start | bytes 393224 | tf_op jit(solution)/shard_map/ppermute | solution.py:20
  21.1 0.7 copy-start.6
  22.5 0.9 %copy-start.3 = (f32[1,1,2,128,128]{4,3,2,1,0:T(8,128)S(1)}, f32[1,1,2,128,128]{4,3,2,1,0:T(8,128)}, u32[]{:S(2)}) copy-start(f32[1,1,2,128,128]{4,3,2,1,0:T(8,128)} %param.17) | copy-start | bytes 393220
  45.4 6.0 %copy-start.5 = (s32[8]{0:T(128)S(1)}, s32[8]{0:T(128)}, u32[]{:S(2)}) copy-start(s32[8]{0:T(128)} %param.19) | copy-start | bytes 100
  45.4 20.5 %all-to-all-start = ((f32[16,2,8,512]{3,2,1,0:T(8,128)}), f32[16,2,8,512]{3,2,1,0:T(8,128)S(1)}, u32[]{:S(2)}, u32[]{:S(2)}) async-start(f32[16,2,8,512]{3,2,1,0:T(8,128)} %shard_map.86), calls=%async_computation | async-start | bytes 1048576 | tf_op jit(solution)/shard_map/all_to_all | solution.py:236
  51.5 0.7 copy-start.4
  68.5 18.6 %all-to-all-start.1 = ((f32[16,2,8,512]{3,2,1,0:T(8,128)}), f32[16,2,8,512]{3,2,1,0:T(8,128)S(1)}, u32[]{:S(2)}, u32[]{:S(2)}) async-start(f32[16,2,8,512]{3,2,1,0:T(8,128)} %bitcast.147), calls=%async_computation.1 | async-start | bytes 1048576 | tf_op jit(solution)/shard_map/all_to_all | solution.py:243

commit v15 on v13

--- a/solution.py
+++ b/solution.py
@@ -69,7 +69,10 @@
 
     def lead_rows_minus(values, schur, rows):
         update = newton_product(schur, rows)
-        return tuple(v.at[..., lead, :].add(-u) for v, u in zip(values, update))
+        return tuple(
+            jnp.concatenate([v[..., lead, :] - u, v[..., edge:, :]], axis=-2)
+            for v, u in zip(values, update)
+        )
 
     applied_guess = first_step_product(blocks, guess)
     first = combine(2.0, guess, first_step_product(guess, applied_guess))

time: 82.8 us -> 82.7 us (level)
  no operation moved by 1% of the time
where the time goes in v15:
time: 82.7 us; the launch traced here: 82.3 us
  waiting for transfers between devices  29.2 us (35%)
  matrix products  24.9 us (30%)
  starting transfers between devices  15.3 us (19%)
  Pallas kernels  6.76 us (8%)
  local copies, waits for them, and re-layouts  3.87 us (5%)
  other arithmetic  1.11 us (1%)
  between operations  1.08 us (1%)
    all_to_all x1, waiting for transfers between devices, body(): self_energy = lax.all_to_all(summed, axes, 0, 2, tiled=True)  13.3 us
    all_to_all x1, waiting for transfers between devices, body(): by_pairs = lax.all_to_all(picked, axes, 0, 0, tiled=True)  13.2 us
    dot_general x11, matrix products, complex_product(): real_real = jnp.matmul(first_real, second_real, precision=precision)  8.16 us
    dot_general x11, matrix products, complex_product(): jnp.matmul(first_real + first_imag, second_real + second_imag, precision=...  7.46 us
    dot_general x11, matrix products, complex_product(): imag_imag = jnp.matmul(first_imag, second_imag, precision=precision)  7.37 us
    pallas_call x1, Pallas kernels, pick_tiles(): pl.pallas_call(pick_kernel, out_shape=jax.ShapeDtypeStruct(shape, jnp.flo...  6.76 us
    all_to_all x1, starting transfers between devices, body(): by_pairs = lax.all_to_all(picked, axes, 0, 0, tiled=True)  6.05 us
    ppermute x1, starting transfers between devices, from_behind(): return lax.ppermute(shard, axis, pairs)  5.07 us
  transfers between devices with their start and end apart: 3, of which 3 were waited for; matrix products, arithmetic and copies ran while one was open for 5% of the time, Pallas kernels for 0%

profile of v15, /device:TPU:0, one launch (start us, length us, event | category | flops | bytes accessed | tf_op | source)
XLA Modules:
  0.0 82.3 jit_solution(2549861756306876478)
XLA Ops:
  0.7 1.9 %fusion.19 = f32[2,256,256]{2,1,0:T(8,128)S(1)} fusion(f32[2,1,1,2,256,256]{5,4,3,2,1,0:T(8,128)} %param.7, f32[2,1,1,2,256,256]{5,4,3,2,1,0:T(8,128)} %param.8), kind=kOutput, calls=%fused_computation.50 | convolution fusion | flops 402653184 | bytes 1572864 | tf_op jit(solution)/shard_map/dot_general | solution.py:32
  2.6 1.8 %fusion.119 = (f32[2,256,256]{2,1,0:T(8,128)S(1)}, f32[2,256,256]{2,1,0:T(8,128)S(1)}) fusion(f32[2,256,256]{2,1,0:T(8,128)S(1)} %fusion.19, f32[2,1,1,2,256,256]{5,4,3,2,1,0:T(8,128)} %param.8, f32[2,1,1,2,256,256]{5,4,3,2,1,0:T(8,128)S(1)} %copy-done.1), kind=kOutput, calls=%fused_computation.169 | convolution fusion | flops 402784256 | bytes 2621440 | tf_op jit(solution)/shard_map/dot_general | solution.py:31
  4.4 0.7 fusion.5
  5.2 0.7 convolution_bitcast_fusion.1
  5.8 0.7 subtract_subtract_fusion.1
  6.6 0.8 fusion.4
  10.5 5.1 %collective-permute-start = (f32[2,2,128,128]{3,2,1,0:T(8,128)S(1)}, f32[2,2,128,128]{3,2,1,0:T(8,128)S(1)}, u32[]{:S(2)}, u32[]{:S(2)}) collective-permute-start(f32[2,2,128,128]{3,2,1,0:T(8,128)S(1)} %pad_maximum_fusion.12), channel_id=1, source_target_pairs={{0,1},{2,3},{4,5},{6,7},{8,9},{10,11},{12,13},{14,15},{16,17},{18,... | collective-permute-start | bytes 786440 | tf_op jit(solution)/shard_map/ppermute | solution.py:20
  18.3 2.6 %collective-permute-done = f32[2,2,128,128]{3,2,1,0:T(8,128)S(1)} collective-permute-done((f32[2,2,128,128]{3,2,1,0:T(8,128)S(1)}, f32[2,2,128,128]{3,2,1,0:T(8,128)S(1)}, u32[]{:S(2)}, u32[]{:S(2)}) %collective-permute-start) | collective-permute-done | bytes 262176 | tf_op jit(solution)/shard_map/ppermute | solution.py:20
  24.5 1.0 %fusion.32 = f32[2,512,256]{2,1,0:T(8,128)S(1)} fusion(f32[2,128,256]{2,1,0:T(8,128)S(1)} %fusion.7, f32[2,256,128]{2,1,0:T(8,128)S(1)} %slice.141, f32[2,256,128]{2,1,0:T(8,128)S(1)} %slice.140), kind=kOutput, calls=%fused_computation.68 | convolution fusion | flops 402784256 | bytes 1835008 | tf_op jit(solution)/shard_map/dot_general | solution.py:32
  25.5 1.0 %fusion.121 = (f32[2,512,256]{2,1,0:T(8,128)S(1)}, f32[2,512,256]{2,1,0:T(8,128)S(1)}) fusion(f32[2,512,256]{2,1,0:T(8,128)S(1)} %fusion.32, f32[2,128,256]{2,1,0:T(8,128)S(1)} %fusion.61, f32[2,128,256]{2,1,0:T(8,128)S(1)} %fusion.58, f32[2,256,128]{2,1,0:T(8,128)S(1)} %slice.129, f32[2,256,128]{2,1,0:T(8,128)S(1)} %slice.128), kind=kOutput, calls=%fused_computation.171 | convolution fusion | flops 403111936 | bytes 4194304 | tf_op jit(solution)/shard_map/dot_general | solution.py:31
  26.5 1.1 %fusion = f32[2,512,256]{2,1,0:T(8,128)S(1)} fusion(f32[2,512,256]{2,1,0:T(8,128)S(1)} %fusion.32, f32[2,512,256]{2,1,0:T(8,128)S(1)} %get-tuple-element.28, f32[2,256,128]{2,1,0:T(8,128)S(1)} %slice.141, f32[2,256,128]{2,1,0:T(8,128)S(1)} %slice.140, f32[2,256,128]{2,1,0:T(8,128)S(1)} %slice.129, f32[2,256,128]{2,1,0:T(8,128)S(1)} %slice.128, ...), kind=kOutput, calls=%fused_computation.1 | convolution fusion | flops 403701760 | bytes 4980736 | tf_op jit(solution)/shard_map/dot_general | solution.py:33
  29.1 0.7 fusion.30
  29.8 1.5 %subtract_subtract_fusion = (f32[2,256,256]{2,1,0:T(8,128)}, f32[2,256,256]{2,1,0:T(8,128)S(1)}) fusion(f32[2,256,256]{2,1,0:T(8,128)S(1)} %fusion.30, f32[2,256,256]{2,1,0:T(8,128)S(1)} %get-tuple-element.33, f32[2,128,256]{2,1,0:T(8,128)S(1)} %get-tuple-element.17, f32[2,128,256]{2,1,0:T(8,128)S(1)} %get-tuple-element.16), kind=kOutput, calls=%fused_computation.60 | convolution fusion | flops 403177472 | bytes 2621440 | tf_op jit(solution)/shard_map/dot_general | solution.py:31
  31.3 1.6 %fusion.2.imag_ref = f32[2,256,256]{2,1,0:T(8,128)} fusion(f32[2,256,256]{2,1,0:T(8,128)S(1)} %fusion.30, f32[2,256,256]{2,1,0:T(8,128)S(1)} %get-tuple-element.32, f32[2,256,256]{2,1,0:T(8,128)S(1)} %get-tuple-element.33, f32[2,256,256]{2,1,0:T(8,128)S(1)} %get-tuple-element.13, f32[2,128,256]{2,1,0:T(8,128)S(1)} %slice.153, f32[2,128,256]{2,1,0:T(8,128)S(1)} %fusion.8, ...), kind=kOutput, calls=%fused_computation.5 | convolution fusion | flops 403701760 | bytes 3670016 | tf_op jit(solution)/shard_map/dot_general | solution.py:33
  32.8 6.8 %shard_map.86 = f32[16,2,8,512]{3,2,1,0:T(8,128)} custom-call(s32[128]{0:T(128)} %and_select_fusion.partner_ref, f32[2,256,256]{2,1,0:T(8,128)} %get-tuple-element.31.real_ref, f32[2,256,256]{2,1,0:T(8,128)} %fusion.2.imag_ref), custom_call_target="tpu_custom_call" | custom-call | tf_op jit(solution)/shard_map/pallas_call | solution.py:200
  39.6 6.0 %all-to-all-start = ((f32[16,2,8,512]{3,2,1,0:T(8,128)}), f32[16,2,8,512]{3,2,1,0:T(8,128)S(1)}, u32[]{:S(2)}, u32[]{:S(2)}) async-start(f32[16,2,8,512]{3,2,1,0:T(8,128)} %shard_map.86), calls=%async_computation | async-start | bytes 1048576 | tf_op jit(solution)/shard_map/all_to_all | solution.py:231
  45.7 0.7 copy-done.6
  46.9 13.2 %all-to-all-done = f32[16,2,8,512]{3,2,1,0:T(8,128)S(1)} async-done(((f32[16,2,8,512]{3,2,1,0:T(8,128)}), f32[16,2,8,512]{3,2,1,0:T(8,128)S(1)}, u32[]{:S(2)}, u32[]{:S(2)}) %all-to-all-start) | async-done | bytes 524320 | tf_op jit(solution)/shard_map/all_to_all | solution.py:231
  60.1 1.5 %convolution_bitcast_fusion = f32[4,4,2,8,512]{4,0,2,1,3:T(4,128)S(1)} fusion(f32[4,4,2,8,512,1,1]{4,3,2,1,0,6,5:T(8,128)S(1)} %bitcast.210, f32[4,4,4,2,4,2]{1,5,4,3,2,0:T(2,128)S(1)} %bitcast.211), kind=kOutput, calls=%fused_computation.2 | convolution fusion | flops 50331648 | bytes 1052672 | tf_op jit(solution)/shard_map/kjabcd,cjdpx->akbpx/dot_general | solution.py:236
  61.6 1.1 %copy.101 = f32[4,4,2,8,512]{4,3,2,1,0:T(8,128)} copy(f32[4,4,2,8,512]{4,0,2,1,3:T(4,128)S(1)} %convolution_bitcast_fusion) | data formatting | bytes 1048576 | tf_op jit(solution)/shard_map/kjabcd,cjdpx->akbpx/transpose | solution.py:236
  62.7 4.2 %all-to-all-start.1 = ((f32[16,2,8,512]{3,2,1,0:T(8,128)}), f32[16,2,8,512]{3,2,1,0:T(8,128)S(1)}, u32[]{:S(2)}, u32[]{:S(2)}) async-start(f32[16,2,8,512]{3,2,1,0:T(8,128)} %bitcast.42), calls=%async_computation.1 | async-start | bytes 1048576 | tf_op jit(solution)/shard_map/all_to_all | solution.py:238
  67.1 1.0 %copy.103 = f32[2,1,1,2,256,256]{5,4,3,2,1,0:T(8,128)} copy(f32[2,1,1,2,256,256]{5,4,0,3,2,1:T(8,128)S(1)} %maximum_bitcast_fusion) | data formatting | bytes 2097152
  68.1 13.3 %all-to-all-done.1 = f32[16,2,8,512]{3,2,1,0:T(8,128)S(1)} async-done(((f32[16,2,8,512]{3,2,1,0:T(8,128)}), f32[16,2,8,512]{3,2,1,0:T(8,128)S(1)}, u32[]{:S(2)}, u32[]{:S(2)}) %all-to-all-start.1) | async-done | bytes 524320 | tf_op jit(solution)/shard_map/all_to_all | solution.py:238
  81.5 0.8 %copy_bitcast_fusion = f32[2,1,1,128,512]{4,3,2,1,0:T(8,128)} fusion(f32[16,2,8,512]{3,2,1,0:T(8,128)S(1)} %all-to-all-done.1), kind=kLoop, calls=%fused_computation.57 | loop fusion | bytes 1048576
  (55 shorter events, 11.4 us)
Async XLA Ops:
  0.6 45.1 %copy-start = (f32[2,8,4]{1,2,0:T(4,128)S(1)}, f32[2,8,4]{1,2,0:T(4,128)}, u32[]{:S(2)}) copy-start(f32[2,8,4]{1,2,0:T(4,128)} %param.12) | copy-start | bytes 772
  0.6 2.0 %copy-start.1 = (f32[2,1,1,2,256,256]{5,4,3,2,1,0:T(8,128)S(1)}, f32[2,1,1,2,256,256]{5,4,3,2,1,0:T(8,128)}, u32[]{:S(2)}) copy-start(f32[2,1,1,2,256,256]{5,4,3,2,1,0:T(8,128)} %param.7) | copy-start | bytes 3145732
  2.6 1.8 %copy-start.2 = (f32[2,1,1,2,256,256]{5,4,3,2,1,0:T(8,128)S(1)}, f32[2,1,1,2,256,256]{5,4,3,2,1,0:T(8,128)}, u32[]{:S(2)}) copy-start(f32[2,1,1,2,256,256]{5,4,3,2,1,0:T(8,128)} %param.8) | copy-start | bytes 3145732
  10.5 10.4 %collective-permute-start = (f32[2,2,128,128]{3,2,1,0:T(8,128)S(1)}, f32[2,2,128,128]{3,2,1,0:T(8,128)S(1)}, u32[]{:S(2)}, u32[]{:S(2)}) collective-permute-start(f32[2,2,128,128]{3,2,1,0:T(8,128)S(1)} %pad_maximum_fusion.12), channel_id=1, source_target_pairs={{0,1},{2,3},{4,5},{6,7},{8,9},{10,11},{12,13},{14,15},{16,17},{18,... | collective-permute-start | bytes 786440 | tf_op jit(solution)/shard_map/ppermute | solution.py:20
  16.4 0.7 copy-start.8
  17.7 3.3 %copy-start.5 = (f32[1,1,2,128,128]{4,3,2,1,0:T(8,128)S(1)}, f32[1,1,2,128,128]{4,3,2,1,0:T(8,128)}, u32[]{:S(2)}) copy-start(f32[1,1,2,128,128]{4,3,2,1,0:T(8,128)} %param.9) | copy-start | bytes 393220
  39.6 6.1 %copy-start.7 = (s32[8]{0:T(128)S(1)}, s32[8]{0:T(128)}, u32[]{:S(2)}) copy-start(s32[8]{0:T(128)} %param.11) | copy-start | bytes 100
  39.6 20.5 %all-to-all-start = ((f32[16,2,8,512]{3,2,1,0:T(8,128)}), f32[16,2,8,512]{3,2,1,0:T(8,128)S(1)}, u32[]{:S(2)}, u32[]{:S(2)}) async-start(f32[16,2,8,512]{3,2,1,0:T(8,128)} %shard_map.86), calls=%async_computation | async-start | bytes 1048576 | tf_op jit(solution)/shard_map/all_to_all | solution.py:231
  45.7 0.7 copy-start.6
  62.7 4.2 %copy-start.3 = (f32[2,256,256]{2,1,0:T(8,128)S(1)}, f32[2,256,256]{2,1,0:T(8,128)}, u32[]{:S(2)}) copy-start(f32[2,256,256]{2,1,0:T(8,128)} %get-tuple-element.31.real_ref) | copy-start | bytes 1572868
  62.7 4.3 %copy-start.4 = (f32[2,256,256]{2,1,0:T(8,128)S(1)}, f32[2,256,256]{2,1,0:T(8,128)}, u32[]{:S(2)}) copy-start(f32[2,256,256]{2,1,0:T(8,128)} %fusion.2.imag_ref) | copy-start | bytes 1572868
  62.7 18.7 %all-to-all-start.1 = ((f32[16,2,8,512]{3,2,1,0:T(8,128)}), f32[16,2,8,512]{3,2,1,0:T(8,128)S(1)}, u32[]{:S(2)}, u32[]{:S(2)}) async-start(f32[16,2,8,512]{3,2,1,0:T(8,128)} %bitcast.42), calls=%async_computation.1 | async-start | bytes 1048576 | tf_op jit(solution)/shard_map/all_to_all | solution.py:238
